TPU v7x, 256 devices: a whole 4x4x8 slice. The times are simulated.
256 devices in a mesh: seq: 16 (over x_lo, y, core), chan: 16 (over x_hi, z).
Axes of the slice: x: 4 (x_hi: 2, x_lo: 2; x = x_hi * 2 + x_lo), y: 4, z: 8, core: 2. Of those that a mesh axis runs over, the one named last changes fastest.
Arguments:
- tokens: int32 [4096], P('seq'), may hold values from 0 to 511
- embedding: bfloat16 [512, 4096], P(None, 'chan'), may hold values from -6 to 6
- norm_gain: float32 [4096], replicated, may hold values from 0.5 to 1.5
- in_weight: bfloat16 [4096, 3, 4096], P(None, None, 'chan'), may hold values from -0.09375 to 0.09375
- short_filter: float32 [3, 3, 4096], P(None, None, 'chan'), may hold values from -3 to 3
- decay_rate: float32 [16, 4096], P(None, 'chan'), may hold values from 4.8828125e-06 to 0.025, as said below
- residue: float32 [16, 4096], P(None, 'chan'), may hold values from -0.06 to 0.06
- skip_gain: float32 [4096], P('chan'), may hold values from -4 to 4
- out_weight: bfloat16 [4096, 4096], P('chan'), may hold values from -0.125 to 0.125
Outputs:
- block_out: bfloat16 [4096, 4096], P('seq', 'chan')
Inputs may be any that keep to these rules, and one draw needn't show every extreme that they name: `decay_rate`: positive rates.
All inputs are finite; a program needn't handle non-finite values.
Results may differ from a plain program's by a relative error of at most 0.0091.
Values may be sent and summed in bfloat16 or wider, within the bound.
No kernel may reach another device: no remote copies, remote signals or barrier semaphores. Data moves between devices by JAX's collectives and lax.ppermute only.
A program may use at most 128 MiB of HBM per device.

v0:
```python
import jax
import jax.numpy as jnp
from jax import lax
from jax.sharding import PartitionSpec as P

FEAT = 3
BLK = 128


def from_behind(value, axis, by):
    devices = lax.axis_size(axis)
    pairs = [(i, i + by) for i in range(devices) if 0 <= i + by < devices]
    return lax.ppermute(value, axis, pairs)


def carried_in(part, axis, combine, identity):
    place = lax.axis_index(axis)
    gathered = jax.tree.map(lambda a: lax.all_gather(a, axis), part)
    state = jax.tree.map(lambda a, e: jnp.zeros_like(a) + jnp.asarray(e, a.dtype), part, identity)

    def one(lap, state):
        return combine(
            state, jax.tree.map(lambda a: lax.dynamic_index_in_dim(a, lap, 0, False), gathered)
        )

    return lax.fori_loop(0, place, one, state)


def combine(earlier, later):
    return (earlier[0] * later[0], later[0] * earlier[1] + later[1])


def on_device(
    tokens,
    embedding,
    norm_gain,
    in_weight,
    short_filter,
    decay_rate,
    residue,
    skip_gain,
    out_weight,
):
    token_rows = tokens.shape[0]
    vocab_size = embedding.shape[0]
    channels = embedding.shape[1]
    one_hot = (tokens[:, None] == jnp.arange(vocab_size, dtype=jnp.int32)[None, :]).astype(
        jnp.bfloat16
    )
    stream = jnp.dot(one_hot, embedding, preferred_element_type=jnp.float32).astype(jnp.bfloat16)
    gathered = lax.all_gather(stream, "chan", axis=1, tiled=True)
    gathered_f = gathered.astype(jnp.float32)
    scale = lax.rsqrt(jnp.mean(gathered_f * gathered_f, axis=1, keepdims=True) + 1e-06)
    normed = (gathered_f * scale * norm_gain[None, :]).astype(jnp.bfloat16)
    proj = jnp.einsum("td,djc->tjc", normed, in_weight, preferred_element_type=jnp.float32).astype(
        jnp.bfloat16
    )
    rim_rows = FEAT - 1
    earlier_rim = from_behind(proj[token_rows - rim_rows :], "seq", 1)
    padded = jnp.concatenate([earlier_rim, proj], axis=0).astype(jnp.float32)
    feat = short_filter[0][None] * padded[rim_rows : rim_rows + token_rows]
    for offset in range(1, FEAT):
        feat = (
            feat
            + short_filter[offset][None]
            * padded[rim_rows - offset : rim_rows - offset + token_rows]
        )
    feat = feat.astype(jnp.bfloat16)
    query = feat[:, 0].astype(jnp.float32)
    driven = feat[:, 1].astype(jnp.float32) * feat[:, 2].astype(jnp.float32)
    num_blocks = token_rows // BLK
    steps_f = jnp.arange(BLK, dtype=jnp.float32)
    lag_table = jnp.arange(BLK)[:, None] - jnp.arange(BLK)[None, :]
    causal = lag_table >= 0
    impulse = jnp.sum(
        residue[:, None, :] * jnp.exp(-decay_rate[:, None, :] * steps_f[None, :, None]), axis=0
    )
    toeplitz = jnp.where(causal[:, :, None], impulse[jnp.clip(lag_table, 0, BLK - 1)], 0.0)
    w_end = jnp.exp(-decay_rate[:, None, :] * (BLK - 1 - steps_f)[None, :, None])
    r_next = residue[:, None, :] * jnp.exp(-decay_rate[:, None, :] * (steps_f + 1.0)[None, :, None])
    blocks = driven.reshape(num_blocks, BLK, channels)
    intra = jnp.einsum("ijc,bjc->bic", toeplitz, blocks, precision=lax.Precision.HIGHEST)
    block_ends = jnp.einsum("njc,bjc->bnc", w_end, blocks, precision=lax.Precision.HIGHEST)
    block_ids = jnp.arange(num_blocks)
    block_gap = block_ids[:, None] - 1 - block_ids[None, :]
    gap_weight = jnp.exp(
        -decay_rate[None, None]
        * (BLK * jnp.maximum(block_gap, 0)).astype(jnp.float32)[:, :, None, None]
    )
    gap_weight = jnp.where((block_gap >= 0)[:, :, None, None], gap_weight, 0.0)
    inner_state = jnp.einsum(
        "xync,ync->xnc", gap_weight, block_ends, precision=lax.Precision.HIGHEST
    )
    tail_weight = jnp.exp(
        -decay_rate[None] * (BLK * (num_blocks - 1 - block_ids)).astype(jnp.float32)[:, None, None]
    )
    device_end = jnp.sum(tail_weight * block_ends, axis=0)
    decay_span = jnp.exp(-decay_rate * token_rows)
    identity = (jnp.ones_like(decay_span), jnp.zeros_like(device_end))
    _, incoming = carried_in((decay_span, device_end), "seq", combine, identity)
    start_weight = jnp.exp(-decay_rate[None] * (BLK * block_ids).astype(jnp.float32)[:, None, None])
    block_in = inner_state + start_weight * incoming[None]
    carried = jnp.einsum("njc,bnc->bjc", r_next, block_in, precision=lax.Precision.HIGHEST)
    long_out = (intra + carried).reshape(token_rows, channels) + skip_gain[None, :] * driven
    hidden = (query * long_out).astype(jnp.bfloat16)
    summed = lax.psum_scatter(
        lax.dot_general(
            out_weight, hidden, (((0,), (1,)), ((), ())), preferred_element_type=jnp.float32
        ),
        "chan",
        scatter_dimension=0,
        tiled=True,
    )
    mixed = summed.T
    return (stream.astype(jnp.float32) + mixed).astype(jnp.bfloat16)


def solution(mesh):
    placed = (
        P("seq"),
        P(None, "chan"),
        P(),
        P(None, None, "chan"),
        P(None, None, "chan"),
        P(None, "chan"),
        P(None, "chan"),
        P("chan"),
        P("chan", None),
    )
    return jax.shard_map(
        on_device, mesh=mesh, in_specs=placed, out_specs=P("seq", "chan"), check_vma=False
    )
```

profile of v0, /device:TPU:8, one launch (start us, length us, event | category | flops | bytes accessed | tf_op | source)
XLA Modules:
  0.0 468.3 jit_solution(13723865632117006521)
XLA Ops:
  6.5 0.0 copy-start
  6.5 0.0 copy-start.4
  6.5 0.0 all-gather.4.cloned.1.call-start
  6.5 2.1 convolution_convert_fusion
  8.6 0.0 copy-start.6
  8.6 0.0 all-gather.4.cloned.1.call-update
  8.6 0.0 reduce-scatter.2.cloned.1.call-start
  8.7 0.7 multiply_exponential_fusion
  9.4 0.1 copy.47
  9.5 0.8 copy.46
  10.3 0.5 iota_add_fusion
  10.8 0.5 multiply_convert_fusion.1
  11.3 0.5 iota_subtract_fusion.1
  11.9 0.6 subtract_compare_fusion
  12.5 18.8 %all-gather = f32[256,256]{1,0:T(8,128)S(1)} all-gather(f32[16,256]{1,0:T(8,128)S(1)} %get-tuple-element.65), channel_id=2, replica_groups=mesh['seq'=16,'chan'=16] {'seq'}, dimensions={0}, use_global_device_ids=true | all-gather | bytes 278528 | tf_op jit(solution)/shard_map/all_gather | solution.py:18
  31.2 1.7 multiply_reduce_fusion
  32.9 0.6 fusion.49
  33.5 0.6 multiply_convert_fusion
  34.1 0.0 copy-done.4
  34.1 63.2 %all-gather.4.cloned.1.call-done = bf16[256,4096]{1,0:T(8,128)(2,1)} async-done(((bf16[256,256]{1,0:T(8,128)(2,1)}), bf16[256,4096]{1,0:T(8,128)(2,1)}) %all-gather.4.cloned.1.call-update) | async-done | bytes 2097168 | tf_op jit(solution)/shard_map/all_gather | solution.py:51
  97.3 0.0 copy-start.1
  97.3 2.2 fusion.4
  99.5 0.0 copy-done.6
  99.6 0.0 copy-done.1
  99.6 4.7 fusion.19
  104.2 1.9 collective-permute-start
  106.2 0.5 multiply_convert_fusion.2
  106.7 0.1 copy.48
  106.8 61.7 %gather_fusion = f32[16384,256]{1,0:T(8,128)} fusion(f32[128,256]{1,0:T(8,128)S(1)} %copy.48, s32[16384]{0:T(1024)S(1)} %fusion.48), kind=kCustom, calls=%fused_computation | custom fusion | bytes 33619968 | tf_op jit(solution)/shard_map/gather | solution.py:78
  168.5 18.1 %copy.49 = f32[128,128,256]{1,0,2:T(8,128)} copy(f32[128,128,256]{2,1,0:T(8,128)} %bitcast.67) | data formatting | bytes 33554432 | tf_op jit(solution)/shard_map/gather | solution.py:78
  186.6 0.0 collective-permute-done
  186.6 0.1 maximum_convert_fusion
  186.7 0.3 fusion.34
  187.0 0.1 copy.50
  187.2 4.7 %fusion.39 = (f32[16,256]{0,1:T(8,128)}, f32[256,2,16]{2,1,0:T(2,128)S(1)}) fusion(f32[16,256]{0,1:T(8,128)S(1)} %copy.47, f32[2]{0:T(128)} %multiply_convert_fusion.1, f32[2,128,256]{1,0,2:T(2,128)S(1)} %copy.50, f32[128]{0:T(128)} %iota_subtract_fusion.1), kind=kOutput, calls=%fused_computation.50 | convolution fusion | flops 13127680 | bytes 328200 | tf_op jit(solution)/shard_map/njc,bjc->bnc/dot_general | solution.py:83
  191.9 0.7 copy.64
  192.6 0.9 multiply_reduce_fusion.1
  193.5 0.8 copy.63
  194.3 1.0 copy.53
  195.3 16.6 %all-gather.1 = f32[256,256]{1,0:T(8,128)S(1)} all-gather(f32[16,256]{1,0:T(8,128)S(1)} %copy.53), channel_id=3, replica_groups=mesh['seq'=16,'chan'=16] {'seq'}, dimensions={0}, use_global_device_ids=true | all-gather | bytes 278528 | tf_op jit(solution)/shard_map/all_gather | solution.py:18
  211.9 0.2 while.12
  212.1 0.1 copy.54
  212.2 0.0 copy-start.3
  212.2 0.0 copy-start.7
  212.2 0.0 copy-start.8
  212.3 28.6 %fusion = f32[256,2,128]{2,1,0:T(2,128)S(1)} fusion(f32[2,128,256]{1,0,2:T(2,128)S(1)} %copy.50, f32[128,128,256]{1,0,2:T(8,128)} %copy.49, pred[128,128]{1,0:T(8,128)(4,1)} %subtract_compare_fusion), kind=kOutput, calls=%fused_computation.3 | convolution fusion | flops 104857600 | bytes 17317888 | tf_op jit(solution)/shard_map/ijc,bjc->bic/dot_general | solution.py:82
  240.9 0.0 copy-done.3
  240.9 0.0 copy-done.7
  240.9 0.0 copy-done.8
  240.9 0.0 copy-start.5
  240.9 3.3 fusion.25
  244.2 0.1 copy.55
  244.4 0.0 copy-done.5
  244.4 0.1 fusion.36
  244.5 0.0 copy-done
  244.5 2.7 convolution_bitcast_fusion
  247.1 0.0 copy-start.2
  247.1 0.0 reduce-scatter.2.cloned.1.call-update
  247.2 212.7 %reduce-scatter.2.cloned.1.call-done = f32[256,256]{0,1:T(8,128)} async-done(((f32[4096,256]{0,1:T(8,128)}), f32[256,256]{0,1:T(8,128)}) %reduce-scatter.2.cloned.1.call-update) | async-done | bytes 262160 | tf_op jit(solution)/shard_map/reduce_scatter | solution.py:106
  459.8 0.0 copy-done.2
  459.8 1.6 fusion.37
  (9 shorter events, 0.1 us)
Async XLA Ops:
  6.5 237.9 %copy-start = (bf16[256,4096]{1,0:T(8,128)(2,1)S(1)}, bf16[256,4096]{1,0:T(8,128)(2,1)}, u32[]{:S(2)}) copy-start(bf16[256,4096]{1,0:T(8,128)(2,1)} %param.19) | copy-start | bytes 6291460
  6.5 27.5 %copy-start.4 = (f32[3,3,256]{2,1,0:T(4,128)S(1)}, f32[3,3,256]{2,1,0:T(4,128)}, u32[]{:S(2)}) copy-start(f32[3,3,256]{2,1,0:T(4,128)} %param.15) | copy-start | bytes 27652
  6.5 90.8 %all-gather.4.cloned.1.call-start = ((), (), s32[]{:S(2)}) async-start(), calls=%async_computation.1 | async-start | bytes 2228224 | tf_op jit(solution)/shard_map/all_gather | solution.py:51
  8.6 90.9 %copy-start.6 = (f32[4096]{0:T(1024)S(1)}, f32[4096]{0:T(1024)}, u32[]{:S(2)}) copy-start(f32[4096]{0:T(1024)} %param.13) | copy-start | bytes 49156
  8.6 451.2 %reduce-scatter.2.cloned.1.call-start = ((), (), s32[]{:S(2)}) async-start(), calls=%async_computation.2 | async-start | bytes 4456448 | tf_op jit(solution)/shard_map/reduce_scatter | solution.py:106
  97.3 2.3 copy-start.1
  104.2 82.4 %collective-permute-start = (bf16[2,3,256]{2,0,1:T(2,128)(2,1)S(1)}, bf16[2,3,256]{2,0,1:T(2,128)(2,1)S(1)}, u32[]{:S(2)}, u32[]{:S(2)}) collective-permute-start(bf16[2,3,256]{2,0,1:T(2,128)(2,1)S(1)} %slice.42), channel_id=1, source_target_pairs={{0,16},{16,32},{32,48},{48,64},{64,80},{80,96},{96,112},{112,128},... | collective-permute-start | bytes 9224 | tf_op jit(solution)/shard_map/ppermute | solution.py:13
  212.2 28.7 %copy-start.3 = (f32[16,256,2]{0,2,1:T(2,128)S(1)}, f32[16,256,2]{0,2,1:T(2,128)}, u32[]{:S(2)}) copy-start(f32[16,256,2]{0,2,1:T(2,128)} %copy.63) | copy-start | bytes 98308
  212.2 28.7 %copy-start.7 = (f32[128]{0:T(128)S(1)}, f32[128]{0:T(128)}, u32[]{:S(2)}) copy-start(f32[128]{0:T(128)} %iota_add_fusion) | copy-start | bytes 1540
  212.2 28.7 %copy-start.8 = (f32[2]{0:T(128)S(1)}, f32[2]{0:T(128)}, u32[]{:S(2)}) copy-start(f32[2]{0:T(128)} %multiply_convert_fusion.2) | copy-start | bytes 28
  240.9 3.5 copy-start.5
  247.1 212.7 %copy-start.2 = (bf16[256,256]{1,0:T(8,128)(2,1)S(1)}, bf16[256,256]{1,0:T(8,128)(2,1)}, u32[]{:S(2)}) copy-start(bf16[256,256]{1,0:T(8,128)(2,1)} %convolution_convert_fusion) | copy-start | bytes 393220
Sparse Core Ops, SparseCore 0:
  9.8 87.4 all-gather.3
  247.3 212.4 reduce-scatter.1
where the time goes:
time: 469 us; the launch traced here: 468 us
  waiting for transfers between devices  276 us (59%)
  local copies, waits for them, and re-layouts  83.8 us (18%)
  matrix products  46.1 us (10%)
  blocking collectives  35.4 us (8%)
  between operations  13.6 us (3%)
  other arithmetic  11.4 us (2%)
    reduce_scatter x1, waiting for transfers between devices, on_device(): lax.psum_scatter(lax.dot_general(out_weight, hidden, (((0,), (1,)), ((),...  213 us
    gather x2, local copies, waits for them, and re-layouts, on_device(): impulse[jnp.clip(lag_table, 0, BLK - 1)]  79.8 us
    all_gather x1, waiting for transfers between devices, on_device(): gathered = lax.all_gather(stream, 'chan', axis=1, tiled=True)  63.2 us
    all_gather x2, blocking collectives, carried_in(): gathered = jax.tree.map(lambda a: lax.all_gather(a, axis), part)  35.4 us
    dot_general x1, matrix products, on_device(): jnp.einsum('ijc,bjc->bic', toeplitz, blocks, precision=lax.Precision.HIGH...  28.6 us
  transfers between devices with their start and end apart: 3, of which 2 were waited for; matrix products, arithmetic and copies ran while one was open for 19% of the time, Pallas kernels for 0%

commit v1 on v0

v1 whole, which is shorter than its diff:
```python
import jax
import jax.numpy as jnp
from jax import lax
from jax.sharding import PartitionSpec as P

FEAT = 3


def from_behind(value, axis, by):
    devices = lax.axis_size(axis)
    pairs = [(i, i + by) for i in range(devices) if 0 <= i + by < devices]
    return lax.ppermute(value, axis, pairs)


def on_device(
    tokens,
    embedding,
    norm_gain,
    in_weight,
    short_filter,
    decay_rate,
    residue,
    skip_gain,
    out_weight,
):
    token_rows = tokens.shape[0]
    vocab_size = embedding.shape[0]
    channels = embedding.shape[1]
    modes = decay_rate.shape[0]
    seq_devices = lax.axis_size("seq")
    place = lax.axis_index("seq")

    weight_cols = lax.all_to_all(out_weight, "chan", 1, 0, tiled=True)

    one_hot = (tokens[:, None] == jnp.arange(vocab_size, dtype=jnp.int32)[None, :]).astype(
        jnp.bfloat16
    )
    stream = jnp.dot(one_hot, embedding, preferred_element_type=jnp.float32).astype(jnp.bfloat16)
    gathered = lax.all_gather(stream, "chan", axis=1, tiled=True)
    gathered_f = gathered.astype(jnp.float32)
    scale = lax.rsqrt(jnp.mean(gathered_f * gathered_f, axis=1, keepdims=True) + 1e-06)
    normed = (gathered_f * scale * norm_gain[None, :]).astype(jnp.bfloat16)
    proj = jnp.einsum("td,djc->tjc", normed, in_weight, preferred_element_type=jnp.float32).astype(
        jnp.bfloat16
    )
    rim_rows = FEAT - 1
    earlier_rim = from_behind(proj[token_rows - rim_rows :], "seq", 1)
    padded = jnp.concatenate([earlier_rim, proj], axis=0).astype(jnp.float32)
    feat = short_filter[0][None] * padded[rim_rows : rim_rows + token_rows]
    for offset in range(1, FEAT):
        feat = (
            feat
            + short_filter[offset][None]
            * padded[rim_rows - offset : rim_rows - offset + token_rows]
        )
    feat = feat.astype(jnp.bfloat16)
    query = feat[:, 0].astype(jnp.float32)
    driven = feat[:, 1].astype(jnp.float32) * feat[:, 2].astype(jnp.float32)

    pos = jnp.arange(token_rows, dtype=jnp.float32)
    rise = jnp.exp(decay_rate[None] * pos[:, None, None])
    fall = residue[None] * jnp.exp(-decay_rate[None] * pos[:, None, None])
    rows = jnp.arange(token_rows)
    lower = (rows[:, None] >= rows[None, :]).astype(jnp.float32)
    lifted = rise * driven[:, None, :]
    running = jnp.dot(
        lower, lifted.reshape(token_rows, modes * channels), precision=lax.Precision.HIGHEST
    ).reshape(token_rows, modes, channels)
    local = jnp.sum(fall * running, axis=1)
    device_end = jnp.exp(-decay_rate * (token_rows - 1)) * jnp.sum(lifted, axis=0)
    ends = lax.all_gather(device_end, "seq")
    gap = place - 1 - jnp.arange(seq_devices)
    span = jnp.exp(
        -decay_rate[None]
        * (token_rows * jnp.maximum(gap, 0)).astype(jnp.float32)[:, None, None]
    )
    span = jnp.where((gap >= 0)[:, None, None], span, 0.0)
    incoming = jnp.sum(span * ends, axis=0) * jnp.exp(-decay_rate)
    carried = jnp.sum(fall * incoming[None], axis=1)
    long_out = local + carried + skip_gain[None, :] * driven
    hidden = (query * long_out).astype(jnp.bfloat16)
    hidden_all = lax.all_gather(hidden, "chan", axis=1, tiled=True)
    mixed = jnp.dot(hidden_all, weight_cols, preferred_element_type=jnp.float32)
    return (stream.astype(jnp.float32) + mixed).astype(jnp.bfloat16)


def solution(mesh):
    placed = (
        P("seq"),
        P(None, "chan"),
        P(),
        P(None, None, "chan"),
        P(None, None, "chan"),
        P(None, "chan"),
        P(None, "chan"),
        P("chan"),
        P("chan", None),
    )
    return jax.shard_map(
        on_device, mesh=mesh, in_specs=placed, out_specs=P("seq", "chan"), check_vma=False
    )
```

time: 469 us -> 252 us (0.54)
  waiting for transfers between devices: 276 us -> 181 us
  local copies, waits for them, and re-layouts: 83.8 us -> 7.62 us
  matrix products: 46.1 us -> 13.7 us
  blocking collectives: 35.4 us -> 16.6 us
  starting transfers between devices: 1.96 us -> 13.1 us
  other arithmetic: 11.4 us -> 6.17 us
    reduce_scatter x1 -> x0, waiting for transfers between devices: 213 us -> none  [on_device(): lax.psum_scatter(lax.dot_general(out_weight, hidden, (((0,), (1,)), ((),...]
    all_gather x0 -> x1, waiting for transfers between devices: none -> 80.3 us  [on_device(): hidden_all = lax.all_gather(hidden, 'chan', axis=1, tiled=True)]
    gather x2 -> x0, local copies, waits for them, and re-layouts: 79.8 us -> none  [on_device(): impulse[jnp.clip(lag_table, 0, BLK - 1)]]
    all_gather x1, waiting for transfers between devices: 63.2 us -> 97.7 us  [on_device(): gathered = lax.all_gather(stream, 'chan', axis=1, tiled=True)]
    dot_general x4 -> x2, matrix products: 39.3 us -> 6.86 us  [the longest x1 3.59 us: on_device(): mixed = jnp.dot(hidden_all, weight_cols, preferred_element_type=jnp.float32)]
    all_gather x2 -> x1, blocking collectives: 35.4 us -> 16.6 us  [on_device(): ends = lax.all_gather(device_end, 'seq')]
    all_to_all x0 -> x1, starting transfers between devices: none -> 11.2 us  [on_device(): weight_cols = lax.all_to_all(out_weight, 'chan', 1, 0, tiled=True)]
  transfers between devices with their start and end apart: 3 -> 4, of which waited for: 2 -> 3; matrix products, arithmetic and copies ran while one was open for 19% -> 8% of each run, Pallas kernels for 0% -> 0%
where the time goes in v1:
time: 252 us
  waiting for transfers between devices  181 us (72%)
  blocking collectives  16.6 us (7%)
  matrix products  13.7 us (5%)
  between operations  13.6 us (5%)
  starting transfers between devices  13.1 us (5%)
  local copies, waits for them, and re-layouts  7.62 us (3%)
  other arithmetic  6.17 us (2%)
    all_gather x1, waiting for transfers between devices, on_device(): gathered = lax.all_gather(stream, 'chan', axis=1, tiled=True)  97.7 us
    all_gather x1, waiting for transfers between devices, on_device(): hidden_all = lax.all_gather(hidden, 'chan', axis=1, tiled=True)  80.3 us
    all_gather x1, blocking collectives, on_device(): ends = lax.all_gather(device_end, 'seq')  16.6 us
    all_to_all x1, starting transfers between devices, on_device(): weight_cols = lax.all_to_all(out_weight, 'chan', 1, 0, tiled=True)  11.2 us
    dot_general x1, matrix products, on_device(): jnp.einsum('td,djc->tjc', normed, in_weight, preferred_element_type=jnp.f...  5.27 us
    unnamed x16, local copies, waits for them, and re-layouts  5.08 us
  transfers between devices with their start and end apart: 4, of which 3 were waited for; matrix products, arithmetic and copies ran while one was open for 8% of the time, Pallas kernels for 0%

profile of v1, /device:TPU:8, one launch (start us, length us, event | category | flops | bytes accessed | tf_op | source)
XLA Modules:
  0.0 251.8 jit_solution(8482166742746502454)
XLA Ops:
  6.5 0.0 copy-start
  6.5 0.0 all-gather.4.cloned.1.call-start
  6.5 0.9 copy-done
  7.5 1.6 convolution_convert_fusion
  9.1 0.0 all-gather.4.cloned.1.call-update
  9.1 0.0 copy-start.3
  9.1 4.1 %copy.11 = bf16[256,4096]{0,1:T(8,128)(2,1)} copy(bf16[256,4096]{1,0:T(8,128)(2,1)} %param.17) | data formatting | bytes 4194304 | tf_op args[8]
  13.2 0.0 copy-start.5
  13.2 11.2 %all-to-all-start = ((bf16[256,16,256]{0,2,1:T(8,128)(2,1)}), bf16[256,16,256]{0,2,1:T(8,128)(2,1)S(1)}, u32[]{:S(2)}, u32[]{:S(2)}) async-start(bf16[256,16,256]{0,2,1:T(8,128)(2,1)} %bitcast.40), calls=%async_computation | async-start | bytes 4194304 | tf_op jit(solution)/shard_map/all_to_all | solution.py:33
  24.4 0.0 all-gather.6.cloned.1.call-start
  24.5 0.0 copy-done.3
  24.5 97.7 %all-gather.4.cloned.1.call-done = bf16[256,4096]{1,0:T(8,128)(2,1)} async-done(((bf16[256,256]{1,0:T(8,128)(2,1)}), bf16[256,4096]{1,0:T(8,128)(2,1)}) %all-gather.4.cloned.1.call-update) | async-done | bytes 2097168 | tf_op jit(solution)/shard_map/all_gather | solution.py:39
  122.2 2.1 fusion
  124.2 0.0 copy-done.5
  124.3 0.0 copy-start.1
  124.3 5.3 %fusion.8 = bf16[256,3,256]{2,0,1:T(8,128)(2,1)S(1)} fusion(bf16[4096,3,256]{2,0,1:T(8,128)(2,1)} %param.12, bf16[256,4096]{1,0:T(8,128)(2,1)} %all-gather.4.cloned.1.call-done, f32[4096]{0:T(1024)S(1)} %copy-done.5, f32[256]{0:T(256)S(1)} %add_rsqrt_fusion), kind=kOutput, calls=%fused_computation.14 | convolution fusion | flops 1615003648 | bytes 8799232 | tf_op jit(solution)/shard_map/td,djc->tjc/dot_general | solution.py:43
  129.6 1.9 collective-permute-start
  131.5 0.0 copy-done.1
  131.5 2.9 %collective-permute-done = bf16[2,3,256]{2,0,1:T(2,128)(2,1)S(1)} collective-permute-done((bf16[2,3,256]{2,0,1:T(2,128)(2,1)S(1)}, bf16[2,3,256]{2,0,1:T(2,128)(2,1)S(1)}, u32[]{:S(2)}, u32[]{:S(2)}) %collective-permute-start) | collective-permute-done | bytes 3104 | tf_op jit(solution)/shard_map/ppermute | solution.py:12
  134.5 0.1 maximum_convert_fusion
  134.6 0.3 fusion.13
  134.8 0.0 copy-start.6
  134.9 0.1 copy.10
  135.0 1.3 multiply_reduce_fusion.1
  136.4 16.6 %all-gather = f32[256,256]{1,0:T(8,128)S(1)} all-gather(f32[16,256]{1,0:T(8,128)S(1)} %get-tuple-element.5), channel_id=2, replica_groups=mesh['seq'=16,'chan'=16] {'seq'}, dimensions={0}, use_global_device_ids=true | all-gather | bytes 278528 | tf_op jit(solution)/shard_map/all_gather | solution.py:71
  153.0 0.1 multiply_reduce_fusion.3
  153.1 0.6 bitcast_multiply_fusion
  153.8 0.0 copy-done.6
  153.8 0.0 copy-start.4
  153.8 0.9 multiply_reduce_fusion
  154.7 3.3 %multiply_reduce_fusion.2 = f32[256,256]{1,0:T(8,128)S(1)} fusion(f32[16,256,256]{2,1,0:T(8,128)S(1)} %bitcast.41, f32[16,256]{1,0:T(8,128)S(1)} %get-tuple-element.6, f32[16,256]{1,0:T(8,128)S(1)} %copy-done.6), kind=kOutput, calls=%fused_computation.8 | convolution fusion | flops 3225419776 | bytes 4489216 | tf_op jit(solution)/shard_map/dot_general | solution.py:66
  157.9 0.0 copy-done.4
  157.9 0.0 copy-start.2
  157.9 0.7 fusion.15
  158.7 0.0 all-gather.6.cloned.1.call-update
  158.7 0.0 all-to-all-done
  158.7 2.4 copy.12
  161.1 80.3 %all-gather.6.cloned.1.call-done = bf16[256,4096]{1,0:T(8,128)(2,1)} async-done(((bf16[256,256]{1,0:T(8,128)(2,1)}), bf16[256,4096]{1,0:T(8,128)(2,1)}) %all-gather.6.cloned.1.call-update) | async-done | bytes 2097168 | tf_op jit(solution)/shard_map/all_gather | solution.py:82
  241.4 0.0 copy-done.2
  241.4 3.6 %fusion.11 = bf16[256,256]{1,0:T(8,128)(2,1)} fusion(bf16[256,4096]{1,0:T(8,128)(2,1)} %all-gather.6.cloned.1.call-done, bf16[4096,256]{1,0:T(8,128)(2,1)} %bitcast.42, bf16[256,256]{1,0:T(8,128)(2,1)S(1)} %copy-done.2), kind=kOutput, calls=%fused_computation.16 | convolution fusion | flops 537067520 | bytes 4456448 | tf_op jit(solution)/shard_map/dot_general | solution.py:83
  (9 shorter events, 0.1 us)
Async XLA Ops:
  6.5 1.0 copy-start
  6.5 115.6 %all-gather.4.cloned.1.call-start = ((), (), s32[]{:S(2)}) async-start(), calls=%async_computation.1 | async-start | bytes 2228224 | tf_op jit(solution)/shard_map/all_gather | solution.py:39
  9.1 15.3 %copy-start.3 = (f32[3,3,256]{2,1,0:T(4,128)S(1)}, f32[3,3,256]{2,1,0:T(4,128)}, u32[]{:S(2)}) copy-start(f32[3,3,256]{2,1,0:T(4,128)} %param.13) | copy-start | bytes 27652
  13.2 111.0 %copy-start.5 = (f32[4096]{0:T(1024)S(1)}, f32[4096]{0:T(1024)}, u32[]{:S(2)}) copy-start(f32[4096]{0:T(1024)} %param.11) | copy-start | bytes 49156
  13.2 145.5 %all-to-all-start = ((bf16[256,16,256]{0,2,1:T(8,128)(2,1)}), bf16[256,16,256]{0,2,1:T(8,128)(2,1)S(1)}, u32[]{:S(2)}, u32[]{:S(2)}) async-start(bf16[256,16,256]{0,2,1:T(8,128)(2,1)} %bitcast.40), calls=%async_computation | async-start | bytes 4194304 | tf_op jit(solution)/shard_map/all_to_all | solution.py:33
  24.4 217.0 %all-gather.6.cloned.1.call-start = ((), (), s32[]{:S(2)}) async-start(), calls=%async_computation.2 | async-start | bytes 2228224 | tf_op jit(solution)/shard_map/all_gather | solution.py:82
  124.3 7.3 %copy-start.1 = (f32[16,256]{1,0:T(8,128)S(1)}, f32[16,256]{1,0:T(8,128)}, u32[]{:S(2)}) copy-start(f32[16,256]{1,0:T(8,128)} %param.14) | copy-start | bytes 49156
  129.6 4.9 %collective-permute-start = (bf16[2,3,256]{2,0,1:T(2,128)(2,1)S(1)}, bf16[2,3,256]{2,0,1:T(2,128)(2,1)S(1)}, u32[]{:S(2)}, u32[]{:S(2)}) collective-permute-start(bf16[2,3,256]{2,0,1:T(2,128)(2,1)S(1)} %slice.40), channel_id=1, source_target_pairs={{0,16},{16,32},{32,48},{48,64},{64,80},{80,96},{96,112},{112,128},... | collective-permute-start | bytes 9224 | tf_op jit(solution)/shard_map/ppermute | solution.py:12
  134.8 18.9 %copy-start.6 = (f32[16,256]{1,0:T(8,128)S(1)}, f32[16,256]{1,0:T(8,128)}, u32[]{:S(2)}) copy-start(f32[16,256]{1,0:T(8,128)} %param.15) | copy-start | bytes 49156
  153.8 4.2 %copy-start.4 = (f32[256]{0:T(256)S(1)}, f32[256]{0:T(256)}, u32[]{:S(2)}) copy-start(f32[256]{0:T(256)} %param.16) | copy-start | bytes 3076
  157.9 83.5 %copy-start.2 = (bf16[256,256]{1,0:T(8,128)(2,1)S(1)}, bf16[256,256]{1,0:T(8,128)(2,1)}, u32[]{:S(2)}) copy-start(bf16[256,256]{1,0:T(8,128)(2,1)} %convolution_convert_fusion) | copy-start | bytes 393220
Sparse Core Ops, SparseCore 0:
  9.8 112.3 all-gather.3
  158.8 82.5 all-gather.5

commit v2 on v1

--- a/solution.py
+++ b/solution.py
@@ -28,15 +28,15 @@
     channels = embedding.shape[1]
     modes = decay_rate.shape[0]
     seq_devices = lax.axis_size("seq")
-    place = lax.axis_index("seq")
-
-    weight_cols = lax.all_to_all(out_weight, "chan", 1, 0, tiled=True)
 
     one_hot = (tokens[:, None] == jnp.arange(vocab_size, dtype=jnp.int32)[None, :]).astype(
         jnp.bfloat16
     )
     stream = jnp.dot(one_hot, embedding, preferred_element_type=jnp.float32).astype(jnp.bfloat16)
-    gathered = lax.all_gather(stream, "chan", axis=1, tiled=True)
+    chan_devices = lax.axis_size("chan")
+    gathered = lax.all_to_all(
+        jnp.tile(stream, (chan_devices, 1)), "chan", 0, 1, tiled=True
+    )
     gathered_f = gathered.astype(jnp.float32)
     scale = lax.rsqrt(jnp.mean(gathered_f * gathered_f, axis=1, keepdims=True) + 1e-06)
     normed = (gathered_f * scale * norm_gain[None, :]).astype(jnp.bfloat16)
@@ -68,8 +68,10 @@
     ).reshape(token_rows, modes, channels)
     local = jnp.sum(fall * running, axis=1)
     device_end = jnp.exp(-decay_rate * (token_rows - 1)) * jnp.sum(lifted, axis=0)
-    ends = lax.all_gather(device_end, "seq")
-    gap = place - 1 - jnp.arange(seq_devices)
+    ends = lax.all_to_all(
+        jnp.tile(device_end, (seq_devices, 1)), "seq", 0, 0, tiled=True
+    ).reshape(seq_devices, modes, channels)
+    gap = lax.axis_index("seq") - 1 - jnp.arange(seq_devices)
     span = jnp.exp(
         -decay_rate[None]
         * (token_rows * jnp.maximum(gap, 0)).astype(jnp.float32)[:, None, None]
@@ -79,8 +81,11 @@
     carried = jnp.sum(fall * incoming[None], axis=1)
     long_out = local + carried + skip_gain[None, :] * driven
     hidden = (query * long_out).astype(jnp.bfloat16)
-    hidden_all = lax.all_gather(hidden, "chan", axis=1, tiled=True)
-    mixed = jnp.dot(hidden_all, weight_cols, preferred_element_type=jnp.float32)
+    partial = jnp.dot(hidden, out_weight, preferred_element_type=jnp.float32).astype(jnp.bfloat16)
+    parts = lax.all_to_all(partial, "chan", 1, 0, tiled=True)
+    mixed = jnp.sum(
+        parts.reshape(chan_devices, token_rows, channels).astype(jnp.float32), axis=0
+    )
     return (stream.astype(jnp.float32) + mixed).astype(jnp.bfloat16)
 
 

time: 252 us -> 159 us (0.63)
  waiting for transfers between devices: 181 us -> 53.2 us
  blocking collectives: 16.6 us -> 57.8 us
  between operations: 13.6 us -> 0.24 us
  starting transfers between devices: 13.1 us -> 18 us
  other arithmetic: 6.17 us -> 10.1 us
    all_gather x2 -> x0, waiting for transfers between devices: 178 us -> none  [the longest x1 97.7 us: on_device(): gathered = lax.all_gather(stream, 'chan', axis=1, tiled=True)]
    all_to_all x0 -> x1, blocking collectives: none -> 57.8 us  [on_device(): parts = lax.all_to_all(partial, 'chan', 1, 0, tiled=True)]
    all_to_all x1 -> x2, waiting for transfers between devices: 0.01 us -> 50.3 us  [the longest x1 50.3 us: on_device(): lax.all_to_all(jnp.tile(stream, (chan_devices, 1)), 'chan', 0, 1, tiled=T...]
    all_gather x1 -> x0, blocking collectives: 16.6 us -> none  [on_device(): ends = lax.all_gather(device_end, 'seq')]
    unnamed x16 -> x13, local copies, waits for them, and re-layouts: 5.08 us -> 0.04 us
    all_to_all x1 -> x2, starting transfers between devices: 11.2 us -> 16 us  [the longest x1 11.1 us: on_device(): lax.all_to_all(jnp.tile(stream, (chan_devices, 1)), 'chan', 0, 1, tiled=T...]
    dot_general x1, matrix products: 3.59 us -> 0.73 us  [on_device(): jnp.dot(hidden, out_weight, preferred_element_type=jnp.float32)]
  transfers between devices with their start and end apart: 4 -> 3, of which waited for: 3 -> 2; matrix products, arithmetic and copies ran while one was open for 8% -> 3% of each run, Pallas kernels for 0% -> 0%
where the time goes in v2:
time: 159 us; the launch traced here: 158 us
  blocking collectives  57.8 us (36%)
  waiting for transfers between devices  53.2 us (33%)
  starting transfers between devices  18 us (11%)
  matrix products  12.2 us (8%)
  other arithmetic  10.1 us (6%)
  local copies, waits for them, and re-layouts  6.52 us (4%)
    all_to_all x1, blocking collectives, on_device(): parts = lax.all_to_all(partial, 'chan', 1, 0, tiled=True)  57.8 us
    all_to_all x1, waiting for transfers between devices, on_device(): lax.all_to_all(jnp.tile(stream, (chan_devices, 1)), 'chan', 0, 1, tiled=T...  50.3 us
    all_to_all x1, starting transfers between devices, on_device(): lax.all_to_all(jnp.tile(stream, (chan_devices, 1)), 'chan', 0, 1, tiled=T...  11.1 us
    dot_general x1, matrix products, on_device(): jnp.dot(lower, lifted.reshape(token_rows, modes * channels), precision=la...  5.44 us
    all_to_all x1, starting transfers between devices, on_device(): lax.all_to_all(jnp.tile(device_end, (seq_devices, 1)), 'seq', 0, 0, tiled...  4.96 us
    dot_general x1, matrix products, on_device(): jnp.einsum('td,djc->tjc', normed, in_weight, preferred_element_type=jnp.f...  4.63 us
    all_to_all x1, local copies, waits for them, and re-layouts, on_device(): lax.all_to_all(jnp.tile(stream, (chan_devices, 1)), 'chan', 0, 1, tiled=T...  3.92 us
  transfers between devices with their start and end apart: 3, of which 2 were waited for; matrix products, arithmetic and copies ran while one was open for 3% of the time, Pallas kernels for 0%

profile of v2, /device:TPU:8, one launch (start us, length us, event | category | flops | bytes accessed | tf_op | source)
XLA Modules:
  0.0 158.0 jit_solution(18166354068730283894)
XLA Ops:
  0.0 0.0 copy-start
  0.0 0.0 copy-start.3
  0.0 1.4 convolution_convert_fusion.1
  1.4 1.5 tile.4
  2.9 11.1 %all-to-all-start = ((bf16[16,256,256]{2,1,0:T(8,128)(2,1)}), bf16[16,256,256]{2,1,0:T(8,128)(2,1)}, u32[]{:S(2)}, u32[]{:S(2)}) async-start(bf16[16,256,256]{2,1,0:T(8,128)(2,1)} %tile.4), calls=%async_computation | async-start | bytes 4194304 | tf_op jit(solution)/shard_map/all_to_all | solution.py:37
  14.0 0.0 copy-start.2
  14.0 0.0 copy-done.3
  14.1 50.3 %all-to-all-done = bf16[16,256,256]{2,1,0:T(8,128)(2,1)} async-done(((bf16[16,256,256]{2,1,0:T(8,128)(2,1)}), bf16[16,256,256]{2,1,0:T(8,128)(2,1)}, u32[]{:S(2)}, u32[]{:S(2)}) %all-to-all-start) | async-done | bytes 2097184 | tf_op jit(solution)/shard_map/all_to_all | solution.py:37
  64.3 3.9 %copy.15 = bf16[16,256,256]{1,2,0:T(8,128)(2,1)} copy(bf16[16,256,256]{2,1,0:T(8,128)(2,1)} %all-to-all-done) | data formatting | bytes 4194304 | tf_op jit(solution)/shard_map/all_to_all | solution.py:37
  68.2 2.2 %multiply_reduce_fusion.3 = f32[256]{0:T(256)S(1)} fusion(bf16[16,256,256]{1,2,0:T(8,128)(2,1)} %copy.15), kind=kLoop, calls=%fused_computation.10 | loop fusion | flops 3145472 | bytes 2098176 | tf_op jit(solution)/shard_map/reduce_sum | solution.py:41
  70.4 0.0 copy-done.2
  70.4 1.9 %fusion.1 = bf16[256,4096]{0,1:T(8,128)(2,1)S(1)} fusion(f32[4096]{0:T(1024)S(1)} %copy-done.2, f32[256]{0:T(256)S(1)} %add_rsqrt_fusion, bf16[16,256,256]{1,2,0:T(8,128)(2,1)} %copy.15), kind=kLoop, calls=%fused_computation.3 | loop fusion | flops 4194304 | bytes 4211712 | tf_op jit(solution)/shard_map/convert_element_type | solution.py:42
  72.4 0.0 copy-start.1
  72.4 4.6 %fusion.4 = bf16[256,3,256]{2,0,1:T(8,128)(2,1)S(1)} fusion(bf16[4096,3,256]{2,0,1:T(8,128)(2,1)} %param.12, bf16[256,4096]{0,1:T(8,128)(2,1)S(1)} %fusion.1), kind=kOutput, calls=%fused_computation.14 | convolution fusion | flops 1610809344 | bytes 8781824 | tf_op jit(solution)/shard_map/td,djc->tjc/dot_general | solution.py:43
  77.0 1.9 %collective-permute-start = (bf16[2,3,256]{2,0,1:T(2,128)(2,1)S(1)}, bf16[2,3,256]{2,0,1:T(2,128)(2,1)S(1)}, u32[]{:S(2)}, u32[]{:S(2)}) collective-permute-start(bf16[2,3,256]{2,0,1:T(2,128)(2,1)S(1)} %slice.40), channel_id=1, source_target_pairs={{0,16},{16,32},{32,48},{48,64},{64,80},{80,96},{96,112},{112,128},... | collective-permute-start | bytes 9224 | tf_op jit(solution)/shard_map/ppermute | solution.py:12
  79.0 0.0 copy-done.1
  79.0 2.9 %collective-permute-done = bf16[2,3,256]{2,0,1:T(2,128)(2,1)S(1)} collective-permute-done((bf16[2,3,256]{2,0,1:T(2,128)(2,1)S(1)}, bf16[2,3,256]{2,0,1:T(2,128)(2,1)S(1)}, u32[]{:S(2)}, u32[]{:S(2)}) %collective-permute-start) | collective-permute-done | bytes 3104 | tf_op jit(solution)/shard_map/ppermute | solution.py:12
  81.9 0.1 maximum_convert_fusion
  82.0 0.3 fusion.8
  82.3 0.0 copy-start.5
  82.3 0.1 copy.17
  82.5 1.3 multiply_reduce_fusion.1
  83.8 2.3 %bitcast_multiply_fusion.1 = f32[256,4096]{0,1:T(8,128)} fusion(f32[256,256]{0,1:T(8,128)S(1)} %copy.17, f32[4096]{0:T(1024)S(1)} %bitcast.52), kind=kLoop, calls=%fused_computation.4 | loop fusion | flops 2097152 | bytes 4472832 | tf_op jit(solution)/shard_map/mul | solution.py:65
  86.1 0.7 tile.5
  86.8 5.0 %all-to-all-start.1 = ((f32[16,16,256]{2,1,0:T(8,128)}), f32[16,16,256]{2,1,0:T(8,128)S(1)}, u32[]{:S(2)}, u32[]{:S(2)}) async-start(f32[16,16,256]{2,1,0:T(8,128)} %tile.5), calls=%async_computation.1 | async-start | bytes 524288 | tf_op jit(solution)/shard_map/all_to_all | solution.py:71
  91.8 0.0 copy-start.4
  91.8 0.0 copy-done.5
  91.8 5.4 %multiply_reduce_fusion.2 = f32[256,256]{1,0:T(8,128)S(1)} fusion(f32[16,256,256]{2,1,0:T(8,128)} %bitcast.50, f32[16,256]{1,0:T(8,128)S(1)} %get-tuple-element.6, f32[16,256]{1,0:T(8,128)S(1)} %copy-done.5), kind=kOutput, calls=%fused_computation.8 | convolution fusion | flops 3225419776 | bytes 4489216 | tf_op jit(solution)/shard_map/dot_general | solution.py:66
  97.3 0.0 all-to-all-done.1
  97.3 0.1 multiply_reduce_fusion.4
  97.4 0.9 multiply_reduce_fusion
  98.3 0.0 copy-done
  98.3 0.0 copy-done.4
  98.3 0.7 convolution_convert_fusion
  99.0 0.2 copy.24
  99.2 57.8 %all_to_all.29 = bf16[256,16,256]{2,0,1:T(8,128)(2,1)S(1)} all-to-all(bf16[256,16,256]{2,0,1:T(8,128)(2,1)S(1)} %bitcast.49), channel_id=1, replica_groups=mesh['seq'=16,'chan'=16] {'chan'}, dimensions={1} | all-to-all | bytes 4194304 | tf_op jit(solution)/shard_map/all_to_all | solution.py:85
  157.0 0.3 convert_reduce_fusion
  157.3 0.7 add_convert_fusion
  (9 shorter events, 0.1 us)
Async XLA Ops:
  0.0 98.3 %copy-start = (bf16[256,4096]{1,0:T(8,128)(2,1)S(1)}, bf16[256,4096]{1,0:T(8,128)(2,1)}, u32[]{:S(2)}) copy-start(bf16[256,4096]{1,0:T(8,128)(2,1)} %param.17) | copy-start | bytes 6291460
  0.0 14.0 %copy-start.3 = (f32[3,3,256]{2,1,0:T(4,128)S(1)}, f32[3,3,256]{2,1,0:T(4,128)}, u32[]{:S(2)}) copy-start(f32[3,3,256]{2,1,0:T(4,128)} %param.13) | copy-start | bytes 27652
  2.9 61.4 %all-to-all-start = ((bf16[16,256,256]{2,1,0:T(8,128)(2,1)}), bf16[16,256,256]{2,1,0:T(8,128)(2,1)}, u32[]{:S(2)}, u32[]{:S(2)}) async-start(bf16[16,256,256]{2,1,0:T(8,128)(2,1)} %tile.4), calls=%async_computation | async-start | bytes 4194304 | tf_op jit(solution)/shard_map/all_to_all | solution.py:37
  14.0 56.4 %copy-start.2 = (f32[4096]{0:T(1024)S(1)}, f32[4096]{0:T(1024)}, u32[]{:S(2)}) copy-start(f32[4096]{0:T(1024)} %param.11) | copy-start | bytes 49156
  72.4 6.6 %copy-start.1 = (f32[16,256]{1,0:T(8,128)S(1)}, f32[16,256]{1,0:T(8,128)}, u32[]{:S(2)}) copy-start(f32[16,256]{1,0:T(8,128)} %param.14) | copy-start | bytes 49156
  77.0 4.9 %collective-permute-start = (bf16[2,3,256]{2,0,1:T(2,128)(2,1)S(1)}, bf16[2,3,256]{2,0,1:T(2,128)(2,1)S(1)}, u32[]{:S(2)}, u32[]{:S(2)}) collective-permute-start(bf16[2,3,256]{2,0,1:T(2,128)(2,1)S(1)} %slice.40), channel_id=1, source_target_pairs={{0,16},{16,32},{32,48},{48,64},{64,80},{80,96},{96,112},{112,128},... | collective-permute-start | bytes 9224 | tf_op jit(solution)/shard_map/ppermute | solution.py:12
  82.3 9.5 %copy-start.5 = (f32[16,256]{1,0:T(8,128)S(1)}, f32[16,256]{1,0:T(8,128)}, u32[]{:S(2)}) copy-start(f32[16,256]{1,0:T(8,128)} %param.15) | copy-start | bytes 49156
  86.8 10.4 %all-to-all-start.1 = ((f32[16,16,256]{2,1,0:T(8,128)}), f32[16,16,256]{2,1,0:T(8,128)S(1)}, u32[]{:S(2)}, u32[]{:S(2)}) async-start(f32[16,16,256]{2,1,0:T(8,128)} %tile.5), calls=%async_computation.1 | async-start | bytes 524288 | tf_op jit(solution)/shard_map/all_to_all | solution.py:71
  91.8 6.5 %copy-start.4 = (f32[256]{0:T(256)S(1)}, f32[256]{0:T(256)}, u32[]{:S(2)}) copy-start(f32[256]{0:T(256)} %param.16) | copy-start | bytes 3076

commit v3 on v2

--- a/solution.py
+++ b/solution.py
@@ -34,9 +34,17 @@
     )
     stream = jnp.dot(one_hot, embedding, preferred_element_type=jnp.float32).astype(jnp.bfloat16)
     chan_devices = lax.axis_size("chan")
-    gathered = lax.all_to_all(
-        jnp.tile(stream, (chan_devices, 1)), "chan", 0, 1, tiled=True
+    half = chan_devices // 2
+    partners = [(i, (i + half) % chan_devices) for i in range(chan_devices)]
+    groups = [list(range(half)), list(range(half, chan_devices))]
+    upper = lax.axis_index("chan") >= half
+    other = lax.ppermute(stream, "chan", partners)
+    pair = jnp.where(upper, jnp.stack([other, stream]), jnp.stack([stream, other]))
+    got = lax.all_to_all(
+        jnp.broadcast_to(pair[None], (half,) + pair.shape),
+        "chan", 0, 0, axis_index_groups=groups,
     )
+    gathered = got.transpose(2, 1, 0, 3).reshape(token_rows, chan_devices * channels)
     gathered_f = gathered.astype(jnp.float32)
     scale = lax.rsqrt(jnp.mean(gathered_f * gathered_f, axis=1, keepdims=True) + 1e-06)
     normed = (gathered_f * scale * norm_gain[None, :]).astype(jnp.bfloat16)
@@ -82,10 +90,12 @@
     long_out = local + carried + skip_gain[None, :] * driven
     hidden = (query * long_out).astype(jnp.bfloat16)
     partial = jnp.dot(hidden, out_weight, preferred_element_type=jnp.float32).astype(jnp.bfloat16)
-    parts = lax.all_to_all(partial, "chan", 1, 0, tiled=True)
-    mixed = jnp.sum(
-        parts.reshape(chan_devices, token_rows, channels).astype(jnp.float32), axis=0
-    )
+    slabs = partial.reshape(token_rows, 2, half, channels).transpose(2, 0, 1, 3)
+    parts = lax.all_to_all(slabs, "chan", 0, 0, axis_index_groups=groups)
+    group_sum = jnp.sum(parts.astype(jnp.float32), axis=0)
+    mine = jnp.where(upper, group_sum[:, 1], group_sum[:, 0])
+    theirs = jnp.where(upper, group_sum[:, 0], group_sum[:, 1])
+    mixed = mine + lax.ppermute(theirs, "chan", partners)
     return (stream.astype(jnp.float32) + mixed).astype(jnp.bfloat16)
 
 

time: 159 us -> 176 us (1.11)
  waiting for transfers between devices: 53.2 us -> 64.2 us
  local copies, waits for them, and re-layouts: 6.52 us -> 11.9 us
  starting transfers between devices: 18 us -> 22.2 us
  blocking collectives: 57.8 us -> 54.2 us
    ppermute x0 -> x2, waiting for transfers between devices: none -> 10.8 us  [the longest x1 7.08 us: on_device(): mixed = mine + lax.ppermute(theirs, 'chan', partners)]
    ppermute x0 -> x2, starting transfers between devices: none -> 5.93 us  [the longest x1 3.11 us: on_device(): other = lax.ppermute(stream, 'chan', partners)]
    all_to_all x1, blocking collectives: 57.8 us -> 54.2 us  [on_device(): parts = lax.all_to_all(slabs, 'chan', 0, 0, axis_index_groups=groups)]
    all_to_all x1, starting transfers between devices: 11.1 us -> 8.46 us  [on_device(): lax.all_to_all(jnp.broadcast_to(pair[None], (half,) + pair.shape), 'chan'...]
    broadcast_in_dim x0 -> x1, local copies, waits for them, and re-layouts: none -> 2.38 us  [on_device(): jnp.broadcast_to(pair[None], (half,) + pair.shape)]
    all_to_all x2 -> x1, local copies, waits for them, and re-layouts: 4.13 us -> 6.11 us  [on_device(): lax.all_to_all(jnp.broadcast_to(pair[None], (half,) + pair.shape), 'chan'...]
  transfers between devices with their start and end apart: 3 -> 5, of which waited for: 2 -> 4; matrix products, arithmetic and copies ran while one was open for 3% -> 3% of each run, Pallas kernels for 0% -> 0%
where the time goes in v3:
time: 176 us; the launch traced here: 175 us
  waiting for transfers between devices  64.2 us (36%)
  blocking collectives  54.2 us (31%)
  starting transfers between devices  22.2 us (13%)
  matrix products  12.2 us (7%)
  local copies, waits for them, and re-layouts  11.9 us (7%)
  other arithmetic  10.1 us (6%)
    all_to_all x1, blocking collectives, on_device(): parts = lax.all_to_all(slabs, 'chan', 0, 0, axis_index_groups=groups)  54.2 us
    all_to_all x1, waiting for transfers between devices, on_device(): lax.all_to_all(jnp.broadcast_to(pair[None], (half,) + pair.shape), 'chan'...  50.5 us
    all_to_all x1, starting transfers between devices, on_device(): lax.all_to_all(jnp.broadcast_to(pair[None], (half,) + pair.shape), 'chan'...  8.46 us
    ppermute x1, waiting for transfers between devices, on_device(): mixed = mine + lax.ppermute(theirs, 'chan', partners)  7.08 us
    all_to_all x1, local copies, waits for them, and re-layouts, on_device(): lax.all_to_all(jnp.broadcast_to(pair[None], (half,) + pair.shape), 'chan'...  6.11 us
    all_to_all x1, starting transfers between devices, on_device(): lax.all_to_all(jnp.tile(device_end, (seq_devices, 1)), 'seq', 0, 0, tiled...  5.86 us
    dot_general x1, matrix products, on_device(): jnp.dot(lower, lifted.reshape(token_rows, modes * channels), precision=la...  5.44 us
    dot_general x1, matrix products, on_device(): jnp.einsum('td,djc->tjc', normed, in_weight, preferred_element_type=jnp.f...  4.63 us
  transfers between devices with their start and end apart: 5, of which 4 were waited for; matrix products, arithmetic and copies ran while one was open for 3% of the time, Pallas kernels for 0%

profile of v3, /device:TPU:8, one launch (start us, length us, event | category | flops | bytes accessed | tf_op | source)
XLA Modules:
  0.0 175.0 jit_solution(2268077421963881149)
XLA Ops:
  0.0 0.0 copy-start
  0.0 0.0 copy-start.3
  0.0 1.4 convolution_convert_fusion.1
  1.4 3.1 %collective-permute-start = (bf16[256,256]{1,0:T(8,128)(2,1)S(1)}, bf16[256,256]{1,0:T(8,128)(2,1)S(1)}, u32[]{:S(2)}, u32[]{:S(2)}) collective-permute-start(bf16[256,256]{1,0:T(8,128)(2,1)S(1)} %convolution_convert_fusion.1), channel_id=1, source_target_pairs={{0,8},{1,9},{2,10},{3,11},{4,12},{5,13},{6,14},{7,15},{8,0},{9,1},... | collective-permute-start | bytes 393224 | tf_op jit(solution)/shard_map/ppermute | solution.py:41
  4.5 3.7 %collective-permute-done = bf16[256,256]{1,0:T(8,128)(2,1)S(1)} collective-permute-done((bf16[256,256]{1,0:T(8,128)(2,1)S(1)}, bf16[256,256]{1,0:T(8,128)(2,1)S(1)}, u32[]{:S(2)}, u32[]{:S(2)}) %collective-permute-start) | collective-permute-done | bytes 131104 | tf_op jit(solution)/shard_map/ppermute | solution.py:41
  8.3 0.3 copy.32
  8.6 2.4 %broadcast_in_dim.10 = bf16[8,2,256,256]{3,1,2,0:T(2,128)(2,1)} broadcast(bf16[2,256,256]{2,0,1:T(2,128)(2,1)S(1)} %copy.32), dimensions={1,2,3} | broadcast | bytes 2359296 | tf_op jit(solution)/shard_map/broadcast_in_dim | solution.py:44
  10.9 8.5 %all-to-all-start = ((bf16[8,2,256,256]{3,1,2,0:T(2,128)(2,1)}), bf16[8,2,256,256]{3,1,2,0:T(2,128)(2,1)}, u32[]{:S(2)}, u32[]{:S(2)}) async-start(bf16[8,2,256,256]{3,1,2,0:T(2,128)(2,1)} %broadcast_in_dim.10), calls=%async_computation | async-start | bytes 4194304 | tf_op jit(solution)/shard_map/all_to_all | solution.py:43
  19.4 0.0 copy-start.2
  19.4 0.0 copy-done.3
  19.4 50.5 %all-to-all-done = bf16[8,2,256,256]{3,1,2,0:T(2,128)(2,1)} async-done(((bf16[8,2,256,256]{3,1,2,0:T(2,128)(2,1)}), bf16[8,2,256,256]{3,1,2,0:T(2,128)(2,1)}, u32[]{:S(2)}, u32[]{:S(2)}) %all-to-all-start) | async-done | bytes 2097184 | tf_op jit(solution)/shard_map/all_to_all | solution.py:43
  69.9 6.1 %copy.33 = bf16[8,2,256,256]{2,3,0,1:T(8,128)(2,1)} copy(bf16[8,2,256,256]{3,1,2,0:T(2,128)(2,1)} %all-to-all-done) | data formatting | bytes 4194304 | tf_op jit(solution)/shard_map/all_to_all | solution.py:43
  76.0 2.2 %multiply_reduce_fusion.3 = f32[256]{0:T(256)S(1)} fusion(bf16[8,2,256,256]{2,3,0,1:T(8,128)(2,1)} %copy.33), kind=kLoop, calls=%fused_computation.10 | loop fusion | flops 3145472 | bytes 2098176 | tf_op jit(solution)/shard_map/reduce_sum | solution.py:49
  78.2 0.0 copy-done.2
  78.2 1.9 %fusion.1 = bf16[256,4096]{0,1:T(8,128)(2,1)S(1)} fusion(f32[4096]{0:T(1024)S(1)} %copy-done.2, f32[256]{0:T(256)S(1)} %add_rsqrt_fusion, bf16[8,2,256,256]{2,3,0,1:T(8,128)(2,1)} %copy.33), kind=kLoop, calls=%fused_computation.3 | loop fusion | flops 4194304 | bytes 4211712 | tf_op jit(solution)/shard_map/convert_element_type | solution.py:50
  80.1 0.0 copy-start.1
  80.2 4.6 %fusion.4 = bf16[256,3,256]{2,0,1:T(8,128)(2,1)S(1)} fusion(bf16[4096,3,256]{2,0,1:T(8,128)(2,1)} %param.12, bf16[256,4096]{0,1:T(8,128)(2,1)S(1)} %fusion.1), kind=kOutput, calls=%fused_computation.14 | convolution fusion | flops 1610809344 | bytes 8781824 | tf_op jit(solution)/shard_map/td,djc->tjc/dot_general | solution.py:51
  84.8 1.9 %collective-permute-start.1 = (bf16[2,3,256]{2,0,1:T(2,128)(2,1)S(1)}, bf16[2,3,256]{2,0,1:T(2,128)(2,1)S(1)}, u32[]{:S(2)}, u32[]{:S(2)}) collective-permute-start(bf16[2,3,256]{2,0,1:T(2,128)(2,1)S(1)} %slice.50), channel_id=1, source_target_pairs={{0,16},{16,32},{32,48},{48,64},{64,80},{80,96},{96,112},{112,128},... | collective-permute-start | bytes 9224 | tf_op jit(solution)/shard_map/ppermute | solution.py:12
  86.7 0.0 copy-done.1
  86.8 2.9 %collective-permute-done.1 = bf16[2,3,256]{2,0,1:T(2,128)(2,1)S(1)} collective-permute-done((bf16[2,3,256]{2,0,1:T(2,128)(2,1)S(1)}, bf16[2,3,256]{2,0,1:T(2,128)(2,1)S(1)}, u32[]{:S(2)}, u32[]{:S(2)}) %collective-permute-start.1) | collective-permute-done | bytes 3104 | tf_op jit(solution)/shard_map/ppermute | solution.py:12
  89.7 0.1 maximum_convert_fusion
  89.8 0.3 fusion.8
  90.1 0.0 copy-start.5
  90.1 0.1 copy.35
  90.3 1.3 multiply_reduce_fusion.1
  91.6 2.3 %bitcast_multiply_fusion.1 = f32[256,4096]{0,1:T(8,128)} fusion(f32[256,256]{0,1:T(8,128)S(1)} %copy.35, f32[4096]{0:T(1024)S(1)} %bitcast.67), kind=kLoop, calls=%fused_computation.4 | loop fusion | flops 2097152 | bytes 4472832 | tf_op jit(solution)/shard_map/mul | solution.py:73
  93.9 0.7 tile.2
  94.6 5.9 %all-to-all-start.1 = ((f32[16,16,256]{2,1,0:T(8,128)}), f32[16,16,256]{2,1,0:T(8,128)S(1)}, u32[]{:S(2)}, u32[]{:S(2)}) async-start(f32[16,16,256]{2,1,0:T(8,128)} %tile.2), calls=%async_computation.1 | async-start | bytes 524288 | tf_op jit(solution)/shard_map/all_to_all | solution.py:79
  100.5 0.0 copy-start.4
  100.5 0.0 copy-done.5
  100.5 5.4 %multiply_reduce_fusion.2 = f32[256,256]{1,0:T(8,128)S(1)} fusion(f32[16,256,256]{2,1,0:T(8,128)} %bitcast.63, f32[16,256]{1,0:T(8,128)S(1)} %get-tuple-element.6, f32[16,256]{1,0:T(8,128)S(1)} %copy-done.5), kind=kOutput, calls=%fused_computation.8 | convolution fusion | flops 3225419776 | bytes 4489216 | tf_op jit(solution)/shard_map/dot_general | solution.py:74
  105.9 0.0 all-to-all-done.1
  105.9 0.1 multiply_reduce_fusion.4
  106.1 0.9 multiply_reduce_fusion
  107.0 0.0 copy-done
  107.0 0.0 copy-done.4
  107.0 0.7 convolution_convert_fusion
  107.7 0.6 copy.49
  108.4 1.6 copy.52
  110.0 54.2 %all_to_all.16 = bf16[8,256,2,256]{3,2,1,0:T(2,128)(2,1)S(1)} all-to-all(bf16[8,256,2,256]{3,2,1,0:T(2,128)(2,1)S(1)} %bitcast.62), channel_id=1, replica_groups={{0,1,2,3,4,5,6,7},{8,9,10,11,12,13,14,15},{16,17,18,19,20,21,22,23},{24..., dimensions={0} | all-to-all | bytes 4194304 | tf_op jit(solution)/shard_map/all_to_all | solution.py:94
  164.1 0.2 convert_reduce_fusion
  164.3 2.8 %collective-permute-start.2 = (f32[256,256]{1,0:T(8,128)S(1)}, f32[256,256]{1,0:T(8,128)S(1)}, u32[]{:S(2)}, u32[]{:S(2)}) collective-permute-start(f32[256,256]{1,0:T(8,128)S(1)} %select_bitcast_fusion), channel_id=1, source_target_pairs={{0,8},{1,9},{2,10},{3,11},{4,12},{5,13},{6,14},{7,15},{8,0},{9,1},... | collective-permute-start | bytes 786440 | tf_op jit(solution)/shard_map/ppermute | solution.py:98
  167.2 7.1 %collective-permute-done.2 = f32[256,256]{1,0:T(8,128)S(1)} collective-permute-done((f32[256,256]{1,0:T(8,128)S(1)}, f32[256,256]{1,0:T(8,128)S(1)}, u32[]{:S(2)}, u32[]{:S(2)}) %collective-permute-start.2) | collective-permute-done | bytes 262176 | tf_op jit(solution)/shard_map/ppermute | solution.py:98
  174.2 0.7 fusion.12
  (11 shorter events, 0.2 us)
Async XLA Ops:
  0.0 107.0 %copy-start = (bf16[256,4096]{1,0:T(8,128)(2,1)S(1)}, bf16[256,4096]{1,0:T(8,128)(2,1)}, u32[]{:S(2)}) copy-start(bf16[256,4096]{1,0:T(8,128)(2,1)} %param.17) | copy-start | bytes 6291460
  0.0 19.4 %copy-start.3 = (f32[3,3,256]{2,1,0:T(4,128)S(1)}, f32[3,3,256]{2,1,0:T(4,128)}, u32[]{:S(2)}) copy-start(f32[3,3,256]{2,1,0:T(4,128)} %param.13) | copy-start | bytes 27652
  1.4 6.8 %collective-permute-start = (bf16[256,256]{1,0:T(8,128)(2,1)S(1)}, bf16[256,256]{1,0:T(8,128)(2,1)S(1)}, u32[]{:S(2)}, u32[]{:S(2)}) collective-permute-start(bf16[256,256]{1,0:T(8,128)(2,1)S(1)} %convolution_convert_fusion.1), channel_id=1, source_target_pairs={{0,8},{1,9},{2,10},{3,11},{4,12},{5,13},{6,14},{7,15},{8,0},{9,1},... | collective-permute-start | bytes 393224 | tf_op jit(solution)/shard_map/ppermute | solution.py:41
  10.9 59.0 %all-to-all-start = ((bf16[8,2,256,256]{3,1,2,0:T(2,128)(2,1)}), bf16[8,2,256,256]{3,1,2,0:T(2,128)(2,1)}, u32[]{:S(2)}, u32[]{:S(2)}) async-start(bf16[8,2,256,256]{3,1,2,0:T(2,128)(2,1)} %broadcast_in_dim.10), calls=%async_computation | async-start | bytes 4194304 | tf_op jit(solution)/shard_map/all_to_all | solution.py:43
  19.4 58.8 %copy-start.2 = (f32[4096]{0:T(1024)S(1)}, f32[4096]{0:T(1024)}, u32[]{:S(2)}) copy-start(f32[4096]{0:T(1024)} %param.11) | copy-start | bytes 49156
  80.1 6.6 %copy-start.1 = (f32[16,256]{1,0:T(8,128)S(1)}, f32[16,256]{1,0:T(8,128)}, u32[]{:S(2)}) copy-start(f32[16,256]{1,0:T(8,128)} %param.14) | copy-start | bytes 49156
  84.8 4.9 %collective-permute-start.1 = (bf16[2,3,256]{2,0,1:T(2,128)(2,1)S(1)}, bf16[2,3,256]{2,0,1:T(2,128)(2,1)S(1)}, u32[]{:S(2)}, u32[]{:S(2)}) collective-permute-start(bf16[2,3,256]{2,0,1:T(2,128)(2,1)S(1)} %slice.50), channel_id=1, source_target_pairs={{0,16},{16,32},{32,48},{48,64},{64,80},{80,96},{96,112},{112,128},... | collective-permute-start | bytes 9224 | tf_op jit(solution)/shard_map/ppermute | solution.py:12
  90.1 10.4 %copy-start.5 = (f32[16,256]{1,0:T(8,128)S(1)}, f32[16,256]{1,0:T(8,128)}, u32[]{:S(2)}) copy-start(f32[16,256]{1,0:T(8,128)} %param.15) | copy-start | bytes 49156
  94.6 11.3 %all-to-all-start.1 = ((f32[16,16,256]{2,1,0:T(8,128)}), f32[16,16,256]{2,1,0:T(8,128)S(1)}, u32[]{:S(2)}, u32[]{:S(2)}) async-start(f32[16,16,256]{2,1,0:T(8,128)} %tile.2), calls=%async_computation.1 | async-start | bytes 524288 | tf_op jit(solution)/shard_map/all_to_all | solution.py:79
  100.5 6.5 %copy-start.4 = (f32[256]{0:T(256)S(1)}, f32[256]{0:T(256)}, u32[]{:S(2)}) copy-start(f32[256]{0:T(256)} %param.16) | copy-start | bytes 3076
  164.3 9.9 %collective-permute-start.2 = (f32[256,256]{1,0:T(8,128)S(1)}, f32[256,256]{1,0:T(8,128)S(1)}, u32[]{:S(2)}, u32[]{:S(2)}) collective-permute-start(f32[256,256]{1,0:T(8,128)S(1)} %select_bitcast_fusion), channel_id=1, source_target_pairs={{0,8},{1,9},{2,10},{3,11},{4,12},{5,13},{6,14},{7,15},{8,0},{9,1},... | collective-permute-start | bytes 786440 | tf_op jit(solution)/shard_map/ppermute | solution.py:98

commit v4 on v2

--- a/solution.py
+++ b/solution.py
@@ -10,6 +10,35 @@
     devices = lax.axis_size(axis)
     pairs = [(i, i + by) for i in range(devices) if 0 <= i + by < devices]
     return lax.ppermute(value, axis, pairs)
+
+
+def gather_chan(block, chan_devices):
+    ring = chan_devices // 2
+    upper = lax.axis_index("chan") >= ring
+    where_in_ring = lax.axis_index("chan") % ring
+
+    def along_ring(value, by):
+        pairs = [
+            (side * ring + z, side * ring + (z + by) % ring)
+            for side in range(2)
+            for z in range(ring)
+        ]
+        return lax.ppermute(value, "chan", pairs)
+
+    other = lax.ppermute(block, "chan", [(i, (i + ring) % chan_devices) for i in range(chan_devices)])
+    pair = jnp.where(upper, jnp.stack([other, block]), jnp.stack([block, other]))
+    ahead, behind = [], []
+    fwd, bwd = pair, pair
+    for step in range(1, ring // 2 + 1):
+        fwd = along_ring(fwd, 1)
+        behind.append(fwd)
+        if step < ring - ring // 2:
+            bwd = along_ring(bwd, -1)
+            ahead.append(bwd)
+    by_offset = jnp.stack([pair] + ahead + behind[::-1])
+    by_place = jnp.roll(by_offset, where_in_ring, axis=0)
+    rows = block.shape[0]
+    return by_place.transpose(2, 1, 0, 3).reshape(rows, chan_devices * block.shape[1])
 
 
 def on_device(
@@ -34,9 +63,7 @@
     )
     stream = jnp.dot(one_hot, embedding, preferred_element_type=jnp.float32).astype(jnp.bfloat16)
     chan_devices = lax.axis_size("chan")
-    gathered = lax.all_to_all(
-        jnp.tile(stream, (chan_devices, 1)), "chan", 0, 1, tiled=True
-    )
+    gathered = gather_chan(stream, chan_devices)
     gathered_f = gathered.astype(jnp.float32)
     scale = lax.rsqrt(jnp.mean(gathered_f * gathered_f, axis=1, keepdims=True) + 1e-06)
     normed = (gathered_f * scale * norm_gain[None, :]).astype(jnp.bfloat16)

time: 159 us -> 131 us (0.82)
  waiting for transfers between devices: 53.2 us -> 29.1 us
  starting transfers between devices: 18 us -> 23.5 us
  matrix products: 12.2 us -> 7.32 us
  other arithmetic: 10.1 us -> 5.81 us
  local copies, waits for them, and re-layouts: 6.52 us -> 4.45 us
    all_to_all x1 -> x0, waiting for transfers between devices: 50.3 us -> none  [on_device(): lax.all_to_all(jnp.tile(stream, (chan_devices, 1)), 'chan', 0, 1, tiled=T...]
    ppermute x0 -> x8, waiting for transfers between devices: none -> 24.7 us  [the longest x7 20.9 us: along_ring(): return lax.ppermute(value, 'chan', pairs)]
    ppermute x0 -> x8, starting transfers between devices: none -> 15.7 us  [the longest x7 12.6 us: along_ring(): return lax.ppermute(value, 'chan', pairs)]
    all_to_all x1 -> x0, starting transfers between devices: 11.1 us -> none  [on_device(): lax.all_to_all(jnp.tile(stream, (chan_devices, 1)), 'chan', 0, 1, tiled=T...]
    all_to_all x1 -> x0, local copies, waits for them, and re-layouts: 3.92 us -> none  [on_device(): lax.all_to_all(jnp.tile(stream, (chan_devices, 1)), 'chan', 0, 1, tiled=T...]
    dot_general x1, matrix products: 4.63 us -> 1.84 us  [on_device(): jnp.einsum('td,djc->tjc', normed, in_weight, preferred_element_type=jnp.f...]
    dot_general x1, matrix products: 5.44 us -> 3.26 us  [on_device(): jnp.dot(lower, lifted.reshape(token_rows, modes * channels), precision=la...]
    mul x2, other arithmetic: 2.33 us -> 0.66 us  [on_device(): lifted = rise * driven[:, None, :]]
  transfers between devices with their start and end apart: 3 -> 10, of which waited for: 2 -> 7; matrix products, arithmetic and copies ran while one was open for 3% -> 4% of each run, Pallas kernels for 0% -> 0%
where the time goes in v4:
time: 131 us; the launch traced here: 130 us
  blocking collectives  59.2 us (45%)
  waiting for transfers between devices  29.1 us (22%)
  starting transfers between devices  23.5 us (18%)
  matrix products  7.32 us (6%)
  other arithmetic  5.81 us (4%)
  local copies, waits for them, and re-layouts  4.45 us (3%)
    all_to_all x1, blocking collectives, on_device(): parts = lax.all_to_all(partial, 'chan', 1, 0, tiled=True)  59.2 us
    ppermute x7, waiting for transfers between devices, along_ring(): return lax.ppermute(value, 'chan', pairs)  20.9 us
    ppermute x7, starting transfers between devices, along_ring(): return lax.ppermute(value, 'chan', pairs)  12.6 us
    all_to_all x1, starting transfers between devices, on_device(): lax.all_to_all(jnp.tile(device_end, (seq_devices, 1)), 'seq', 0, 0, tiled...  5.86 us
    ppermute x1, waiting for transfers between devices, gather_chan(): lax.ppermute(block, 'chan', [(i, (i + ring) % chan_devices) for i in rang...  3.72 us
    dot_general x1, matrix products, on_device(): jnp.dot(lower, lifted.reshape(token_rows, modes * channels), precision=la...  3.26 us
    ppermute x1, starting transfers between devices, gather_chan(): lax.ppermute(block, 'chan', [(i, (i + ring) % chan_devices) for i in rang...  3.1 us
    ppermute x1, waiting for transfers between devices, from_behind(): return lax.ppermute(value, axis, pairs)  2.94 us
  transfers between devices with their start and end apart: 10, of which 7 were waited for; matrix products, arithmetic and copies ran while one was open for 4% of the time, Pallas kernels for 0%

profile of v4, /device:TPU:8, one launch (start us, length us, event | category | flops | bytes accessed | tf_op | source)
XLA Modules:
  0.0 129.8 jit_solution(10982365993183454987)
XLA Ops:
  0.0 0.0 copy-start
  0.0 1.5 %convolution_convert_fusion.1 = bf16[256,256]{0,1:T(8,128)(2,1)S(1)} fusion(bf16[512,256]{1,0:T(8,128)(2,1)} %param.10, s32[256]{0:T(256)} %param.9), kind=kOutput, calls=%fused_computation.17 | convolution fusion | flops 67305472 | bytes 394240 | tf_op jit(solution)/shard_map/dot_general | solution.py:64
  1.5 3.1 %collective-permute-start = (bf16[256,256]{0,1:T(8,128)(2,1)S(1)}, bf16[256,256]{0,1:T(8,128)(2,1)S(1)}, u32[]{:S(2)}, u32[]{:S(2)}) collective-permute-start(bf16[256,256]{0,1:T(8,128)(2,1)S(1)} %convolution_convert_fusion.1), channel_id=1, source_target_pairs={{0,8},{1,9},{2,10},{3,11},{4,12},{5,13},{6,14},{7,15},{8,0},{9,1},... | collective-permute-start | bytes 393224 | tf_op jit(solution)/shard_map/ppermute | solution.py:28
  4.6 3.7 %collective-permute-done = bf16[256,256]{0,1:T(8,128)(2,1)S(1)} collective-permute-done((bf16[256,256]{0,1:T(8,128)(2,1)S(1)}, bf16[256,256]{0,1:T(8,128)(2,1)S(1)}, u32[]{:S(2)}, u32[]{:S(2)}) %collective-permute-start) | collective-permute-done | bytes 131104 | tf_op jit(solution)/shard_map/ppermute | solution.py:28
  8.3 2.0 %collective-permute-start.4 = (bf16[2,256,256]{1,2,0:T(8,128)(2,1)S(1)}, bf16[2,256,256]{1,2,0:T(8,128)(2,1)S(1)}, u32[]{:S(2)}, u32[]{:S(2)}) collective-permute-start(bf16[2,256,256]{1,2,0:T(8,128)(2,1)S(1)} %maximum_select_fusion.1), channel_id=1, source_target_pairs={{0,1},{1,2},{2,3},{3,4},{4,5},{5,6},{6,7},{7,0},{8,9},{9,10},{10,1... | collective-permute-start | bytes 786440 | tf_op jit(solution)/shard_map/ppermute | solution.py:26
  10.3 4.0 %collective-permute-start.1 = (bf16[2,256,256]{1,2,0:T(8,128)(2,1)S(1)}, bf16[2,256,256]{1,2,0:T(8,128)(2,1)S(1)}, u32[]{:S(2)}, u32[]{:S(2)}) collective-permute-start(bf16[2,256,256]{1,2,0:T(8,128)(2,1)S(1)} %maximum_select_fusion.1), channel_id=1, source_target_pairs={{0,7},{1,0},{2,1},{3,2},{4,3},{5,4},{6,5},{7,6},{8,15},{9,8},{10,9... | collective-permute-start | bytes 786440 | tf_op jit(solution)/shard_map/ppermute | solution.py:26
  14.4 5.4 %collective-permute-done.4 = bf16[2,256,256]{1,2,0:T(8,128)(2,1)S(1)} collective-permute-done((bf16[2,256,256]{1,2,0:T(8,128)(2,1)S(1)}, bf16[2,256,256]{1,2,0:T(8,128)(2,1)S(1)}, u32[]{:S(2)}, u32[]{:S(2)}) %collective-permute-start.4) | collective-permute-done | bytes 262176 | tf_op jit(solution)/shard_map/ppermute | solution.py:26
  19.7 0.0 collective-permute-start.5
  19.7 0.0 collective-permute-done.1
  19.7 3.2 %collective-permute-start.2 = (bf16[2,256,256]{1,2,0:T(8,128)(2,1)S(1)}, bf16[2,256,256]{1,2,0:T(8,128)(2,1)S(1)}, u32[]{:S(2)}, u32[]{:S(2)}) collective-permute-start(bf16[2,256,256]{1,2,0:T(8,128)(2,1)S(1)} %collective-permute-done.1), channel_id=1, source_target_pairs={{0,7},{1,0},{2,1},{3,2},{4,3},{5,4},{6,5},{7,6},{8,15},{9,8},{10,9... | collective-permute-start | bytes 786440 | tf_op jit(solution)/shard_map/ppermute | solution.py:26
  23.0 0.7 slice_bitcast_fusion.4
  23.7 3.9 %collective-permute-done.5 = bf16[2,256,256]{1,2,0:T(8,128)(2,1)S(1)} collective-permute-done((bf16[2,256,256]{1,2,0:T(8,128)(2,1)S(1)}, bf16[2,256,256]{1,2,0:T(8,128)(2,1)S(1)}, u32[]{:S(2)}, u32[]{:S(2)}) %collective-permute-start.5) | collective-permute-done | bytes 262176 | tf_op jit(solution)/shard_map/ppermute | solution.py:26
  27.6 0.0 collective-permute-start.6
  27.6 0.0 collective-permute-done.2
  27.6 3.3 %collective-permute-start.3 = (bf16[2,256,256]{1,2,0:T(8,128)(2,1)S(1)}, bf16[2,256,256]{1,2,0:T(8,128)(2,1)S(1)}, u32[]{:S(2)}, u32[]{:S(2)}) collective-permute-start(bf16[2,256,256]{1,2,0:T(8,128)(2,1)S(1)} %collective-permute-done.2), channel_id=1, source_target_pairs={{0,7},{1,0},{2,1},{3,2},{4,3},{5,4},{6,5},{7,6},{8,15},{9,8},{10,9... | collective-permute-start | bytes 786440 | tf_op jit(solution)/shard_map/ppermute | solution.py:26
  31.0 4.2 %collective-permute-done.6 = bf16[2,256,256]{1,2,0:T(8,128)(2,1)S(1)} collective-permute-done((bf16[2,256,256]{1,2,0:T(8,128)(2,1)S(1)}, bf16[2,256,256]{1,2,0:T(8,128)(2,1)S(1)}, u32[]{:S(2)}, u32[]{:S(2)}) %collective-permute-start.6) | collective-permute-done | bytes 262176 | tf_op jit(solution)/shard_map/ppermute | solution.py:26
  35.2 0.0 collective-permute-start.7
  35.2 0.0 collective-permute-done.3
  35.2 7.5 %collective-permute-done.7 = bf16[2,256,256]{1,2,0:T(8,128)(2,1)S(1)} collective-permute-done((bf16[2,256,256]{1,2,0:T(8,128)(2,1)S(1)}, bf16[2,256,256]{1,2,0:T(8,128)(2,1)S(1)}, u32[]{:S(2)}, u32[]{:S(2)}) %collective-permute-start.7) | collective-permute-done | bytes 262176 | tf_op jit(solution)/shard_map/ppermute | solution.py:26
  42.8 0.1 fusion.18
  43.1 0.6 fusion
  43.7 0.0 slice-start
  43.7 0.5 convert_bitcast_fusion
  44.1 0.0 copy-start.2
  44.2 0.0 slice-start.1
  44.2 0.4 copy.21
  44.6 0.5 copy-done.2
  45.1 1.0 fusion.2
  46.1 0.0 slice-done
  46.1 0.6 slice-done.1
  46.7 0.0 copy-start.1
  46.7 1.8 %fusion.5 = bf16[256,3,256]{2,0,1:T(8,128)(2,1)S(1)} fusion(bf16[4096,3,256]{2,0,1:T(8,128)(2,1)S(1)} %bitcast.74, bf16[256,4096]{0,1:T(8,128)(2,1)S(1)} %fusion.2), kind=kOutput, calls=%fused_computation.16 | convolution fusion | flops 1610809344 | bytes 8781824 | tf_op jit(solution)/shard_map/td,djc->tjc/dot_general | solution.py:70
  48.5 1.9 %collective-permute-start.8 = (bf16[2,3,256]{2,0,1:T(2,128)(2,1)S(1)}, bf16[2,3,256]{2,0,1:T(2,128)(2,1)S(1)}, u32[]{:S(2)}, u32[]{:S(2)}) collective-permute-start(bf16[2,3,256]{2,0,1:T(2,128)(2,1)S(1)} %slice.40), channel_id=1, source_target_pairs={{0,16},{16,32},{32,48},{48,64},{64,80},{80,96},{96,112},{112,128},... | collective-permute-start | bytes 9224 | tf_op jit(solution)/shard_map/ppermute | solution.py:12
  50.5 0.0 copy-done.1
  50.5 2.9 %collective-permute-done.8 = bf16[2,3,256]{2,0,1:T(2,128)(2,1)S(1)} collective-permute-done((bf16[2,3,256]{2,0,1:T(2,128)(2,1)S(1)}, bf16[2,3,256]{2,0,1:T(2,128)(2,1)S(1)}, u32[]{:S(2)}, u32[]{:S(2)}) %collective-permute-start.8) | collective-permute-done | bytes 3104 | tf_op jit(solution)/shard_map/ppermute | solution.py:12
  53.5 0.1 maximum_convert_fusion
  53.5 0.3 fusion.9
  53.8 0.0 copy-start.4
  53.9 0.1 copy.23
  54.0 1.3 %multiply_reduce_fusion.1 = f32[16,256]{1,0:T(8,128)S(1)} fusion(f32[16,256]{1,0:T(8,128)S(1)} %copy-done.1, f32[256,256]{0,1:T(8,128)S(1)} %copy.23), kind=kLoop, calls=%fused_computation.10 | loop fusion | flops 3141632 | bytes 294912 | tf_op jit(solution)/shard_map/reduce_sum | solution.py:97
  55.3 0.7 tile.2
  56.0 5.9 %all-to-all-start = ((f32[16,16,256]{2,1,0:T(8,128)}), f32[16,16,256]{2,1,0:T(8,128)S(1)}, u32[]{:S(2)}, u32[]{:S(2)}) async-start(f32[16,16,256]{2,1,0:T(8,128)} %tile.2), calls=%async_computation | async-start | bytes 524288 | tf_op jit(solution)/shard_map/all_to_all | solution.py:98
  61.9 0.6 bitcast_multiply_fusion
  62.5 0.0 copy-start.3
  62.6 0.0 copy-done.4
  62.6 3.3 %multiply_reduce_fusion.2 = f32[256,256]{1,0:T(8,128)S(1)} fusion(f32[16,256,256]{2,1,0:T(8,128)S(1)} %bitcast.77, f32[16,256]{1,0:T(8,128)S(1)} %get-tuple-element.6, f32[16,256]{1,0:T(8,128)S(1)} %copy-done.4), kind=kOutput, calls=%fused_computation.11 | convolution fusion | flops 3225419776 | bytes 4489216 | tf_op jit(solution)/shard_map/dot_general | solution.py:93
  65.8 1.5 %all-to-all-done = f32[16,16,256]{2,1,0:T(8,128)S(1)} async-done(((f32[16,16,256]{2,1,0:T(8,128)}), f32[16,16,256]{2,1,0:T(8,128)S(1)}, u32[]{:S(2)}, u32[]{:S(2)}) %all-to-all-start) | async-done | bytes 262176 | tf_op jit(solution)/shard_map/all_to_all | solution.py:98
  67.3 0.1 multiply_reduce_fusion.3
  67.5 0.9 multiply_reduce_fusion
  68.3 0.0 copy-done
  68.4 0.0 copy-done.3
  68.4 0.7 convolution_convert_fusion
  69.1 0.2 copy.34
  69.3 59.2 %all_to_all.19 = bf16[256,16,256]{2,0,1:T(8,128)(2,1)S(1)} all-to-all(bf16[256,16,256]{2,0,1:T(8,128)(2,1)S(1)} %bitcast.76), channel_id=1, replica_groups=mesh['seq'=16,'chan'=16] {'chan'}, dimensions={1} | all-to-all | bytes 4194304 | tf_op jit(solution)/shard_map/all_to_all | solution.py:112
  128.6 0.3 convert_reduce_fusion
  128.8 0.1 copy.26
  129.0 0.8 copy.27
  (26 shorter events, 0.5 us)
Async XLA Ops:
  0.0 68.3 %copy-start = (bf16[256,4096]{1,0:T(8,128)(2,1)S(1)}, bf16[256,4096]{1,0:T(8,128)(2,1)}, u32[]{:S(2)}) copy-start(bf16[256,4096]{1,0:T(8,128)(2,1)} %param.17) | copy-start | bytes 6291460
  1.5 6.8 %collective-permute-start = (bf16[256,256]{0,1:T(8,128)(2,1)S(1)}, bf16[256,256]{0,1:T(8,128)(2,1)S(1)}, u32[]{:S(2)}, u32[]{:S(2)}) collective-permute-start(bf16[256,256]{0,1:T(8,128)(2,1)S(1)} %convolution_convert_fusion.1), channel_id=1, source_target_pairs={{0,8},{1,9},{2,10},{3,11},{4,12},{5,13},{6,14},{7,15},{8,0},{9,1},... | collective-permute-start | bytes 393224 | tf_op jit(solution)/shard_map/ppermute | solution.py:28
  8.3 11.4 %collective-permute-start.4 = (bf16[2,256,256]{1,2,0:T(8,128)(2,1)S(1)}, bf16[2,256,256]{1,2,0:T(8,128)(2,1)S(1)}, u32[]{:S(2)}, u32[]{:S(2)}) collective-permute-start(bf16[2,256,256]{1,2,0:T(8,128)(2,1)S(1)} %maximum_select_fusion.1), channel_id=1, source_target_pairs={{0,1},{1,2},{2,3},{3,4},{4,5},{5,6},{6,7},{7,0},{8,9},{9,10},{10,1... | collective-permute-start | bytes 786440 | tf_op jit(solution)/shard_map/ppermute | solution.py:26
  10.3 9.4 %collective-permute-start.1 = (bf16[2,256,256]{1,2,0:T(8,128)(2,1)S(1)}, bf16[2,256,256]{1,2,0:T(8,128)(2,1)S(1)}, u32[]{:S(2)}, u32[]{:S(2)}) collective-permute-start(bf16[2,256,256]{1,2,0:T(8,128)(2,1)S(1)} %maximum_select_fusion.1), channel_id=1, source_target_pairs={{0,7},{1,0},{2,1},{3,2},{4,3},{5,4},{6,5},{7,6},{8,15},{9,8},{10,9... | collective-permute-start | bytes 786440 | tf_op jit(solution)/shard_map/ppermute | solution.py:26
  19.7 7.8 %collective-permute-start.5 = (bf16[2,256,256]{1,2,0:T(8,128)(2,1)S(1)}, bf16[2,256,256]{1,2,0:T(8,128)(2,1)S(1)}, u32[]{:S(2)}, u32[]{:S(2)}) collective-permute-start(bf16[2,256,256]{1,2,0:T(8,128)(2,1)S(1)} %collective-permute-done.4), channel_id=1, source_target_pairs={{0,1},{1,2},{2,3},{3,4},{4,5},{5,6},{6,7},{7,0},{8,9},{9,10},{10,1... | collective-permute-start | bytes 786440 | tf_op jit(solution)/shard_map/ppermute | solution.py:26
  19.7 7.9 %collective-permute-start.2 = (bf16[2,256,256]{1,2,0:T(8,128)(2,1)S(1)}, bf16[2,256,256]{1,2,0:T(8,128)(2,1)S(1)}, u32[]{:S(2)}, u32[]{:S(2)}) collective-permute-start(bf16[2,256,256]{1,2,0:T(8,128)(2,1)S(1)} %collective-permute-done.1), channel_id=1, source_target_pairs={{0,7},{1,0},{2,1},{3,2},{4,3},{5,4},{6,5},{7,6},{8,15},{9,8},{10,9... | collective-permute-start | bytes 786440 | tf_op jit(solution)/shard_map/ppermute | solution.py:26
  27.6 7.6 %collective-permute-start.6 = (bf16[2,256,256]{1,2,0:T(8,128)(2,1)S(1)}, bf16[2,256,256]{1,2,0:T(8,128)(2,1)S(1)}, u32[]{:S(2)}, u32[]{:S(2)}) collective-permute-start(bf16[2,256,256]{1,2,0:T(8,128)(2,1)S(1)} %collective-permute-done.5), channel_id=1, source_target_pairs={{0,1},{1,2},{2,3},{3,4},{4,5},{5,6},{6,7},{7,0},{8,9},{9,10},{10,1... | collective-permute-start | bytes 786440 | tf_op jit(solution)/shard_map/ppermute | solution.py:26
  27.6 7.5 %collective-permute-start.3 = (bf16[2,256,256]{1,2,0:T(8,128)(2,1)S(1)}, bf16[2,256,256]{1,2,0:T(8,128)(2,1)S(1)}, u32[]{:S(2)}, u32[]{:S(2)}) collective-permute-start(bf16[2,256,256]{1,2,0:T(8,128)(2,1)S(1)} %collective-permute-done.2), channel_id=1, source_target_pairs={{0,7},{1,0},{2,1},{3,2},{4,3},{5,4},{6,5},{7,6},{8,15},{9,8},{10,9... | collective-permute-start | bytes 786440 | tf_op jit(solution)/shard_map/ppermute | solution.py:26
  35.2 7.6 %collective-permute-start.7 = (bf16[2,256,256]{1,2,0:T(8,128)(2,1)S(1)}, bf16[2,256,256]{1,2,0:T(8,128)(2,1)S(1)}, u32[]{:S(2)}, u32[]{:S(2)}) collective-permute-start(bf16[2,256,256]{1,2,0:T(8,128)(2,1)S(1)} %collective-permute-done.6), channel_id=1, source_target_pairs={{0,1},{1,2},{2,3},{3,4},{4,5},{5,6},{6,7},{7,0},{8,9},{9,10},{10,1... | collective-permute-start | bytes 786440 | tf_op jit(solution)/shard_map/ppermute | solution.py:26
  43.7 2.4 %slice-start = ((s8[6291456]{0:T(1024)(128)(4,1)}), s8[4194304]{0:T(1024)(128)(4,1)S(1)}, s32[]{:S(2)}) async-start(s8[6291456]{0:T(1024)(128)(4,1)} %bitcast.73), calls=%async_computation.2 | async-start | bytes 8388608
  44.1 1.0 copy-start.2
  44.2 2.5 %slice-start.1 = ((s8[6291456]{0:T(1024)(128)(4,1)}), s8[2097152]{0:T(1024)(128)(4,1)S(1)}, s32[]{:S(2)}) async-start(s8[6291456]{0:T(1024)(128)(4,1)} %bitcast.73), calls=%async_computation.3 | async-start | bytes 4194304
  46.7 3.8 %copy-start.1 = (f32[16,256]{1,0:T(8,128)S(1)}, f32[16,256]{1,0:T(8,128)}, u32[]{:S(2)}) copy-start(f32[16,256]{1,0:T(8,128)} %param.14) | copy-start | bytes 49156
  48.5 4.9 %collective-permute-start.8 = (bf16[2,3,256]{2,0,1:T(2,128)(2,1)S(1)}, bf16[2,3,256]{2,0,1:T(2,128)(2,1)S(1)}, u32[]{:S(2)}, u32[]{:S(2)}) collective-permute-start(bf16[2,3,256]{2,0,1:T(2,128)(2,1)S(1)} %slice.40), channel_id=1, source_target_pairs={{0,16},{16,32},{32,48},{48,64},{64,80},{80,96},{96,112},{112,128},... | collective-permute-start | bytes 9224 | tf_op jit(solution)/shard_map/ppermute | solution.py:12
  53.8 8.8 %copy-start.4 = (f32[16,256]{1,0:T(8,128)S(1)}, f32[16,256]{1,0:T(8,128)}, u32[]{:S(2)}) copy-start(f32[16,256]{1,0:T(8,128)} %param.15) | copy-start | bytes 49156
  56.0 11.3 %all-to-all-start = ((f32[16,16,256]{2,1,0:T(8,128)}), f32[16,16,256]{2,1,0:T(8,128)S(1)}, u32[]{:S(2)}, u32[]{:S(2)}) async-start(f32[16,16,256]{2,1,0:T(8,128)} %tile.2), calls=%async_computation | async-start | bytes 524288 | tf_op jit(solution)/shard_map/all_to_all | solution.py:98
  62.5 5.8 %copy-start.3 = (f32[256]{0:T(256)S(1)}, f32[256]{0:T(256)}, u32[]{:S(2)}) copy-start(f32[256]{0:T(256)} %param.16) | copy-start | bytes 3076

commit v5 on v4

--- a/solution.py
+++ b/solution.py
@@ -39,6 +39,45 @@
     by_place = jnp.roll(by_offset, where_in_ring, axis=0)
     rows = block.shape[0]
     return by_place.transpose(2, 1, 0, 3).reshape(rows, chan_devices * block.shape[1])
+
+
+def reduce_chan(partial, chan_devices, width):
+    ring = chan_devices // 2
+    upper = lax.axis_index("chan") >= ring
+    where_in_ring = lax.axis_index("chan") % ring
+    rows = partial.shape[0]
+    slabs = partial.reshape(rows, 2, ring, width)
+
+    def along_ring(value, by):
+        pairs = [
+            (side * ring + z, side * ring + (z + by) % ring)
+            for side in range(2)
+            for z in range(ring)
+        ]
+        return lax.ppermute(value, "chan", pairs)
+
+    def slab(offset):
+        return lax.dynamic_index_in_dim(slabs, (where_in_ring + offset) % ring, 2, False)
+
+    forward_steps = ring // 2
+    backward_steps = ring - 1 - forward_steps
+    fwd = slab(forward_steps)
+    for step in range(1, forward_steps + 1):
+        fwd = along_ring(fwd.astype(jnp.bfloat16), 1).astype(jnp.float32)
+        if step < forward_steps:
+            fwd = fwd + slab(forward_steps - step)
+    total = slab(0) + fwd
+    if backward_steps > 0:
+        bwd = slab(-backward_steps)
+        for step in range(1, backward_steps + 1):
+            bwd = along_ring(bwd.astype(jnp.bfloat16), -1).astype(jnp.float32)
+            if step < backward_steps:
+                bwd = bwd + slab(step - backward_steps)
+        total = total + bwd
+    mine = jnp.where(upper, total[:, 1], total[:, 0])
+    theirs = jnp.where(upper, total[:, 0], total[:, 1])
+    partners = [(i, (i + ring) % chan_devices) for i in range(chan_devices)]
+    return mine + lax.ppermute(theirs, "chan", partners)
 
 
 def on_device(
@@ -108,11 +147,8 @@
     carried = jnp.sum(fall * incoming[None], axis=1)
     long_out = local + carried + skip_gain[None, :] * driven
     hidden = (query * long_out).astype(jnp.bfloat16)
-    partial = jnp.dot(hidden, out_weight, preferred_element_type=jnp.float32).astype(jnp.bfloat16)
-    parts = lax.all_to_all(partial, "chan", 1, 0, tiled=True)
-    mixed = jnp.sum(
-        parts.reshape(chan_devices, token_rows, channels).astype(jnp.float32), axis=0
-    )
+    partial = jnp.dot(hidden, out_weight, preferred_element_type=jnp.float32)
+    mixed = reduce_chan(partial, chan_devices, channels)
     return (stream.astype(jnp.float32) + mixed).astype(jnp.bfloat16)
 
 

time: 131 us -> 123 us (0.939)
  blocking collectives: 59.2 us -> 0 us
  waiting for transfers between devices: 29.1 us -> 49.3 us
  starting transfers between devices: 23.5 us -> 38 us
  local copies, waits for them, and re-layouts: 4.45 us -> 17.9 us
  other arithmetic: 5.81 us -> 10.4 us
    all_to_all x1 -> x0, blocking collectives: 59.2 us -> none  [on_device(): parts = lax.all_to_all(partial, 'chan', 1, 0, tiled=True)]
    ppermute x7 -> x14, waiting for transfers between devices: 20.9 us -> 38.9 us  [along_ring(): return lax.ppermute(value, 'chan', pairs)]
    ppermute x7 -> x14, starting transfers between devices: 12.6 us -> 23.3 us  [along_ring(): return lax.ppermute(value, 'chan', pairs)]
    unnamed x28 -> x32, local copies, waits for them, and re-layouts: 1.38 us -> 6.89 us
    ppermute x0 -> x1, waiting for transfers between devices: none -> 5.17 us  [reduce_chan(): return mine + lax.ppermute(theirs, 'chan', partners)]
    dynamic_slice x0 -> x8, local copies, waits for them, and re-layouts: none -> 4.96 us  [slab(): lax.dynamic_index_in_dim(slabs, (where_in_ring + offset) % ring, 2, False)]
    convert_element_type x0 -> x5, other arithmetic: none -> 4.69 us  [the longest x3 2.93 us: reduce_chan(): fwd = along_ring(fwd.astype(jnp.bfloat16), 1).astype(jnp.float32)]
    dot_general x0 -> x1, local copies, waits for them, and re-layouts: none -> 3.28 us  [on_device(): partial = jnp.dot(hidden, out_weight, preferred_element_type=jnp.float32)]
  transfers between devices with their start and end apart: 10 -> 18, of which waited for: 7 -> 14; matrix products, arithmetic and copies ran while one was open for 4% -> 15% of each run, Pallas kernels for 0% -> 0%
where the time goes in v5:
time: 123 us
  waiting for transfers between devices  49.3 us (40%)
  starting transfers between devices  38 us (31%)
  local copies, waits for them, and re-layouts  17.9 us (15%)
  other arithmetic  10.4 us (8%)
  matrix products  6.89 us (6%)
    ppermute x14, waiting for transfers between devices, along_ring(): return lax.ppermute(value, 'chan', pairs)  38.9 us
    ppermute x14, starting transfers between devices, along_ring(): return lax.ppermute(value, 'chan', pairs)  23.3 us
    unnamed x32, local copies, waits for them, and re-layouts  6.89 us
    all_to_all x1, starting transfers between devices, on_device(): lax.all_to_all(jnp.tile(device_end, (seq_devices, 1)), 'seq', 0, 0, tiled...  6.85 us
    ppermute x1, waiting for transfers between devices, reduce_chan(): return mine + lax.ppermute(theirs, 'chan', partners)  5.17 us
    dynamic_slice x8, local copies, waits for them, and re-layouts, slab(): lax.dynamic_index_in_dim(slabs, (where_in_ring + offset) % ring, 2, False)  4.96 us
    ppermute x1, waiting for transfers between devices, gather_chan(): lax.ppermute(block, 'chan', [(i, (i + ring) % chan_devices) for i in rang...  3.72 us
    dot_general x1, local copies, waits for them, and re-layouts, on_device(): partial = jnp.dot(hidden, out_weight, preferred_element_type=jnp.float32)  3.28 us
  transfers between devices with their start and end apart: 18, of which 14 were waited for; matrix products, arithmetic and copies ran while one was open for 15% of the time, Pallas kernels for 0%

profile of v5, /device:TPU:8, one launch (start us, length us, event | category | flops | bytes accessed | tf_op | source)
XLA Modules:
  0.0 123.0 jit_solution(13730735913253493608)
XLA Ops:
  0.0 0.9 copy-done
  1.0 1.0 convolution_convert_fusion
  2.0 3.1 %collective-permute-start = (bf16[256,256]{0,1:T(8,128)(2,1)S(1)}, bf16[256,256]{0,1:T(8,128)(2,1)S(1)}, u32[]{:S(2)}, u32[]{:S(2)}) collective-permute-start(bf16[256,256]{0,1:T(8,128)(2,1)S(1)} %convolution_convert_fusion), channel_id=1, source_target_pairs={{0,8},{1,9},{2,10},{3,11},{4,12},{5,13},{6,14},{7,15},{8,0},{9,1},... | collective-permute-start | bytes 393224 | tf_op jit(solution)/shard_map/ppermute | solution.py:28
  5.1 3.7 %collective-permute-done = bf16[256,256]{0,1:T(8,128)(2,1)S(1)} collective-permute-done((bf16[256,256]{0,1:T(8,128)(2,1)S(1)}, bf16[256,256]{0,1:T(8,128)(2,1)S(1)}, u32[]{:S(2)}, u32[]{:S(2)}) %collective-permute-start) | collective-permute-done | bytes 131104 | tf_op jit(solution)/shard_map/ppermute | solution.py:28
  8.9 2.0 %collective-permute-start.4 = (bf16[2,256,256]{1,2,0:T(8,128)(2,1)S(1)}, bf16[2,256,256]{1,2,0:T(8,128)(2,1)S(1)}, u32[]{:S(2)}, u32[]{:S(2)}) collective-permute-start(bf16[2,256,256]{1,2,0:T(8,128)(2,1)S(1)} %maximum_select_fusion.1), channel_id=1, source_target_pairs={{0,1},{1,2},{2,3},{3,4},{4,5},{5,6},{6,7},{7,0},{8,9},{9,10},{10,1... | collective-permute-start | bytes 786440 | tf_op jit(solution)/shard_map/ppermute | solution.py:26
  10.8 4.0 %collective-permute-start.1 = (bf16[2,256,256]{1,2,0:T(8,128)(2,1)S(1)}, bf16[2,256,256]{1,2,0:T(8,128)(2,1)S(1)}, u32[]{:S(2)}, u32[]{:S(2)}) collective-permute-start(bf16[2,256,256]{1,2,0:T(8,128)(2,1)S(1)} %maximum_select_fusion.1), channel_id=1, source_target_pairs={{0,7},{1,0},{2,1},{3,2},{4,3},{5,4},{6,5},{7,6},{8,15},{9,8},{10,9... | collective-permute-start | bytes 786440 | tf_op jit(solution)/shard_map/ppermute | solution.py:26
  14.9 5.4 %collective-permute-done.4 = bf16[2,256,256]{1,2,0:T(8,128)(2,1)S(1)} collective-permute-done((bf16[2,256,256]{1,2,0:T(8,128)(2,1)S(1)}, bf16[2,256,256]{1,2,0:T(8,128)(2,1)S(1)}, u32[]{:S(2)}, u32[]{:S(2)}) %collective-permute-start.4) | collective-permute-done | bytes 262176 | tf_op jit(solution)/shard_map/ppermute | solution.py:26
  20.2 3.2 %collective-permute-start.2 = (bf16[2,256,256]{1,2,0:T(8,128)(2,1)S(1)}, bf16[2,256,256]{1,2,0:T(8,128)(2,1)S(1)}, u32[]{:S(2)}, u32[]{:S(2)}) collective-permute-start(bf16[2,256,256]{1,2,0:T(8,128)(2,1)S(1)} %collective-permute-done.1), channel_id=1, source_target_pairs={{0,7},{1,0},{2,1},{3,2},{4,3},{5,4},{6,5},{7,6},{8,15},{9,8},{10,9... | collective-permute-start | bytes 786440 | tf_op jit(solution)/shard_map/ppermute | solution.py:26
  23.5 0.7 slice_bitcast_fusion.2
  24.2 3.9 %collective-permute-done.5 = bf16[2,256,256]{1,2,0:T(8,128)(2,1)S(1)} collective-permute-done((bf16[2,256,256]{1,2,0:T(8,128)(2,1)S(1)}, bf16[2,256,256]{1,2,0:T(8,128)(2,1)S(1)}, u32[]{:S(2)}, u32[]{:S(2)}) %collective-permute-start.5) | collective-permute-done | bytes 262176 | tf_op jit(solution)/shard_map/ppermute | solution.py:26
  28.1 3.3 %collective-permute-start.3 = (bf16[2,256,256]{1,2,0:T(8,128)(2,1)S(1)}, bf16[2,256,256]{1,2,0:T(8,128)(2,1)S(1)}, u32[]{:S(2)}, u32[]{:S(2)}) collective-permute-start(bf16[2,256,256]{1,2,0:T(8,128)(2,1)S(1)} %collective-permute-done.2), channel_id=1, source_target_pairs={{0,7},{1,0},{2,1},{3,2},{4,3},{5,4},{6,5},{7,6},{8,15},{9,8},{10,9... | collective-permute-start | bytes 786440 | tf_op jit(solution)/shard_map/ppermute | solution.py:26
  31.5 4.2 %collective-permute-done.6 = bf16[2,256,256]{1,2,0:T(8,128)(2,1)S(1)} collective-permute-done((bf16[2,256,256]{1,2,0:T(8,128)(2,1)S(1)}, bf16[2,256,256]{1,2,0:T(8,128)(2,1)S(1)}, u32[]{:S(2)}, u32[]{:S(2)}) %collective-permute-start.6) | collective-permute-done | bytes 262176 | tf_op jit(solution)/shard_map/ppermute | solution.py:26
  35.7 7.5 %collective-permute-done.7 = bf16[2,256,256]{1,2,0:T(8,128)(2,1)S(1)} collective-permute-done((bf16[2,256,256]{1,2,0:T(8,128)(2,1)S(1)}, bf16[2,256,256]{1,2,0:T(8,128)(2,1)S(1)}, u32[]{:S(2)}, u32[]{:S(2)}) %collective-permute-start.7) | collective-permute-done | bytes 262176 | tf_op jit(solution)/shard_map/ppermute | solution.py:26
  43.6 0.6 fusion
  44.2 0.5 convert_bitcast_fusion
  44.7 0.4 copy.34
  45.1 0.5 copy-done.3
  45.6 1.0 fusion.2
  46.6 0.6 slice-done.1
  47.2 1.8 %fusion.5 = bf16[256,3,256]{2,0,1:T(8,128)(2,1)S(1)} fusion(bf16[4096,3,256]{2,0,1:T(8,128)(2,1)S(1)} %bitcast.117, bf16[256,4096]{0,1:T(8,128)(2,1)S(1)} %fusion.2), kind=kOutput, calls=%fused_computation.13 | convolution fusion | flops 1610809344 | bytes 8781824 | tf_op jit(solution)/shard_map/td,djc->tjc/dot_general | solution.py:109
  49.0 1.9 %collective-permute-start.8 = (bf16[2,3,256]{2,0,1:T(2,128)(2,1)S(1)}, bf16[2,3,256]{2,0,1:T(2,128)(2,1)S(1)}, u32[]{:S(2)}, u32[]{:S(2)}) collective-permute-start(bf16[2,3,256]{2,0,1:T(2,128)(2,1)S(1)} %slice.50), channel_id=1, source_target_pairs={{0,16},{16,32},{32,48},{48,64},{64,80},{80,96},{96,112},{112,128},... | collective-permute-start | bytes 9224 | tf_op jit(solution)/shard_map/ppermute | solution.py:12
  51.0 3.3 %copy.50 = bf16[4096,256]{1,0:T(8,128)(2,1)S(1)} copy(bf16[4096,256]{0,1:T(8,128)(2,1)} %bitcast.120) | data formatting | bytes 4194304 | tf_op jit(solution)/shard_map/dot_general | solution.py:150
  54.4 0.1 maximum_convert_fusion
  54.4 0.3 fusion.9
  54.8 0.1 copy.36
  54.9 1.3 %multiply_reduce_fusion.1 = f32[16,256]{1,0:T(8,128)S(1)} fusion(f32[16,256]{1,0:T(8,128)S(1)} %copy-done.2, f32[256,256]{0,1:T(8,128)S(1)} %copy.36), kind=kLoop, calls=%fused_computation.8 | loop fusion | flops 3141632 | bytes 294912 | tf_op jit(solution)/shard_map/reduce_sum | solution.py:136
  56.2 0.7 tile.2
  57.0 6.9 %all-to-all-start = ((f32[16,16,256]{2,1,0:T(8,128)}), f32[16,16,256]{2,1,0:T(8,128)S(1)}, u32[]{:S(2)}, u32[]{:S(2)}) async-start(f32[16,16,256]{2,1,0:T(8,128)} %tile.2), calls=%async_computation | async-start | bytes 524288 | tf_op jit(solution)/shard_map/all_to_all | solution.py:137
  63.8 0.6 bitcast_multiply_fusion
  64.5 3.2 %multiply_reduce_fusion.2 = f32[256,256]{1,0:T(8,128)S(1)} fusion(f32[16,256,256]{2,1,0:T(8,128)S(1)} %bitcast.119, f32[16,256]{1,0:T(8,128)S(1)} %get-tuple-element.14, f32[16,256]{1,0:T(8,128)S(1)} %copy-done.5), kind=kOutput, calls=%fused_computation.9 | convolution fusion | flops 3225419776 | bytes 4489216 | tf_op jit(solution)/shard_map/dot_general | solution.py:132
  67.7 1.5 %all-to-all-done = f32[16,16,256]{2,1,0:T(8,128)S(1)} async-done(((f32[16,16,256]{2,1,0:T(8,128)}), f32[16,16,256]{2,1,0:T(8,128)S(1)}, u32[]{:S(2)}, u32[]{:S(2)}) %all-to-all-start) | async-done | bytes 262176 | tf_op jit(solution)/shard_map/all_to_all | solution.py:137
  69.2 0.1 multiply_reduce_fusion.3
  69.4 0.9 multiply_reduce_fusion
  70.3 0.8 fusion.26
  71.0 1.9 %copy-done.1 = f32[256,2,8,256]{3,0,2,1:T(8,128)} copy-done((f32[256,2,8,256]{3,0,2,1:T(8,128)}, f32[256,2,8,256]{3,0,2,1:T(8,128)S(1)}, u32[]{:S(2)}) %copy-start.1) | copy-done | bytes 4194328
  73.0 0.8 constant_dynamic-slice_fusion.6
  73.7 0.8 copy.51
  74.6 2.2 %constant_dynamic-slice_fusion.5 = (f32[256,2,1,256]{3,0,2,1:T(8,128)S(1)}, f32[256,2,1,256]{3,0,2,1:T(8,128)S(1)}, f32[256,2,1,256]{3,0,2,1:T(8,128)S(1)}, f32[...) fusion(f32[256,2,8,256]{3,0,2,1:T(8,128)} %copy-done.1, ...), kind=kLoop, calls=%fused_computation.84 | loop fusion | bytes 6291480 | tf_op jit(solution)/shard_map/jit(dynamic_index_in_dim)/dynamic_slice | solution.py:60
  76.8 1.0 copy.40
  77.8 1.8 %copy.52 = bf16[256,2,1,256]{0,3,1,2:T(8,128)(2,1)} copy(bf16[256,2,1,256]{3,0,2,1:T(8,128)(2,1)} %get-tuple-element.6) | data formatting | bytes 524288
  79.6 3.2 %collective-permute-start.13 = (bf16[256,2,256]{0,2,1:T(8,128)(2,1)}, bf16[256,2,256]{0,2,1:T(8,128)(2,1)}, u32[]{:S(2)}, u32[]{:S(2)}) collective-permute-start(bf16[256,2,256]{0,2,1:T(8,128)(2,1)} %bitcast.110), channel_id=1, source_target_pairs={{0,7},{1,0},{2,1},{3,2},{4,3},{5,4},{6,5},{7,6},{8,15},{9,8},{10,9... | collective-permute-start | bytes 786440 | tf_op jit(solution)/shard_map/ppermute | solution.py:57
  82.8 2.3 %collective-permute-done.9 = bf16[256,2,256]{0,2,1:T(8,128)(2,1)} collective-permute-done((bf16[256,2,256]{0,2,1:T(8,128)(2,1)}, bf16[256,2,256]{0,2,1:T(8,128)(2,1)}, u32[]{:S(2)}, u32[]{:S(2)}) %collective-permute-start.9) | collective-permute-done | bytes 262176 | tf_op jit(solution)/shard_map/ppermute | solution.py:57
  85.1 1.9 %fusion.15 = bf16[256,2,256]{0,2,1:T(8,128)(2,1)} fusion(f32[256,2,1,256]{0,3,1,2:T(8,128)} %copy.40, bf16[256,2,256]{0,2,1:T(8,128)(2,1)} %collective-permute-done.9), kind=kLoop, calls=%fused_computation.30 | loop fusion | flops 393216 | bytes 1048576 | tf_op jit(solution)/shard_map/convert_element_type | solution.py:66
  87.0 0.2 copy.44
  87.2 0.2 copy.41
  87.4 2.0 %collective-permute-done.13 = bf16[256,2,256]{0,2,1:T(8,128)(2,1)} collective-permute-done((bf16[256,2,256]{0,2,1:T(8,128)(2,1)}, bf16[256,2,256]{0,2,1:T(8,128)(2,1)}, u32[]{:S(2)}, u32[]{:S(2)}) %collective-permute-start.13) | collective-permute-done | bytes 262176 | tf_op jit(solution)/shard_map/ppermute | solution.py:57
  89.4 1.7 %fusion.12 = bf16[256,2,256]{0,2,1:T(8,128)(2,1)} fusion(f32[256,2,1,256]{0,3,1,2:T(8,128)S(1)} %copy.44, bf16[256,2,256]{0,2,1:T(8,128)(2,1)} %collective-permute-done.13), kind=kLoop, calls=%fused_computation.24 | loop fusion | flops 393216 | bytes 1048576 | tf_op jit(solution)/shard_map/convert_element_type | solution.py:73
  91.1 3.7 %collective-permute-start.14 = (bf16[256,2,256]{0,2,1:T(8,128)(2,1)}, bf16[256,2,256]{0,2,1:T(8,128)(2,1)S(1)}, u32[]{:S(2)}, u32[]{:S(2)}) collective-permute-start(bf16[256,2,256]{0,2,1:T(8,128)(2,1)} %fusion.12), channel_id=1, source_target_pairs={{0,7},{1,0},{2,1},{3,2},{4,3},{5,4},{6,5},{7,6},{8,15},{9,8},{10,9... | collective-permute-start | bytes 786440 | tf_op jit(solution)/shard_map/ppermute | solution.py:57
  94.8 1.9 %collective-permute-done.10 = bf16[256,2,256]{0,2,1:T(8,128)(2,1)} collective-permute-done((bf16[256,2,256]{0,2,1:T(8,128)(2,1)}, bf16[256,2,256]{0,2,1:T(8,128)(2,1)}, u32[]{:S(2)}, u32[]{:S(2)}) %collective-permute-start.10) | collective-permute-done | bytes 262176 | tf_op jit(solution)/shard_map/ppermute | solution.py:57
  96.7 1.0 fusion.14
  97.7 0.1 collective-permute-start.11
  97.8 0.2 copy.45
  98.0 0.2 copy.42
  98.2 2.3 %collective-permute-done.14 = bf16[256,2,256]{0,2,1:T(8,128)(2,1)S(1)} collective-permute-done((bf16[256,2,256]{0,2,1:T(8,128)(2,1)}, bf16[256,2,256]{0,2,1:T(8,128)(2,1)S(1)}, u32[]{:S(2)}, u32[]{:S(2)}) %collective-permute-start.14) | collective-permute-done | bytes 262176 | tf_op jit(solution)/shard_map/ppermute | solution.py:57
  100.6 3.7 %collective-permute-start.15 = (bf16[256,2,256]{0,2,1:T(8,128)(2,1)S(1)}, bf16[256,2,256]{0,2,1:T(8,128)(2,1)S(1)}, u32[]{:S(2)}, u32[]{:S(2)}) collective-permute-start(bf16[256,2,256]{0,2,1:T(8,128)(2,1)S(1)} %fusion.11), channel_id=1, source_target_pairs={{0,7},{1,0},{2,1},{3,2},{4,3},{5,4},{6,5},{7,6},{8,15},{9,8},{10,9... | collective-permute-start | bytes 786440 | tf_op jit(solution)/shard_map/ppermute | solution.py:57
  104.3 2.1 %collective-permute-done.11 = bf16[256,2,256]{0,2,1:T(8,128)(2,1)S(1)} collective-permute-done((bf16[256,2,256]{0,2,1:T(8,128)(2,1)S(1)}, bf16[256,2,256]{0,2,1:T(8,128)(2,1)S(1)}, u32[]{:S(2)}, u32[]{:S(2)}) %collective-permute-start.11) | collective-permute-done | bytes 262176 | tf_op jit(solution)/shard_map/ppermute | solution.py:57
  106.4 0.1 collective-permute-start.12
  106.5 0.2 copy.38
  106.7 2.1 %collective-permute-done.15 = bf16[256,2,256]{0,2,1:T(8,128)(2,1)S(1)} collective-permute-done((bf16[256,2,256]{0,2,1:T(8,128)(2,1)S(1)}, bf16[256,2,256]{0,2,1:T(8,128)(2,1)S(1)}, u32[]{:S(2)}, u32[]{:S(2)}) %collective-permute-start.15) | collective-permute-done | bytes 262176 | tf_op jit(solution)/shard_map/ppermute | solution.py:57
  108.8 5.3 %collective-permute-done.12 = bf16[256,2,256]{0,2,1:T(8,128)(2,1)S(1)} collective-permute-done((bf16[256,2,256]{0,2,1:T(8,128)(2,1)S(1)}, bf16[256,2,256]{0,2,1:T(8,128)(2,1)S(1)}, u32[]{:S(2)}, u32[]{:S(2)}) %collective-permute-start.12) | collective-permute-done | bytes 262176 | tf_op jit(solution)/shard_map/ppermute | solution.py:57
  114.1 0.1 fusion.16
  114.2 2.8 %collective-permute-start.16 = (f32[256,256]{0,1:T(8,128)S(1)}, f32[256,256]{0,1:T(8,128)S(1)}, u32[]{:S(2)}, u32[]{:S(2)}) collective-permute-start(f32[256,256]{0,1:T(8,128)S(1)} %select_bitcast_fusion), channel_id=1, source_target_pairs={{0,8},{1,9},{2,10},{3,11},{4,12},{5,13},{6,14},{7,15},{8,0},{9,1},... | collective-permute-start | bytes 786440 | tf_op jit(solution)/shard_map/ppermute | solution.py:80
  117.0 5.2 %collective-permute-done.16 = f32[256,256]{0,1:T(8,128)S(1)} collective-permute-done((f32[256,256]{0,1:T(8,128)S(1)}, f32[256,256]{0,1:T(8,128)S(1)}, u32[]{:S(2)}, u32[]{:S(2)}) %collective-permute-start.16) | collective-permute-done | bytes 262176 | tf_op jit(solution)/shard_map/ppermute | solution.py:80
  122.3 0.8 copy.46
  (51 shorter events, 0.8 us)
Async XLA Ops:
  0.0 1.0 copy-start
  2.0 6.8 %collective-permute-start = (bf16[256,256]{0,1:T(8,128)(2,1)S(1)}, bf16[256,256]{0,1:T(8,128)(2,1)S(1)}, u32[]{:S(2)}, u32[]{:S(2)}) collective-permute-start(bf16[256,256]{0,1:T(8,128)(2,1)S(1)} %convolution_convert_fusion), channel_id=1, source_target_pairs={{0,8},{1,9},{2,10},{3,11},{4,12},{5,13},{6,14},{7,15},{8,0},{9,1},... | collective-permute-start | bytes 393224 | tf_op jit(solution)/shard_map/ppermute | solution.py:28
  8.9 11.4 %collective-permute-start.4 = (bf16[2,256,256]{1,2,0:T(8,128)(2,1)S(1)}, bf16[2,256,256]{1,2,0:T(8,128)(2,1)S(1)}, u32[]{:S(2)}, u32[]{:S(2)}) collective-permute-start(bf16[2,256,256]{1,2,0:T(8,128)(2,1)S(1)} %maximum_select_fusion.1), channel_id=1, source_target_pairs={{0,1},{1,2},{2,3},{3,4},{4,5},{5,6},{6,7},{7,0},{8,9},{9,10},{10,1... | collective-permute-start | bytes 786440 | tf_op jit(solution)/shard_map/ppermute | solution.py:26
  10.8 9.4 %collective-permute-start.1 = (bf16[2,256,256]{1,2,0:T(8,128)(2,1)S(1)}, bf16[2,256,256]{1,2,0:T(8,128)(2,1)S(1)}, u32[]{:S(2)}, u32[]{:S(2)}) collective-permute-start(bf16[2,256,256]{1,2,0:T(8,128)(2,1)S(1)} %maximum_select_fusion.1), channel_id=1, source_target_pairs={{0,7},{1,0},{2,1},{3,2},{4,3},{5,4},{6,5},{7,6},{8,15},{9,8},{10,9... | collective-permute-start | bytes 786440 | tf_op jit(solution)/shard_map/ppermute | solution.py:26
  20.2 7.8 %collective-permute-start.5 = (bf16[2,256,256]{1,2,0:T(8,128)(2,1)S(1)}, bf16[2,256,256]{1,2,0:T(8,128)(2,1)S(1)}, u32[]{:S(2)}, u32[]{:S(2)}) collective-permute-start(bf16[2,256,256]{1,2,0:T(8,128)(2,1)S(1)} %collective-permute-done.4), channel_id=1, source_target_pairs={{0,1},{1,2},{2,3},{3,4},{4,5},{5,6},{6,7},{7,0},{8,9},{9,10},{10,1... | collective-permute-start | bytes 786440 | tf_op jit(solution)/shard_map/ppermute | solution.py:26
  20.2 7.9 %collective-permute-start.2 = (bf16[2,256,256]{1,2,0:T(8,128)(2,1)S(1)}, bf16[2,256,256]{1,2,0:T(8,128)(2,1)S(1)}, u32[]{:S(2)}, u32[]{:S(2)}) collective-permute-start(bf16[2,256,256]{1,2,0:T(8,128)(2,1)S(1)} %collective-permute-done.1), channel_id=1, source_target_pairs={{0,7},{1,0},{2,1},{3,2},{4,3},{5,4},{6,5},{7,6},{8,15},{9,8},{10,9... | collective-permute-start | bytes 786440 | tf_op jit(solution)/shard_map/ppermute | solution.py:26
  28.1 7.6 %collective-permute-start.6 = (bf16[2,256,256]{1,2,0:T(8,128)(2,1)S(1)}, bf16[2,256,256]{1,2,0:T(8,128)(2,1)S(1)}, u32[]{:S(2)}, u32[]{:S(2)}) collective-permute-start(bf16[2,256,256]{1,2,0:T(8,128)(2,1)S(1)} %collective-permute-done.5), channel_id=1, source_target_pairs={{0,1},{1,2},{2,3},{3,4},{4,5},{5,6},{6,7},{7,0},{8,9},{9,10},{10,1... | collective-permute-start | bytes 786440 | tf_op jit(solution)/shard_map/ppermute | solution.py:26
  28.1 7.5 %collective-permute-start.3 = (bf16[2,256,256]{1,2,0:T(8,128)(2,1)S(1)}, bf16[2,256,256]{1,2,0:T(8,128)(2,1)S(1)}, u32[]{:S(2)}, u32[]{:S(2)}) collective-permute-start(bf16[2,256,256]{1,2,0:T(8,128)(2,1)S(1)} %collective-permute-done.2), channel_id=1, source_target_pairs={{0,7},{1,0},{2,1},{3,2},{4,3},{5,4},{6,5},{7,6},{8,15},{9,8},{10,9... | collective-permute-start | bytes 786440 | tf_op jit(solution)/shard_map/ppermute | solution.py:26
  35.6 7.6 %collective-permute-start.7 = (bf16[2,256,256]{1,2,0:T(8,128)(2,1)S(1)}, bf16[2,256,256]{1,2,0:T(8,128)(2,1)S(1)}, u32[]{:S(2)}, u32[]{:S(2)}) collective-permute-start(bf16[2,256,256]{1,2,0:T(8,128)(2,1)S(1)} %collective-permute-done.6), channel_id=1, source_target_pairs={{0,1},{1,2},{2,3},{3,4},{4,5},{5,6},{6,7},{7,0},{8,9},{9,10},{10,1... | collective-permute-start | bytes 786440 | tf_op jit(solution)/shard_map/ppermute | solution.py:26
  44.2 2.4 %slice-start = ((s8[6291456]{0:T(1024)(128)(4,1)}), s8[4194304]{0:T(1024)(128)(4,1)S(1)}, s32[]{:S(2)}) async-start(s8[6291456]{0:T(1024)(128)(4,1)} %bitcast.116), calls=%async_computation.1 | async-start | bytes 8388608
  44.6 1.0 copy-start.3
  44.6 2.5 %slice-start.1 = ((s8[6291456]{0:T(1024)(128)(4,1)}), s8[2097152]{0:T(1024)(128)(4,1)S(1)}, s32[]{:S(2)}) async-start(s8[6291456]{0:T(1024)(128)(4,1)} %bitcast.116), calls=%async_computation.2 | async-start | bytes 4194304
  47.2 3.8 %copy-start.2 = (f32[16,256]{1,0:T(8,128)S(1)}, f32[16,256]{1,0:T(8,128)}, u32[]{:S(2)}) copy-start(f32[16,256]{1,0:T(8,128)} %param.14) | copy-start | bytes 49156
  49.0 5.3 %collective-permute-start.8 = (bf16[2,3,256]{2,0,1:T(2,128)(2,1)S(1)}, bf16[2,3,256]{2,0,1:T(2,128)(2,1)S(1)}, u32[]{:S(2)}, u32[]{:S(2)}) collective-permute-start(bf16[2,3,256]{2,0,1:T(2,128)(2,1)S(1)} %slice.50), channel_id=1, source_target_pairs={{0,16},{16,32},{32,48},{48,64},{64,80},{80,96},{96,112},{112,128},... | collective-permute-start | bytes 9224 | tf_op jit(solution)/shard_map/ppermute | solution.py:12
  54.7 9.8 %copy-start.5 = (f32[16,256]{1,0:T(8,128)S(1)}, f32[16,256]{1,0:T(8,128)}, u32[]{:S(2)}) copy-start(f32[16,256]{1,0:T(8,128)} %param.15) | copy-start | bytes 49156
  57.0 12.3 %all-to-all-start = ((f32[16,16,256]{2,1,0:T(8,128)}), f32[16,16,256]{2,1,0:T(8,128)S(1)}, u32[]{:S(2)}, u32[]{:S(2)}) async-start(f32[16,16,256]{2,1,0:T(8,128)} %tile.2), calls=%async_computation | async-start | bytes 524288 | tf_op jit(solution)/shard_map/all_to_all | solution.py:137
  64.5 5.8 %copy-start.4 = (f32[256]{0:T(256)S(1)}, f32[256]{0:T(256)}, u32[]{:S(2)}) copy-start(f32[256]{0:T(256)} %param.16) | copy-start | bytes 3076
  71.0 2.0 %copy-start.1 = (f32[256,2,8,256]{3,0,2,1:T(8,128)}, f32[256,2,8,256]{3,0,2,1:T(8,128)S(1)}, u32[]{:S(2)}) copy-start(f32[256,2,8,256]{3,0,2,1:T(8,128)S(1)} %fusion.26) | copy-start | bytes 12582916
  74.6 10.6 %collective-permute-start.9 = (bf16[256,2,256]{0,2,1:T(8,128)(2,1)}, bf16[256,2,256]{0,2,1:T(8,128)(2,1)}, u32[]{:S(2)}, u32[]{:S(2)}) collective-permute-start(bf16[256,2,256]{0,2,1:T(8,128)(2,1)} %bitcast.111), channel_id=1, source_target_pairs={{0,1},{1,2},{2,3},{3,4},{4,5},{5,6},{6,7},{7,0},{8,9},{9,10},{10,1... | collective-permute-start | bytes 786440 | tf_op jit(solution)/shard_map/ppermute | solution.py:57
  79.6 9.8 %collective-permute-start.13 = (bf16[256,2,256]{0,2,1:T(8,128)(2,1)}, bf16[256,2,256]{0,2,1:T(8,128)(2,1)}, u32[]{:S(2)}, u32[]{:S(2)}) collective-permute-start(bf16[256,2,256]{0,2,1:T(8,128)(2,1)} %bitcast.110), channel_id=1, source_target_pairs={{0,7},{1,0},{2,1},{3,2},{4,3},{5,4},{6,5},{7,6},{8,15},{9,8},{10,9... | collective-permute-start | bytes 786440 | tf_op jit(solution)/shard_map/ppermute | solution.py:57
  87.0 9.7 %collective-permute-start.10 = (bf16[256,2,256]{0,2,1:T(8,128)(2,1)}, bf16[256,2,256]{0,2,1:T(8,128)(2,1)}, u32[]{:S(2)}, u32[]{:S(2)}) collective-permute-start(bf16[256,2,256]{0,2,1:T(8,128)(2,1)} %fusion.15), channel_id=1, source_target_pairs={{0,1},{1,2},{2,3},{3,4},{4,5},{5,6},{6,7},{7,0},{8,9},{9,10},{10,1... | collective-permute-start | bytes 786440 | tf_op jit(solution)/shard_map/ppermute | solution.py:57
  91.1 9.4 %collective-permute-start.14 = (bf16[256,2,256]{0,2,1:T(8,128)(2,1)}, bf16[256,2,256]{0,2,1:T(8,128)(2,1)S(1)}, u32[]{:S(2)}, u32[]{:S(2)}) collective-permute-start(bf16[256,2,256]{0,2,1:T(8,128)(2,1)} %fusion.12), channel_id=1, source_target_pairs={{0,7},{1,0},{2,1},{3,2},{4,3},{5,4},{6,5},{7,6},{8,15},{9,8},{10,9... | collective-permute-start | bytes 786440 | tf_op jit(solution)/shard_map/ppermute | solution.py:57
  97.7 8.6 %collective-permute-start.11 = (bf16[256,2,256]{0,2,1:T(8,128)(2,1)S(1)}, bf16[256,2,256]{0,2,1:T(8,128)(2,1)S(1)}, u32[]{:S(2)}, u32[]{:S(2)}) collective-permute-start(bf16[256,2,256]{0,2,1:T(8,128)(2,1)S(1)} %fusion.14), channel_id=1, source_target_pairs={{0,1},{1,2},{2,3},{3,4},{4,5},{5,6},{6,7},{7,0},{8,9},{9,10},{10,1... | collective-permute-start | bytes 786440 | tf_op jit(solution)/shard_map/ppermute | solution.py:57
  100.6 8.2 %collective-permute-start.15 = (bf16[256,2,256]{0,2,1:T(8,128)(2,1)S(1)}, bf16[256,2,256]{0,2,1:T(8,128)(2,1)S(1)}, u32[]{:S(2)}, u32[]{:S(2)}) collective-permute-start(bf16[256,2,256]{0,2,1:T(8,128)(2,1)S(1)} %fusion.11), channel_id=1, source_target_pairs={{0,7},{1,0},{2,1},{3,2},{4,3},{5,4},{6,5},{7,6},{8,15},{9,8},{10,9... | collective-permute-start | bytes 786440 | tf_op jit(solution)/shard_map/ppermute | solution.py:57
  106.4 7.7 %collective-permute-start.12 = (bf16[256,2,256]{0,2,1:T(8,128)(2,1)S(1)}, bf16[256,2,256]{0,2,1:T(8,128)(2,1)S(1)}, u32[]{:S(2)}, u32[]{:S(2)}) collective-permute-start(bf16[256,2,256]{0,2,1:T(8,128)(2,1)S(1)} %fusion.13), channel_id=1, source_target_pairs={{0,1},{1,2},{2,3},{3,4},{4,5},{5,6},{6,7},{7,0},{8,9},{9,10},{10,1... | collective-permute-start | bytes 786440 | tf_op jit(solution)/shard_map/ppermute | solution.py:57
  114.2 8.0 %collective-permute-start.16 = (f32[256,256]{0,1:T(8,128)S(1)}, f32[256,256]{0,1:T(8,128)S(1)}, u32[]{:S(2)}, u32[]{:S(2)}) collective-permute-start(f32[256,256]{0,1:T(8,128)S(1)} %select_bitcast_fusion), channel_id=1, source_target_pairs={{0,8},{1,9},{2,10},{3,11},{4,12},{5,13},{6,14},{7,15},{8,0},{9,1},... | collective-permute-start | bytes 786440 | tf_op jit(solution)/shard_map/ppermute | solution.py:80

commit v6 on v5

--- a/solution.py
+++ b/solution.py
@@ -41,12 +41,17 @@
     return by_place.transpose(2, 1, 0, 3).reshape(rows, chan_devices * block.shape[1])
 
 
-def reduce_chan(partial, chan_devices, width):
+def reduce_chan(hidden, out_weight, chan_devices, width):
     ring = chan_devices // 2
     upper = lax.axis_index("chan") >= ring
     where_in_ring = lax.axis_index("chan") % ring
-    rows = partial.shape[0]
-    slabs = partial.reshape(rows, 2, ring, width)
+    rows = hidden.shape[0]
+    rolled = jnp.roll(
+        out_weight.reshape(out_weight.shape[0], 2, ring, width), -where_in_ring, axis=2
+    ).reshape(out_weight.shape)
+    slabs = jnp.dot(hidden, rolled, preferred_element_type=jnp.float32).reshape(
+        rows, 2, ring, width
+    )
 
     def along_ring(value, by):
         pairs = [
@@ -57,7 +62,7 @@
         return lax.ppermute(value, "chan", pairs)
 
     def slab(offset):
-        return lax.dynamic_index_in_dim(slabs, (where_in_ring + offset) % ring, 2, False)
+        return slabs[:, :, offset % ring]
 
     forward_steps = ring // 2
     backward_steps = ring - 1 - forward_steps
@@ -147,8 +152,7 @@
     carried = jnp.sum(fall * incoming[None], axis=1)
     long_out = local + carried + skip_gain[None, :] * driven
     hidden = (query * long_out).astype(jnp.bfloat16)
-    partial = jnp.dot(hidden, out_weight, preferred_element_type=jnp.float32)
-    mixed = reduce_chan(partial, chan_devices, channels)
+    mixed = reduce_chan(hidden, out_weight, chan_devices, channels)
     return (stream.astype(jnp.float32) + mixed).astype(jnp.bfloat16)
 
 

time: 123 us -> 124 us (level)
  waiting for transfers between devices: 49.3 us -> 63.5 us
  local copies, waits for them, and re-layouts: 17.9 us -> 7.96 us
  starting transfers between devices: 38 us -> 34.6 us
  other arithmetic: 10.4 us -> 9.02 us
    ppermute x14, waiting for transfers between devices: 38.9 us -> 50.2 us  [along_ring(): return lax.ppermute(value, 'chan', pairs)]
    dynamic_slice x8 -> x0, local copies, waits for them, and re-layouts: 4.96 us -> none  [slab(): lax.dynamic_index_in_dim(slabs, (where_in_ring + offset) % ring, 2, False)]
    dot_general x1 -> x0, local copies, waits for them, and re-layouts: 3.28 us -> none  [on_device(): partial = jnp.dot(hidden, out_weight, preferred_element_type=jnp.float32)]
    dot_general x0 -> x1, other arithmetic: none -> 3.01 us  [reduce_chan(): jnp.dot(hidden, rolled, preferred_element_type=jnp.float32)]
    ppermute x1, waiting for transfers between devices: 0.01 us -> 2.94 us  [from_behind(): return lax.ppermute(value, axis, pairs)]
    convert_element_type x3, other arithmetic: 2.93 us -> 0.27 us  [reduce_chan(): fwd = along_ring(fwd.astype(jnp.bfloat16), 1).astype(jnp.float32)]
    ppermute x14, starting transfers between devices: 23.3 us -> 20.8 us  [along_ring(): return lax.ppermute(value, 'chan', pairs)]
    convert_element_type x2 -> x1, other arithmetic: 1.75 us -> 0.06 us  [reduce_chan(): bwd = along_ring(bwd.astype(jnp.bfloat16), -1).astype(jnp.float32)]
  transfers between devices with their start and end apart: 18 -> 18, of which waited for: 14 -> 15; matrix products, arithmetic and copies ran while one was open for 15% -> 9% of each run, Pallas kernels for 0% -> 0%
where the time goes in v6:
time: 124 us; the launch traced here: 123 us
  waiting for transfers between devices  63.5 us (51%)
  starting transfers between devices  34.6 us (28%)
  other arithmetic  9.02 us (7%)
  local copies, waits for them, and re-layouts  7.96 us (6%)
  matrix products  7.6 us (6%)
    ppermute x14, waiting for transfers between devices, along_ring(): return lax.ppermute(value, 'chan', pairs)  50.2 us
    ppermute x14, starting transfers between devices, along_ring(): return lax.ppermute(value, 'chan', pairs)  20.8 us
    unnamed x31, local copies, waits for them, and re-layouts  5.91 us
    all_to_all x1, starting transfers between devices, on_device(): lax.all_to_all(jnp.tile(device_end, (seq_devices, 1)), 'seq', 0, 0, tiled...  5.86 us
    ppermute x1, waiting for transfers between devices, reduce_chan(): return mine + lax.ppermute(theirs, 'chan', partners)  5.11 us
    ppermute x1, waiting for transfers between devices, gather_chan(): lax.ppermute(block, 'chan', [(i, (i + ring) % chan_devices) for i in rang...  3.72 us
    dot_general x1, matrix products, on_device(): jnp.dot(lower, lifted.reshape(token_rows, modes * channels), precision=la...  3.25 us
    ppermute x1, starting transfers between devices, gather_chan(): lax.ppermute(block, 'chan', [(i, (i + ring) % chan_devices) for i in rang...  3.1 us
  transfers between devices with their start and end apart: 18, of which 15 were waited for; matrix products, arithmetic and copies ran while one was open for 9% of the time, Pallas kernels for 0%

profile of v6, /device:TPU:8, one launch (start us, length us, event | category | flops | bytes accessed | tf_op | source)
XLA Modules:
  0.0 123.1 jit_solution(299974885274540292)
XLA Ops:
  0.0 0.9 copy-done
  1.0 1.0 convolution_convert_fusion
  2.0 3.1 %collective-permute-start = (bf16[256,256]{0,1:T(8,128)(2,1)S(1)}, bf16[256,256]{0,1:T(8,128)(2,1)S(1)}, u32[]{:S(2)}, u32[]{:S(2)}) collective-permute-start(bf16[256,256]{0,1:T(8,128)(2,1)S(1)} %convolution_convert_fusion), channel_id=1, source_target_pairs={{0,8},{1,9},{2,10},{3,11},{4,12},{5,13},{6,14},{7,15},{8,0},{9,1},... | collective-permute-start | bytes 393224 | tf_op jit(solution)/shard_map/ppermute | solution.py:28
  5.1 3.7 %collective-permute-done = bf16[256,256]{0,1:T(8,128)(2,1)S(1)} collective-permute-done((bf16[256,256]{0,1:T(8,128)(2,1)S(1)}, bf16[256,256]{0,1:T(8,128)(2,1)S(1)}, u32[]{:S(2)}, u32[]{:S(2)}) %collective-permute-start) | collective-permute-done | bytes 131104 | tf_op jit(solution)/shard_map/ppermute | solution.py:28
  8.9 2.0 %collective-permute-start.4 = (bf16[2,256,256]{1,2,0:T(8,128)(2,1)S(1)}, bf16[2,256,256]{1,2,0:T(8,128)(2,1)S(1)}, u32[]{:S(2)}, u32[]{:S(2)}) collective-permute-start(bf16[2,256,256]{1,2,0:T(8,128)(2,1)S(1)} %maximum_select_fusion.1), channel_id=1, source_target_pairs={{0,1},{1,2},{2,3},{3,4},{4,5},{5,6},{6,7},{7,0},{8,9},{9,10},{10,1... | collective-permute-start | bytes 786440 | tf_op jit(solution)/shard_map/ppermute | solution.py:26
  10.8 3.6 %copy.50 = bf16[32,8,16,256]{3,2,1,0:T(8,128)(2,1)} copy(bf16[32,8,16,256]{3,1,2,0:T(8,128)(2,1)} %bitcast.137) | data formatting | bytes 4194304
  14.4 4.0 %collective-permute-start.1 = (bf16[2,256,256]{1,2,0:T(8,128)(2,1)S(1)}, bf16[2,256,256]{1,2,0:T(8,128)(2,1)S(1)}, u32[]{:S(2)}, u32[]{:S(2)}) collective-permute-start(bf16[2,256,256]{1,2,0:T(8,128)(2,1)S(1)} %maximum_select_fusion.1), channel_id=1, source_target_pairs={{0,7},{1,0},{2,1},{3,2},{4,3},{5,4},{6,5},{7,6},{8,15},{9,8},{10,9... | collective-permute-start | bytes 786440 | tf_op jit(solution)/shard_map/ppermute | solution.py:26
  18.4 1.8 %collective-permute-done.4 = bf16[2,256,256]{1,2,0:T(8,128)(2,1)S(1)} collective-permute-done((bf16[2,256,256]{1,2,0:T(8,128)(2,1)S(1)}, bf16[2,256,256]{1,2,0:T(8,128)(2,1)S(1)}, u32[]{:S(2)}, u32[]{:S(2)}) %collective-permute-start.4) | collective-permute-done | bytes 262176 | tf_op jit(solution)/shard_map/ppermute | solution.py:26
  20.2 2.9 %collective-permute-done.1 = bf16[2,256,256]{1,2,0:T(8,128)(2,1)S(1)} collective-permute-done((bf16[2,256,256]{1,2,0:T(8,128)(2,1)S(1)}, bf16[2,256,256]{1,2,0:T(8,128)(2,1)S(1)}, u32[]{:S(2)}, u32[]{:S(2)}) %collective-permute-start.1) | collective-permute-done | bytes 262176 | tf_op jit(solution)/shard_map/ppermute | solution.py:26
  23.1 3.7 %collective-permute-start.2 = (bf16[2,256,256]{1,2,0:T(8,128)(2,1)S(1)}, bf16[2,256,256]{1,2,0:T(8,128)(2,1)S(1)}, u32[]{:S(2)}, u32[]{:S(2)}) collective-permute-start(bf16[2,256,256]{1,2,0:T(8,128)(2,1)S(1)} %collective-permute-done.1), channel_id=1, source_target_pairs={{0,7},{1,0},{2,1},{3,2},{4,3},{5,4},{6,5},{7,6},{8,15},{9,8},{10,9... | collective-permute-start | bytes 786440 | tf_op jit(solution)/shard_map/ppermute | solution.py:26
  26.8 3.0 %fusion.4 = bf16[2,8,256,256]{2,1,0,3:T(8,128)(2,1)S(1)} fusion(s32[]{:T(128)S(6)} %select_n.82, bf16[256,2,8,256]{3,2,1,0:T(8,128)(2,1)} %bitcast.135), kind=kLoop, calls=%fused_computation.14 | loop fusion | flops 4194304 | bytes 4194308 | tf_op jit(solution)/shard_map/dot_general | solution.py:52
  29.9 0.1 collective-permute-start.6
  30.0 0.7 collective-permute-done.2
  30.7 3.7 %collective-permute-start.3 = (bf16[2,256,256]{1,2,0:T(8,128)(2,1)S(1)}, bf16[2,256,256]{1,2,0:T(8,128)(2,1)S(1)}, u32[]{:S(2)}, u32[]{:S(2)}) collective-permute-start(bf16[2,256,256]{1,2,0:T(8,128)(2,1)S(1)} %collective-permute-done.2), channel_id=1, source_target_pairs={{0,7},{1,0},{2,1},{3,2},{4,3},{5,4},{6,5},{7,6},{8,15},{9,8},{10,9... | collective-permute-start | bytes 786440 | tf_op jit(solution)/shard_map/ppermute | solution.py:26
  34.4 3.1 %collective-permute-done.6 = bf16[2,256,256]{1,2,0:T(8,128)(2,1)S(1)} collective-permute-done((bf16[2,256,256]{1,2,0:T(8,128)(2,1)S(1)}, bf16[2,256,256]{1,2,0:T(8,128)(2,1)S(1)}, u32[]{:S(2)}, u32[]{:S(2)}) %collective-permute-start.6) | collective-permute-done | bytes 262176 | tf_op jit(solution)/shard_map/ppermute | solution.py:26
  37.6 0.8 collective-permute-done.3
  38.3 6.8 %collective-permute-done.7 = bf16[2,256,256]{1,2,0:T(8,128)(2,1)S(1)} collective-permute-done((bf16[2,256,256]{1,2,0:T(8,128)(2,1)S(1)}, bf16[2,256,256]{1,2,0:T(8,128)(2,1)S(1)}, u32[]{:S(2)}, u32[]{:S(2)}) %collective-permute-start.7) | collective-permute-done | bytes 262176 | tf_op jit(solution)/shard_map/ppermute | solution.py:26
  45.2 0.1 fusion.42
  45.5 0.6 fusion
  46.1 0.5 convert_bitcast_fusion
  46.5 0.0 copy-start.2
  46.5 0.0 slice-start.1
  46.5 0.4 copy.32
  47.0 0.5 copy-done.2
  47.5 1.0 fusion.2
  48.5 0.6 slice-done.1
  49.1 1.8 %fusion.9 = bf16[256,3,256]{2,0,1:T(8,128)(2,1)S(1)} fusion(bf16[4096,3,256]{2,0,1:T(8,128)(2,1)S(1)} %bitcast.134, bf16[256,4096]{0,1:T(8,128)(2,1)S(1)} %fusion.2), kind=kOutput, calls=%fused_computation.19 | convolution fusion | flops 1610809344 | bytes 8781824 | tf_op jit(solution)/shard_map/td,djc->tjc/dot_general | solution.py:114
  50.9 1.9 %collective-permute-start.8 = (bf16[2,3,256]{2,0,1:T(2,128)(2,1)S(1)}, bf16[2,3,256]{2,0,1:T(2,128)(2,1)S(1)}, u32[]{:S(2)}, u32[]{:S(2)}) collective-permute-start(bf16[2,3,256]{2,0,1:T(2,128)(2,1)S(1)} %slice.84), channel_id=1, source_target_pairs={{0,16},{16,32},{32,48},{48,64},{64,80},{80,96},{96,112},{112,128},... | collective-permute-start | bytes 9224 | tf_op jit(solution)/shard_map/ppermute | solution.py:12
  52.9 2.9 %collective-permute-done.8 = bf16[2,3,256]{2,0,1:T(2,128)(2,1)S(1)} collective-permute-done((bf16[2,3,256]{2,0,1:T(2,128)(2,1)S(1)}, bf16[2,3,256]{2,0,1:T(2,128)(2,1)S(1)}, u32[]{:S(2)}, u32[]{:S(2)}) %collective-permute-start.8) | collective-permute-done | bytes 3104 | tf_op jit(solution)/shard_map/ppermute | solution.py:12
  55.8 0.1 maximum_convert_fusion
  55.9 0.3 fusion.13
  56.2 0.0 copy-start.5
  56.2 0.1 copy.34
  56.4 1.3 %multiply_reduce_fusion.1 = f32[16,256]{1,0:T(8,128)S(1)} fusion(f32[16,256]{1,0:T(8,128)S(1)} %copy-done.1, f32[256,256]{0,1:T(8,128)S(1)} %copy.34), kind=kLoop, calls=%fused_computation.10 | loop fusion | flops 3141632 | bytes 294912 | tf_op jit(solution)/shard_map/reduce_sum | solution.py:141
  57.7 0.7 tile.2
  58.4 5.9 %all-to-all-start = ((f32[16,16,256]{2,1,0:T(8,128)}), f32[16,16,256]{2,1,0:T(8,128)S(1)}, u32[]{:S(2)}, u32[]{:S(2)}) async-start(f32[16,16,256]{2,1,0:T(8,128)} %tile.2), calls=%async_computation | async-start | bytes 524288 | tf_op jit(solution)/shard_map/all_to_all | solution.py:142
  64.3 0.6 bitcast_multiply_fusion
  64.9 0.0 copy-start.4
  64.9 3.3 %multiply_reduce_fusion.2 = f32[256,256]{1,0:T(8,128)S(1)} fusion(f32[16,256,256]{2,1,0:T(8,128)S(1)} %bitcast.136, f32[16,256]{1,0:T(8,128)S(1)} %get-tuple-element.10, f32[16,256]{1,0:T(8,128)S(1)} %copy-done.5), kind=kOutput, calls=%fused_computation.11 | convolution fusion | flops 3225419776 | bytes 4489216 | tf_op jit(solution)/shard_map/dot_general | solution.py:137
  68.2 1.5 %all-to-all-done = f32[16,16,256]{2,1,0:T(8,128)S(1)} async-done(((f32[16,16,256]{2,1,0:T(8,128)}), f32[16,16,256]{2,1,0:T(8,128)S(1)}, u32[]{:S(2)}, u32[]{:S(2)}) %all-to-all-start) | async-done | bytes 262176 | tf_op jit(solution)/shard_map/all_to_all | solution.py:142
  69.7 0.1 multiply_reduce_fusion.3
  69.8 0.9 multiply_reduce_fusion
  70.7 1.5 %fusion.44 = (bf16[256,2,8,256]{0,3,1,2:T(8,128)(2,1)S(1)}, f32[256,2,8,256]{0,3,1,2:T(8,128)S(1)}) fusion(bf16[2,8,256,256]{2,1,0,3:T(8,128)(2,1)S(1)} %fusion.4, f32[256,256]{1,0:T(8,128)S(1)} %multiply_reduce_fusion.2, f32[256,256]{1,0:T(8,128)S(1)} %multiply_reduce_fusion, bf16[256,3,256]{2,0,1:T(8,128)(2,1)S(1)} %fusion.13, f32[256]{0:T(256)S(1)} %copy-done.4), kind=kOutput, calls=%fused_computation.94 | convolution fusion | flops 538509312 | bytes 9307136 | tf_op jit(solution)/shard_map/dot_general | solution.py:52
  72.2 0.3 collective-permute-start.9
  72.6 10.2 %collective-permute-done.9 = bf16[256,2,256]{0,2,1:T(8,128)(2,1)S(1)} collective-permute-done((bf16[256,2,256]{0,2,1:T(8,128)(2,1)S(1)}, bf16[256,2,256]{0,2,1:T(8,128)(2,1)S(1)}, u32[]{:S(2)}, u32[]{:S(2)}) %collective-permute-start.9) | collective-permute-done | bytes 262176 | tf_op jit(solution)/shard_map/ppermute | solution.py:62
  82.8 0.1 fusion.24
  82.8 0.1 collective-permute-start.10
  82.9 3.2 %collective-permute-start.13 = (bf16[256,2,256]{0,2,1:T(8,128)(2,1)S(1)}, bf16[256,2,256]{0,2,1:T(8,128)(2,1)S(1)}, u32[]{:S(2)}, u32[]{:S(2)}) collective-permute-start(bf16[256,2,256]{0,2,1:T(8,128)(2,1)S(1)} %get-tuple-element.8), channel_id=1, source_target_pairs={{0,7},{1,0},{2,1},{3,2},{4,3},{5,4},{6,5},{7,6},{8,15},{9,8},{10,9... | collective-permute-start | bytes 786440 | tf_op jit(solution)/shard_map/ppermute | solution.py:62
  86.2 6.1 %collective-permute-done.10 = bf16[256,2,256]{0,2,1:T(8,128)(2,1)S(1)} collective-permute-done((bf16[256,2,256]{0,2,1:T(8,128)(2,1)S(1)}, bf16[256,2,256]{0,2,1:T(8,128)(2,1)S(1)}, u32[]{:S(2)}, u32[]{:S(2)}) %collective-permute-start.10) | collective-permute-done | bytes 262176 | tf_op jit(solution)/shard_map/ppermute | solution.py:62
  92.3 0.1 fusion.22
  92.4 0.1 collective-permute-start.11
  92.5 8.5 %collective-permute-done.11 = bf16[256,2,256]{0,2,1:T(8,128)(2,1)S(1)} collective-permute-done((bf16[256,2,256]{0,2,1:T(8,128)(2,1)S(1)}, bf16[256,2,256]{0,2,1:T(8,128)(2,1)S(1)}, u32[]{:S(2)}, u32[]{:S(2)}) %collective-permute-start.11) | collective-permute-done | bytes 262176 | tf_op jit(solution)/shard_map/ppermute | solution.py:62
  101.0 0.1 fusion.20
  101.1 0.1 collective-permute-start.14
  101.2 2.0 %collective-permute-start.12 = (bf16[256,2,256]{0,2,1:T(8,128)(2,1)S(1)}, bf16[256,2,256]{0,2,1:T(8,128)(2,1)S(1)}, u32[]{:S(2)}, u32[]{:S(2)}) collective-permute-start(bf16[256,2,256]{0,2,1:T(8,128)(2,1)S(1)} %get-tuple-element.5), channel_id=1, source_target_pairs={{0,1},{1,2},{2,3},{3,4},{4,5},{5,6},{6,7},{7,0},{8,9},{9,10},{10,1... | collective-permute-start | bytes 786440 | tf_op jit(solution)/shard_map/ppermute | solution.py:62
  103.2 4.4 %collective-permute-done.14 = bf16[256,2,256]{0,2,1:T(8,128)(2,1)S(1)} collective-permute-done((bf16[256,2,256]{0,2,1:T(8,128)(2,1)S(1)}, bf16[256,2,256]{0,2,1:T(8,128)(2,1)S(1)}, u32[]{:S(2)}, u32[]{:S(2)}) %collective-permute-start.14) | collective-permute-done | bytes 262176 | tf_op jit(solution)/shard_map/ppermute | solution.py:62
  107.7 0.1 fusion.16
  107.7 1.6 %collective-permute-start.15 = (bf16[256,2,256]{0,2,1:T(8,128)(2,1)S(1)}, bf16[256,2,256]{0,2,1:T(8,128)(2,1)S(1)}, u32[]{:S(2)}, u32[]{:S(2)}) collective-permute-start(bf16[256,2,256]{0,2,1:T(8,128)(2,1)S(1)} %fusion.16), channel_id=1, source_target_pairs={{0,7},{1,0},{2,1},{3,2},{4,3},{5,4},{6,5},{7,6},{8,15},{9,8},{10,9... | collective-permute-start | bytes 786440 | tf_op jit(solution)/shard_map/ppermute | solution.py:62
  109.3 4.9 %collective-permute-done.15 = bf16[256,2,256]{0,2,1:T(8,128)(2,1)S(1)} collective-permute-done((bf16[256,2,256]{0,2,1:T(8,128)(2,1)S(1)}, bf16[256,2,256]{0,2,1:T(8,128)(2,1)S(1)}, u32[]{:S(2)}, u32[]{:S(2)}) %collective-permute-start.15) | collective-permute-done | bytes 262176 | tf_op jit(solution)/shard_map/ppermute | solution.py:62
  114.2 0.1 fusion.26
  114.3 2.9 %collective-permute-start.16 = (f32[256,256]{0,1:T(8,128)S(1)}, f32[256,256]{0,1:T(8,128)S(1)}, u32[]{:S(2)}, u32[]{:S(2)}) collective-permute-start(f32[256,256]{0,1:T(8,128)S(1)} %select_bitcast_fusion), channel_id=1, source_target_pairs={{0,8},{1,9},{2,10},{3,11},{4,12},{5,13},{6,14},{7,15},{8,0},{9,1},... | collective-permute-start | bytes 786440 | tf_op jit(solution)/shard_map/ppermute | solution.py:85
  117.1 5.1 %collective-permute-done.16 = f32[256,256]{0,1:T(8,128)S(1)} collective-permute-done((f32[256,256]{0,1:T(8,128)S(1)}, f32[256,256]{0,1:T(8,128)S(1)}, u32[]{:S(2)}, u32[]{:S(2)}) %collective-permute-start.16) | collective-permute-done | bytes 262176 | tf_op jit(solution)/shard_map/ppermute | solution.py:85
  122.3 0.1 fusion.28
  122.3 0.8 copy.43
  (42 shorter events, 0.5 us)
Async XLA Ops:
  0.0 1.0 copy-start
  0.0 18.4 %copy-start.3 = (f32[3,3,256]{2,1,0:T(4,128)S(1)}, f32[3,3,256]{2,1,0:T(4,128)}, u32[]{:S(2)}) copy-start(f32[3,3,256]{2,1,0:T(4,128)} %param.13) | copy-start | bytes 27652
  2.0 6.8 %collective-permute-start = (bf16[256,256]{0,1:T(8,128)(2,1)S(1)}, bf16[256,256]{0,1:T(8,128)(2,1)S(1)}, u32[]{:S(2)}, u32[]{:S(2)}) collective-permute-start(bf16[256,256]{0,1:T(8,128)(2,1)S(1)} %convolution_convert_fusion), channel_id=1, source_target_pairs={{0,8},{1,9},{2,10},{3,11},{4,12},{5,13},{6,14},{7,15},{8,0},{9,1},... | collective-permute-start | bytes 393224 | tf_op jit(solution)/shard_map/ppermute | solution.py:28
  8.9 11.4 %collective-permute-start.4 = (bf16[2,256,256]{1,2,0:T(8,128)(2,1)S(1)}, bf16[2,256,256]{1,2,0:T(8,128)(2,1)S(1)}, u32[]{:S(2)}, u32[]{:S(2)}) collective-permute-start(bf16[2,256,256]{1,2,0:T(8,128)(2,1)S(1)} %maximum_select_fusion.1), channel_id=1, source_target_pairs={{0,1},{1,2},{2,3},{3,4},{4,5},{5,6},{6,7},{7,0},{8,9},{9,10},{10,1... | collective-permute-start | bytes 786440 | tf_op jit(solution)/shard_map/ppermute | solution.py:26
  14.4 8.7 %collective-permute-start.1 = (bf16[2,256,256]{1,2,0:T(8,128)(2,1)S(1)}, bf16[2,256,256]{1,2,0:T(8,128)(2,1)S(1)}, u32[]{:S(2)}, u32[]{:S(2)}) collective-permute-start(bf16[2,256,256]{1,2,0:T(8,128)(2,1)S(1)} %maximum_select_fusion.1), channel_id=1, source_target_pairs={{0,7},{1,0},{2,1},{3,2},{4,3},{5,4},{6,5},{7,6},{8,15},{9,8},{10,9... | collective-permute-start | bytes 786440 | tf_op jit(solution)/shard_map/ppermute | solution.py:26
  20.2 9.6 %collective-permute-start.5 = (bf16[2,256,256]{1,2,0:T(8,128)(2,1)S(1)}, bf16[2,256,256]{1,2,0:T(8,128)(2,1)S(1)}, u32[]{:S(2)}, u32[]{:S(2)}) collective-permute-start(bf16[2,256,256]{1,2,0:T(8,128)(2,1)S(1)} %collective-permute-done.4), channel_id=1, source_target_pairs={{0,1},{1,2},{2,3},{3,4},{4,5},{5,6},{6,7},{7,0},{8,9},{9,10},{10,1... | collective-permute-start | bytes 786440 | tf_op jit(solution)/shard_map/ppermute | solution.py:26
  23.1 7.6 %collective-permute-start.2 = (bf16[2,256,256]{1,2,0:T(8,128)(2,1)S(1)}, bf16[2,256,256]{1,2,0:T(8,128)(2,1)S(1)}, u32[]{:S(2)}, u32[]{:S(2)}) collective-permute-start(bf16[2,256,256]{1,2,0:T(8,128)(2,1)S(1)} %collective-permute-done.1), channel_id=1, source_target_pairs={{0,7},{1,0},{2,1},{3,2},{4,3},{5,4},{6,5},{7,6},{8,15},{9,8},{10,9... | collective-permute-start | bytes 786440 | tf_op jit(solution)/shard_map/ppermute | solution.py:26
  29.9 7.7 %collective-permute-start.6 = (bf16[2,256,256]{1,2,0:T(8,128)(2,1)S(1)}, bf16[2,256,256]{1,2,0:T(8,128)(2,1)S(1)}, u32[]{:S(2)}, u32[]{:S(2)}) collective-permute-start(bf16[2,256,256]{1,2,0:T(8,128)(2,1)S(1)} %collective-permute-done.5), channel_id=1, source_target_pairs={{0,1},{1,2},{2,3},{3,4},{4,5},{5,6},{6,7},{7,0},{8,9},{9,10},{10,1... | collective-permute-start | bytes 786440 | tf_op jit(solution)/shard_map/ppermute | solution.py:26
  30.7 7.6 %collective-permute-start.3 = (bf16[2,256,256]{1,2,0:T(8,128)(2,1)S(1)}, bf16[2,256,256]{1,2,0:T(8,128)(2,1)S(1)}, u32[]{:S(2)}, u32[]{:S(2)}) collective-permute-start(bf16[2,256,256]{1,2,0:T(8,128)(2,1)S(1)} %collective-permute-done.2), channel_id=1, source_target_pairs={{0,7},{1,0},{2,1},{3,2},{4,3},{5,4},{6,5},{7,6},{8,15},{9,8},{10,9... | collective-permute-start | bytes 786440 | tf_op jit(solution)/shard_map/ppermute | solution.py:26
  37.5 7.6 %collective-permute-start.7 = (bf16[2,256,256]{1,2,0:T(8,128)(2,1)S(1)}, bf16[2,256,256]{1,2,0:T(8,128)(2,1)S(1)}, u32[]{:S(2)}, u32[]{:S(2)}) collective-permute-start(bf16[2,256,256]{1,2,0:T(8,128)(2,1)S(1)} %collective-permute-done.6), channel_id=1, source_target_pairs={{0,1},{1,2},{2,3},{3,4},{4,5},{5,6},{6,7},{7,0},{8,9},{9,10},{10,1... | collective-permute-start | bytes 786440 | tf_op jit(solution)/shard_map/ppermute | solution.py:26
  46.1 2.4 %slice-start = ((s8[6291456]{0:T(1024)(128)(4,1)}), s8[4194304]{0:T(1024)(128)(4,1)S(1)}, s32[]{:S(2)}) async-start(s8[6291456]{0:T(1024)(128)(4,1)} %bitcast.133), calls=%async_computation.1 | async-start | bytes 8388608
  46.5 1.0 copy-start.2
  46.5 2.5 %slice-start.1 = ((s8[6291456]{0:T(1024)(128)(4,1)}), s8[2097152]{0:T(1024)(128)(4,1)S(1)}, s32[]{:S(2)}) async-start(s8[6291456]{0:T(1024)(128)(4,1)} %bitcast.133), calls=%async_computation.2 | async-start | bytes 4194304
  49.1 3.8 %copy-start.1 = (f32[16,256]{1,0:T(8,128)S(1)}, f32[16,256]{1,0:T(8,128)}, u32[]{:S(2)}) copy-start(f32[16,256]{1,0:T(8,128)} %param.14) | copy-start | bytes 49156
  50.9 4.9 %collective-permute-start.8 = (bf16[2,3,256]{2,0,1:T(2,128)(2,1)S(1)}, bf16[2,3,256]{2,0,1:T(2,128)(2,1)S(1)}, u32[]{:S(2)}, u32[]{:S(2)}) collective-permute-start(bf16[2,3,256]{2,0,1:T(2,128)(2,1)S(1)} %slice.84), channel_id=1, source_target_pairs={{0,16},{16,32},{32,48},{48,64},{64,80},{80,96},{96,112},{112,128},... | collective-permute-start | bytes 9224 | tf_op jit(solution)/shard_map/ppermute | solution.py:12
  56.2 8.8 %copy-start.5 = (f32[16,256]{1,0:T(8,128)S(1)}, f32[16,256]{1,0:T(8,128)}, u32[]{:S(2)}) copy-start(f32[16,256]{1,0:T(8,128)} %param.15) | copy-start | bytes 49156
  58.4 11.3 %all-to-all-start = ((f32[16,16,256]{2,1,0:T(8,128)}), f32[16,16,256]{2,1,0:T(8,128)S(1)}, u32[]{:S(2)}, u32[]{:S(2)}) async-start(f32[16,16,256]{2,1,0:T(8,128)} %tile.2), calls=%async_computation | async-start | bytes 524288 | tf_op jit(solution)/shard_map/all_to_all | solution.py:142
  64.9 5.8 %copy-start.4 = (f32[256]{0:T(256)S(1)}, f32[256]{0:T(256)}, u32[]{:S(2)}) copy-start(f32[256]{0:T(256)} %param.16) | copy-start | bytes 3076
  72.2 10.5 %collective-permute-start.9 = (bf16[256,2,256]{0,2,1:T(8,128)(2,1)S(1)}, bf16[256,2,256]{0,2,1:T(8,128)(2,1)S(1)}, u32[]{:S(2)}, u32[]{:S(2)}) collective-permute-start(bf16[256,2,256]{0,2,1:T(8,128)(2,1)S(1)} %get-tuple-element.7), channel_id=1, source_target_pairs={{0,1},{1,2},{2,3},{3,4},{4,5},{5,6},{6,7},{7,0},{8,9},{9,10},{10,1... | collective-permute-start | bytes 786440 | tf_op jit(solution)/shard_map/ppermute | solution.py:62
  82.8 9.5 %collective-permute-start.10 = (bf16[256,2,256]{0,2,1:T(8,128)(2,1)S(1)}, bf16[256,2,256]{0,2,1:T(8,128)(2,1)S(1)}, u32[]{:S(2)}, u32[]{:S(2)}) collective-permute-start(bf16[256,2,256]{0,2,1:T(8,128)(2,1)S(1)} %fusion.24), channel_id=1, source_target_pairs={{0,1},{1,2},{2,3},{3,4},{4,5},{5,6},{6,7},{7,0},{8,9},{9,10},{10,1... | collective-permute-start | bytes 786440 | tf_op jit(solution)/shard_map/ppermute | solution.py:62
  82.9 9.5 %collective-permute-start.13 = (bf16[256,2,256]{0,2,1:T(8,128)(2,1)S(1)}, bf16[256,2,256]{0,2,1:T(8,128)(2,1)S(1)}, u32[]{:S(2)}, u32[]{:S(2)}) collective-permute-start(bf16[256,2,256]{0,2,1:T(8,128)(2,1)S(1)} %get-tuple-element.8), channel_id=1, source_target_pairs={{0,7},{1,0},{2,1},{3,2},{4,3},{5,4},{6,5},{7,6},{8,15},{9,8},{10,9... | collective-permute-start | bytes 786440 | tf_op jit(solution)/shard_map/ppermute | solution.py:62
  92.4 8.6 %collective-permute-start.11 = (bf16[256,2,256]{0,2,1:T(8,128)(2,1)S(1)}, bf16[256,2,256]{0,2,1:T(8,128)(2,1)S(1)}, u32[]{:S(2)}, u32[]{:S(2)}) collective-permute-start(bf16[256,2,256]{0,2,1:T(8,128)(2,1)S(1)} %fusion.22), channel_id=1, source_target_pairs={{0,1},{1,2},{2,3},{3,4},{4,5},{5,6},{6,7},{7,0},{8,9},{9,10},{10,1... | collective-permute-start | bytes 786440 | tf_op jit(solution)/shard_map/ppermute | solution.py:62
  101.1 6.5 %collective-permute-start.14 = (bf16[256,2,256]{0,2,1:T(8,128)(2,1)S(1)}, bf16[256,2,256]{0,2,1:T(8,128)(2,1)S(1)}, u32[]{:S(2)}, u32[]{:S(2)}) collective-permute-start(bf16[256,2,256]{0,2,1:T(8,128)(2,1)S(1)} %get-tuple-element.6), channel_id=1, source_target_pairs={{0,7},{1,0},{2,1},{3,2},{4,3},{5,4},{6,5},{7,6},{8,15},{9,8},{10,9... | collective-permute-start | bytes 786440 | tf_op jit(solution)/shard_map/ppermute | solution.py:62
  101.2 8.1 %collective-permute-start.12 = (bf16[256,2,256]{0,2,1:T(8,128)(2,1)S(1)}, bf16[256,2,256]{0,2,1:T(8,128)(2,1)S(1)}, u32[]{:S(2)}, u32[]{:S(2)}) collective-permute-start(bf16[256,2,256]{0,2,1:T(8,128)(2,1)S(1)} %get-tuple-element.5), channel_id=1, source_target_pairs={{0,1},{1,2},{2,3},{3,4},{4,5},{5,6},{6,7},{7,0},{8,9},{9,10},{10,1... | collective-permute-start | bytes 786440 | tf_op jit(solution)/shard_map/ppermute | solution.py:62
  107.7 6.5 %collective-permute-start.15 = (bf16[256,2,256]{0,2,1:T(8,128)(2,1)S(1)}, bf16[256,2,256]{0,2,1:T(8,128)(2,1)S(1)}, u32[]{:S(2)}, u32[]{:S(2)}) collective-permute-start(bf16[256,2,256]{0,2,1:T(8,128)(2,1)S(1)} %fusion.16), channel_id=1, source_target_pairs={{0,7},{1,0},{2,1},{3,2},{4,3},{5,4},{6,5},{7,6},{8,15},{9,8},{10,9... | collective-permute-start | bytes 786440 | tf_op jit(solution)/shard_map/ppermute | solution.py:62
  114.3 8.0 %collective-permute-start.16 = (f32[256,256]{0,1:T(8,128)S(1)}, f32[256,256]{0,1:T(8,128)S(1)}, u32[]{:S(2)}, u32[]{:S(2)}) collective-permute-start(f32[256,256]{0,1:T(8,128)S(1)} %select_bitcast_fusion), channel_id=1, source_target_pairs={{0,8},{1,9},{2,10},{3,11},{4,12},{5,13},{6,14},{7,15},{8,0},{9,1},... | collective-permute-start | bytes 786440 | tf_op jit(solution)/shard_map/ppermute | solution.py:85

commit v7 on v6

--- a/solution.py
+++ b/solution.py
@@ -67,17 +67,17 @@
     forward_steps = ring // 2
     backward_steps = ring - 1 - forward_steps
     fwd = slab(forward_steps)
+    bwd = slab(-backward_steps)
     for step in range(1, forward_steps + 1):
         fwd = along_ring(fwd.astype(jnp.bfloat16), 1).astype(jnp.float32)
+        if step <= backward_steps:
+            bwd = along_ring(bwd.astype(jnp.bfloat16), -1).astype(jnp.float32)
         if step < forward_steps:
             fwd = fwd + slab(forward_steps - step)
+        if step < backward_steps:
+            bwd = bwd + slab(step - backward_steps)
     total = slab(0) + fwd
     if backward_steps > 0:
-        bwd = slab(-backward_steps)
-        for step in range(1, backward_steps + 1):
-            bwd = along_ring(bwd.astype(jnp.bfloat16), -1).astype(jnp.float32)
-            if step < backward_steps:
-                bwd = bwd + slab(step - backward_steps)
         total = total + bwd
     mine = jnp.where(upper, total[:, 1], total[:, 0])
     theirs = jnp.where(upper, total[:, 0], total[:, 1])
@@ -139,6 +139,7 @@
     ).reshape(token_rows, modes, channels)
     local = jnp.sum(fall * running, axis=1)
     device_end = jnp.exp(-decay_rate * (token_rows - 1)) * jnp.sum(lifted, axis=0)
+    held_weight, device_end = lax.optimization_barrier((out_weight, device_end))
     ends = lax.all_to_all(
         jnp.tile(device_end, (seq_devices, 1)), "seq", 0, 0, tiled=True
     ).reshape(seq_devices, modes, channels)
@@ -152,7 +153,7 @@
     carried = jnp.sum(fall * incoming[None], axis=1)
     long_out = local + carried + skip_gain[None, :] * driven
     hidden = (query * long_out).astype(jnp.bfloat16)
-    mixed = reduce_chan(hidden, out_weight, chan_devices, channels)
+    mixed = reduce_chan(hidden, held_weight, chan_devices, channels)
     return (stream.astype(jnp.float32) + mixed).astype(jnp.bfloat16)
 
 

time: 124 us -> 121 us (0.976)
  waiting for transfers between devices: 63.5 us -> 66.8 us
  starting transfers between devices: 34.6 us -> 32.3 us
  local copies, waits for them, and re-layouts: 7.96 us -> 5.75 us
  other arithmetic: 9.02 us -> 7.48 us
    ppermute x14, waiting for transfers between devices: 50.2 us -> 55 us  [along_ring(): return lax.ppermute(value, 'chan', pairs)]
    unnamed x31, local copies, waits for them, and re-layouts: 5.91 us -> 2.97 us
    ppermute x14, starting transfers between devices: 20.8 us -> 18.7 us  [along_ring(): return lax.ppermute(value, 'chan', pairs)]
    dot_general x1, other arithmetic: 3.01 us -> 1.43 us  [reduce_chan(): jnp.dot(hidden, rolled, preferred_element_type=jnp.float32)]
    all_to_all x1, waiting for transfers between devices: 1.51 us -> 0.01 us  [on_device(): lax.all_to_all(jnp.tile(device_end, (seq_devices, 1)), 'seq', 0, 0, tiled...]
  transfers between devices with their start and end apart: 18 -> 18, of which waited for: 15 -> 12; matrix products, arithmetic and copies ran while one was open for 9% -> 6% of each run, Pallas kernels for 0% -> 0%
where the time goes in v7:
time: 121 us; the launch traced here: 120 us
  waiting for transfers between devices  66.8 us (55%)
  starting transfers between devices  32.3 us (27%)
  matrix products  7.57 us (6%)
  other arithmetic  7.48 us (6%)
  local copies, waits for them, and re-layouts  5.75 us (5%)
    ppermute x14, waiting for transfers between devices, along_ring(): return lax.ppermute(value, 'chan', pairs)  55 us
    ppermute x14, starting transfers between devices, along_ring(): return lax.ppermute(value, 'chan', pairs)  18.7 us
    all_to_all x1, starting transfers between devices, on_device(): lax.all_to_all(jnp.tile(device_end, (seq_devices, 1)), 'seq', 0, 0, tiled...  5.86 us
    ppermute x1, waiting for transfers between devices, reduce_chan(): return mine + lax.ppermute(theirs, 'chan', partners)  5.18 us
    ppermute x1, waiting for transfers between devices, gather_chan(): lax.ppermute(block, 'chan', [(i, (i + ring) % chan_devices) for i in rang...  3.72 us
    dot_general x1, matrix products, on_device(): jnp.dot(lower, lifted.reshape(token_rows, modes * channels), precision=la...  3.25 us
    ppermute x1, starting transfers between devices, gather_chan(): lax.ppermute(block, 'chan', [(i, (i + ring) % chan_devices) for i in rang...  3.1 us
    unnamed x31, local copies, waits for them, and re-layouts  2.97 us
  transfers between devices with their start and end apart: 18, of which 12 were waited for; matrix products, arithmetic and copies ran while one was open for 6% of the time, Pallas kernels for 0%

profile of v7, /device:TPU:8, one launch (start us, length us, event | category | flops | bytes accessed | tf_op | source)
XLA Modules:
  0.0 120.5 jit_solution(3664170134609910410)
XLA Ops:
  0.0 0.9 copy-done
  1.0 1.0 convolution_convert_fusion
  2.0 3.1 %collective-permute-start = (bf16[256,256]{0,1:T(8,128)(2,1)S(1)}, bf16[256,256]{0,1:T(8,128)(2,1)S(1)}, u32[]{:S(2)}, u32[]{:S(2)}) collective-permute-start(bf16[256,256]{0,1:T(8,128)(2,1)S(1)} %convolution_convert_fusion), channel_id=1, source_target_pairs={{0,8},{1,9},{2,10},{3,11},{4,12},{5,13},{6,14},{7,15},{8,0},{9,1},... | collective-permute-start | bytes 393224 | tf_op jit(solution)/shard_map/ppermute | solution.py:28
  5.1 3.7 %collective-permute-done = bf16[256,256]{0,1:T(8,128)(2,1)S(1)} collective-permute-done((bf16[256,256]{0,1:T(8,128)(2,1)S(1)}, bf16[256,256]{0,1:T(8,128)(2,1)S(1)}, u32[]{:S(2)}, u32[]{:S(2)}) %collective-permute-start) | collective-permute-done | bytes 131104 | tf_op jit(solution)/shard_map/ppermute | solution.py:28
  8.9 2.0 %collective-permute-start.4 = (bf16[2,256,256]{1,2,0:T(8,128)(2,1)S(1)}, bf16[2,256,256]{1,2,0:T(8,128)(2,1)S(1)}, u32[]{:S(2)}, u32[]{:S(2)}) collective-permute-start(bf16[2,256,256]{1,2,0:T(8,128)(2,1)S(1)} %maximum_select_fusion.1), channel_id=1, source_target_pairs={{0,1},{1,2},{2,3},{3,4},{4,5},{5,6},{6,7},{7,0},{8,9},{9,10},{10,1... | collective-permute-start | bytes 786440 | tf_op jit(solution)/shard_map/ppermute | solution.py:26
  10.8 4.0 %collective-permute-start.1 = (bf16[2,256,256]{1,2,0:T(8,128)(2,1)S(1)}, bf16[2,256,256]{1,2,0:T(8,128)(2,1)S(1)}, u32[]{:S(2)}, u32[]{:S(2)}) collective-permute-start(bf16[2,256,256]{1,2,0:T(8,128)(2,1)S(1)} %maximum_select_fusion.1), channel_id=1, source_target_pairs={{0,7},{1,0},{2,1},{3,2},{4,3},{5,4},{6,5},{7,6},{8,15},{9,8},{10,9... | collective-permute-start | bytes 786440 | tf_op jit(solution)/shard_map/ppermute | solution.py:26
  14.9 5.4 %collective-permute-done.4 = bf16[2,256,256]{1,2,0:T(8,128)(2,1)S(1)} collective-permute-done((bf16[2,256,256]{1,2,0:T(8,128)(2,1)S(1)}, bf16[2,256,256]{1,2,0:T(8,128)(2,1)S(1)}, u32[]{:S(2)}, u32[]{:S(2)}) %collective-permute-start.4) | collective-permute-done | bytes 262176 | tf_op jit(solution)/shard_map/ppermute | solution.py:26
  20.2 3.2 %collective-permute-start.2 = (bf16[2,256,256]{1,2,0:T(8,128)(2,1)S(1)}, bf16[2,256,256]{1,2,0:T(8,128)(2,1)S(1)}, u32[]{:S(2)}, u32[]{:S(2)}) collective-permute-start(bf16[2,256,256]{1,2,0:T(8,128)(2,1)S(1)} %collective-permute-done.1), channel_id=1, source_target_pairs={{0,7},{1,0},{2,1},{3,2},{4,3},{5,4},{6,5},{7,6},{8,15},{9,8},{10,9... | collective-permute-start | bytes 786440 | tf_op jit(solution)/shard_map/ppermute | solution.py:26
  23.5 0.7 slice_bitcast_fusion.10
  24.2 3.9 %collective-permute-done.5 = bf16[2,256,256]{1,2,0:T(8,128)(2,1)S(1)} collective-permute-done((bf16[2,256,256]{1,2,0:T(8,128)(2,1)S(1)}, bf16[2,256,256]{1,2,0:T(8,128)(2,1)S(1)}, u32[]{:S(2)}, u32[]{:S(2)}) %collective-permute-start.5) | collective-permute-done | bytes 262176 | tf_op jit(solution)/shard_map/ppermute | solution.py:26
  28.1 0.0 collective-permute-start.6
  28.1 3.3 %collective-permute-start.3 = (bf16[2,256,256]{1,2,0:T(8,128)(2,1)S(1)}, bf16[2,256,256]{1,2,0:T(8,128)(2,1)S(1)}, u32[]{:S(2)}, u32[]{:S(2)}) collective-permute-start(bf16[2,256,256]{1,2,0:T(8,128)(2,1)S(1)} %collective-permute-done.2), channel_id=1, source_target_pairs={{0,7},{1,0},{2,1},{3,2},{4,3},{5,4},{6,5},{7,6},{8,15},{9,8},{10,9... | collective-permute-start | bytes 786440 | tf_op jit(solution)/shard_map/ppermute | solution.py:26
  31.5 4.2 %collective-permute-done.6 = bf16[2,256,256]{1,2,0:T(8,128)(2,1)S(1)} collective-permute-done((bf16[2,256,256]{1,2,0:T(8,128)(2,1)S(1)}, bf16[2,256,256]{1,2,0:T(8,128)(2,1)S(1)}, u32[]{:S(2)}, u32[]{:S(2)}) %collective-permute-start.6) | collective-permute-done | bytes 262176 | tf_op jit(solution)/shard_map/ppermute | solution.py:26
  35.6 0.0 collective-permute-start.7
  35.7 0.0 collective-permute-done.3
  35.7 7.5 %collective-permute-done.7 = bf16[2,256,256]{1,2,0:T(8,128)(2,1)S(1)} collective-permute-done((bf16[2,256,256]{1,2,0:T(8,128)(2,1)S(1)}, bf16[2,256,256]{1,2,0:T(8,128)(2,1)S(1)}, u32[]{:S(2)}, u32[]{:S(2)}) %collective-permute-start.7) | collective-permute-done | bytes 262176 | tf_op jit(solution)/shard_map/ppermute | solution.py:26
  43.3 0.1 fusion.42
  43.6 0.6 fusion
  44.2 0.5 convert_bitcast_fusion
  44.6 0.0 copy-start.3
  44.6 0.0 slice-start.1
  44.7 0.4 copy.32
  45.1 0.5 copy-done.3
  45.6 1.0 fusion.2
  46.6 0.6 slice-done.1
  47.2 1.8 %fusion.9 = bf16[256,3,256]{2,0,1:T(8,128)(2,1)S(1)} fusion(bf16[4096,3,256]{2,0,1:T(8,128)(2,1)S(1)} %bitcast.134, bf16[256,4096]{0,1:T(8,128)(2,1)S(1)} %fusion.2), kind=kOutput, calls=%fused_computation.19 | convolution fusion | flops 1610809344 | bytes 8781824 | tf_op jit(solution)/shard_map/td,djc->tjc/dot_general | solution.py:114
  49.0 1.9 %collective-permute-start.8 = (bf16[2,3,256]{2,0,1:T(2,128)(2,1)S(1)}, bf16[2,3,256]{2,0,1:T(2,128)(2,1)S(1)}, u32[]{:S(2)}, u32[]{:S(2)}) collective-permute-start(bf16[2,3,256]{2,0,1:T(2,128)(2,1)S(1)} %slice.84), channel_id=1, source_target_pairs={{0,16},{16,32},{32,48},{48,64},{64,80},{80,96},{96,112},{112,128},... | collective-permute-start | bytes 9224 | tf_op jit(solution)/shard_map/ppermute | solution.py:12
  51.0 2.9 %collective-permute-done.8 = bf16[2,3,256]{2,0,1:T(2,128)(2,1)S(1)} collective-permute-done((bf16[2,3,256]{2,0,1:T(2,128)(2,1)S(1)}, bf16[2,3,256]{2,0,1:T(2,128)(2,1)S(1)}, u32[]{:S(2)}, u32[]{:S(2)}) %collective-permute-start.8) | collective-permute-done | bytes 3104 | tf_op jit(solution)/shard_map/ppermute | solution.py:12
  53.9 0.1 maximum_convert_fusion
  54.0 0.3 fusion.13
  54.3 0.0 copy-start.5
  54.3 0.1 copy.34
  54.5 1.3 %multiply_reduce_fusion.1 = f32[16,256]{1,0:T(8,128)S(1)} fusion(f32[16,256]{1,0:T(8,128)S(1)} %copy-done.2, f32[256,256]{0,1:T(8,128)S(1)} %copy.34), kind=kLoop, calls=%fused_computation.10 | loop fusion | flops 3141632 | bytes 294912 | tf_op jit(solution)/shard_map/reduce_sum | solution.py:141
  55.8 0.7 tile.2
  56.5 5.9 %all-to-all-start = ((f32[16,16,256]{2,1,0:T(8,128)}), f32[16,16,256]{2,1,0:T(8,128)S(1)}, u32[]{:S(2)}, u32[]{:S(2)}) async-start(f32[16,16,256]{2,1,0:T(8,128)} %tile.2), calls=%async_computation | async-start | bytes 524288 | tf_op jit(solution)/shard_map/all_to_all | solution.py:143
  62.4 0.6 bitcast_multiply_fusion
  63.1 3.2 %multiply_reduce_fusion.2 = f32[256,256]{1,0:T(8,128)S(1)} fusion(f32[16,256,256]{2,1,0:T(8,128)S(1)} %bitcast.136, f32[16,256]{1,0:T(8,128)S(1)} %get-tuple-element.13, f32[16,256]{1,0:T(8,128)S(1)} %copy-done.5), kind=kOutput, calls=%fused_computation.11 | convolution fusion | flops 3225419776 | bytes 4489216 | tf_op jit(solution)/shard_map/dot_general | solution.py:137
  66.3 0.6 copy.50
  67.0 0.0 copy-start.4
  67.0 1.4 %fusion.4 = bf16[2,8,256,256]{2,1,0,3:T(8,128)(2,1)S(1)} fusion(s32[]{:T(128)S(6)} %select_n.82, bf16[256,2,8,256]{3,2,1,0:T(8,128)(2,1)S(1)} %bitcast.135), kind=kLoop, calls=%fused_computation.14 | loop fusion | flops 4194304 | bytes 4194308 | tf_op jit(solution)/shard_map/dot_general | solution.py:52
  68.4 0.1 multiply_reduce_fusion.3
  68.6 0.9 multiply_reduce_fusion
  69.5 1.4 %fusion.45 = (bf16[256,2,8,256]{0,3,1,2:T(8,128)(2,1)S(1)}, f32[256,2,8,256]{0,3,1,2:T(8,128)S(1)}) fusion(bf16[2,8,256,256]{2,1,0,3:T(8,128)(2,1)S(1)} %fusion.4, f32[256,256]{1,0:T(8,128)S(1)} %multiply_reduce_fusion.2, f32[256,256]{1,0:T(8,128)S(1)} %multiply_reduce_fusion, bf16[256,3,256]{2,0,1:T(8,128)(2,1)S(1)} %fusion.13, f32[256]{0:T(256)S(1)} %copy-done.4), kind=kOutput, calls=%fused_computation.95 | convolution fusion | flops 538509312 | bytes 9307136 | tf_op jit(solution)/shard_map/dot_general | solution.py:52
  70.9 0.1 collective-permute-start.9
  71.0 9.6 %collective-permute-done.9 = bf16[256,2,256]{0,2,1:T(8,128)(2,1)S(1)} collective-permute-done((bf16[256,2,256]{0,2,1:T(8,128)(2,1)S(1)}, bf16[256,2,256]{0,2,1:T(8,128)(2,1)S(1)}, u32[]{:S(2)}, u32[]{:S(2)}) %collective-permute-start.9) | collective-permute-done | bytes 262176 | tf_op jit(solution)/shard_map/ppermute | solution.py:62
  80.7 0.1 fusion.24
  80.7 0.1 collective-permute-start.10
  80.8 3.2 %collective-permute-start.13 = (bf16[256,2,256]{0,2,1:T(8,128)(2,1)S(1)}, bf16[256,2,256]{0,2,1:T(8,128)(2,1)S(1)}, u32[]{:S(2)}, u32[]{:S(2)}) collective-permute-start(bf16[256,2,256]{0,2,1:T(8,128)(2,1)S(1)} %get-tuple-element.12), channel_id=1, source_target_pairs={{0,7},{1,0},{2,1},{3,2},{4,3},{5,4},{6,5},{7,6},{8,15},{9,8},{10,9... | collective-permute-start | bytes 786440 | tf_op jit(solution)/shard_map/ppermute | solution.py:62
  84.0 5.5 %collective-permute-done.10 = bf16[256,2,256]{0,2,1:T(8,128)(2,1)S(1)} collective-permute-done((bf16[256,2,256]{0,2,1:T(8,128)(2,1)S(1)}, bf16[256,2,256]{0,2,1:T(8,128)(2,1)S(1)}, u32[]{:S(2)}, u32[]{:S(2)}) %collective-permute-start.10) | collective-permute-done | bytes 262176 | tf_op jit(solution)/shard_map/ppermute | solution.py:62
  89.6 0.1 fusion.22
  89.6 0.1 collective-permute-start.11
  89.7 7.9 %collective-permute-done.11 = bf16[256,2,256]{0,2,1:T(8,128)(2,1)S(1)} collective-permute-done((bf16[256,2,256]{0,2,1:T(8,128)(2,1)S(1)}, bf16[256,2,256]{0,2,1:T(8,128)(2,1)S(1)}, u32[]{:S(2)}, u32[]{:S(2)}) %collective-permute-start.11) | collective-permute-done | bytes 262176 | tf_op jit(solution)/shard_map/ppermute | solution.py:62
  97.6 0.1 fusion.20
  97.8 0.1 collective-permute-start.14
  97.9 2.0 %collective-permute-start.12 = (bf16[256,2,256]{0,2,1:T(8,128)(2,1)S(1)}, bf16[256,2,256]{0,2,1:T(8,128)(2,1)S(1)}, u32[]{:S(2)}, u32[]{:S(2)}) collective-permute-start(bf16[256,2,256]{0,2,1:T(8,128)(2,1)S(1)} %get-tuple-element.9), channel_id=1, source_target_pairs={{0,1},{1,2},{2,3},{3,4},{4,5},{5,6},{6,7},{7,0},{8,9},{9,10},{10,1... | collective-permute-start | bytes 786440 | tf_op jit(solution)/shard_map/ppermute | solution.py:62
  99.9 5.1 %collective-permute-done.14 = bf16[256,2,256]{0,2,1:T(8,128)(2,1)S(1)} collective-permute-done((bf16[256,2,256]{0,2,1:T(8,128)(2,1)S(1)}, bf16[256,2,256]{0,2,1:T(8,128)(2,1)S(1)}, u32[]{:S(2)}, u32[]{:S(2)}) %collective-permute-start.14) | collective-permute-done | bytes 262176 | tf_op jit(solution)/shard_map/ppermute | solution.py:62
  105.0 0.1 fusion.16
  105.1 0.5 collective-permute-start.15
  105.6 5.9 %collective-permute-done.15 = bf16[256,2,256]{0,2,1:T(8,128)(2,1)S(1)} collective-permute-done((bf16[256,2,256]{0,2,1:T(8,128)(2,1)S(1)}, bf16[256,2,256]{0,2,1:T(8,128)(2,1)S(1)}, u32[]{:S(2)}, u32[]{:S(2)}) %collective-permute-start.15) | collective-permute-done | bytes 262176 | tf_op jit(solution)/shard_map/ppermute | solution.py:62
  111.5 0.1 fusion.26
  111.7 2.8 %collective-permute-start.16 = (f32[256,256]{0,1:T(8,128)S(1)}, f32[256,256]{0,1:T(8,128)S(1)}, u32[]{:S(2)}, u32[]{:S(2)}) collective-permute-start(f32[256,256]{0,1:T(8,128)S(1)} %select_bitcast_fusion), channel_id=1, source_target_pairs={{0,8},{1,9},{2,10},{3,11},{4,12},{5,13},{6,14},{7,15},{8,0},{9,1},... | collective-permute-start | bytes 786440 | tf_op jit(solution)/shard_map/ppermute | solution.py:85
  114.4 5.2 %collective-permute-done.16 = f32[256,256]{0,1:T(8,128)S(1)} collective-permute-done((f32[256,256]{0,1:T(8,128)S(1)}, f32[256,256]{0,1:T(8,128)S(1)}, u32[]{:S(2)}, u32[]{:S(2)}) %collective-permute-start.16) | collective-permute-done | bytes 262176 | tf_op jit(solution)/shard_map/ppermute | solution.py:85
  119.6 0.1 fusion.28
  119.7 0.8 copy.43
  (42 shorter events, 0.5 us)
Async XLA Ops:
  0.0 1.0 copy-start
  2.0 6.8 %collective-permute-start = (bf16[256,256]{0,1:T(8,128)(2,1)S(1)}, bf16[256,256]{0,1:T(8,128)(2,1)S(1)}, u32[]{:S(2)}, u32[]{:S(2)}) collective-permute-start(bf16[256,256]{0,1:T(8,128)(2,1)S(1)} %convolution_convert_fusion), channel_id=1, source_target_pairs={{0,8},{1,9},{2,10},{3,11},{4,12},{5,13},{6,14},{7,15},{8,0},{9,1},... | collective-permute-start | bytes 393224 | tf_op jit(solution)/shard_map/ppermute | solution.py:28
  8.9 11.4 %collective-permute-start.4 = (bf16[2,256,256]{1,2,0:T(8,128)(2,1)S(1)}, bf16[2,256,256]{1,2,0:T(8,128)(2,1)S(1)}, u32[]{:S(2)}, u32[]{:S(2)}) collective-permute-start(bf16[2,256,256]{1,2,0:T(8,128)(2,1)S(1)} %maximum_select_fusion.1), channel_id=1, source_target_pairs={{0,1},{1,2},{2,3},{3,4},{4,5},{5,6},{6,7},{7,0},{8,9},{9,10},{10,1... | collective-permute-start | bytes 786440 | tf_op jit(solution)/shard_map/ppermute | solution.py:26
  10.8 9.4 %collective-permute-start.1 = (bf16[2,256,256]{1,2,0:T(8,128)(2,1)S(1)}, bf16[2,256,256]{1,2,0:T(8,128)(2,1)S(1)}, u32[]{:S(2)}, u32[]{:S(2)}) collective-permute-start(bf16[2,256,256]{1,2,0:T(8,128)(2,1)S(1)} %maximum_select_fusion.1), channel_id=1, source_target_pairs={{0,7},{1,0},{2,1},{3,2},{4,3},{5,4},{6,5},{7,6},{8,15},{9,8},{10,9... | collective-permute-start | bytes 786440 | tf_op jit(solution)/shard_map/ppermute | solution.py:26
  20.2 7.8 %collective-permute-start.5 = (bf16[2,256,256]{1,2,0:T(8,128)(2,1)S(1)}, bf16[2,256,256]{1,2,0:T(8,128)(2,1)S(1)}, u32[]{:S(2)}, u32[]{:S(2)}) collective-permute-start(bf16[2,256,256]{1,2,0:T(8,128)(2,1)S(1)} %collective-permute-done.4), channel_id=1, source_target_pairs={{0,1},{1,2},{2,3},{3,4},{4,5},{5,6},{6,7},{7,0},{8,9},{9,10},{10,1... | collective-permute-start | bytes 786440 | tf_op jit(solution)/shard_map/ppermute | solution.py:26
  20.2 7.9 %collective-permute-start.2 = (bf16[2,256,256]{1,2,0:T(8,128)(2,1)S(1)}, bf16[2,256,256]{1,2,0:T(8,128)(2,1)S(1)}, u32[]{:S(2)}, u32[]{:S(2)}) collective-permute-start(bf16[2,256,256]{1,2,0:T(8,128)(2,1)S(1)} %collective-permute-done.1), channel_id=1, source_target_pairs={{0,7},{1,0},{2,1},{3,2},{4,3},{5,4},{6,5},{7,6},{8,15},{9,8},{10,9... | collective-permute-start | bytes 786440 | tf_op jit(solution)/shard_map/ppermute | solution.py:26
  28.1 7.6 %collective-permute-start.6 = (bf16[2,256,256]{1,2,0:T(8,128)(2,1)S(1)}, bf16[2,256,256]{1,2,0:T(8,128)(2,1)S(1)}, u32[]{:S(2)}, u32[]{:S(2)}) collective-permute-start(bf16[2,256,256]{1,2,0:T(8,128)(2,1)S(1)} %collective-permute-done.5), channel_id=1, source_target_pairs={{0,1},{1,2},{2,3},{3,4},{4,5},{5,6},{6,7},{7,0},{8,9},{9,10},{10,1... | collective-permute-start | bytes 786440 | tf_op jit(solution)/shard_map/ppermute | solution.py:26
  28.1 7.5 %collective-permute-start.3 = (bf16[2,256,256]{1,2,0:T(8,128)(2,1)S(1)}, bf16[2,256,256]{1,2,0:T(8,128)(2,1)S(1)}, u32[]{:S(2)}, u32[]{:S(2)}) collective-permute-start(bf16[2,256,256]{1,2,0:T(8,128)(2,1)S(1)} %collective-permute-done.2), channel_id=1, source_target_pairs={{0,7},{1,0},{2,1},{3,2},{4,3},{5,4},{6,5},{7,6},{8,15},{9,8},{10,9... | collective-permute-start | bytes 786440 | tf_op jit(solution)/shard_map/ppermute | solution.py:26
  35.6 7.6 %collective-permute-start.7 = (bf16[2,256,256]{1,2,0:T(8,128)(2,1)S(1)}, bf16[2,256,256]{1,2,0:T(8,128)(2,1)S(1)}, u32[]{:S(2)}, u32[]{:S(2)}) collective-permute-start(bf16[2,256,256]{1,2,0:T(8,128)(2,1)S(1)} %collective-permute-done.6), channel_id=1, source_target_pairs={{0,1},{1,2},{2,3},{3,4},{4,5},{5,6},{6,7},{7,0},{8,9},{9,10},{10,1... | collective-permute-start | bytes 786440 | tf_op jit(solution)/shard_map/ppermute | solution.py:26
  44.2 2.4 %slice-start = ((s8[6291456]{0:T(1024)(128)(4,1)}), s8[4194304]{0:T(1024)(128)(4,1)S(1)}, s32[]{:S(2)}) async-start(s8[6291456]{0:T(1024)(128)(4,1)} %bitcast.133), calls=%async_computation.1 | async-start | bytes 8388608
  44.6 1.0 copy-start.3
  44.6 2.5 %slice-start.1 = ((s8[6291456]{0:T(1024)(128)(4,1)}), s8[2097152]{0:T(1024)(128)(4,1)S(1)}, s32[]{:S(2)}) async-start(s8[6291456]{0:T(1024)(128)(4,1)} %bitcast.133), calls=%async_computation.2 | async-start | bytes 4194304
  47.2 3.8 %copy-start.2 = (f32[16,256]{1,0:T(8,128)S(1)}, f32[16,256]{1,0:T(8,128)}, u32[]{:S(2)}) copy-start(f32[16,256]{1,0:T(8,128)} %param.14) | copy-start | bytes 49156
  49.0 4.9 %collective-permute-start.8 = (bf16[2,3,256]{2,0,1:T(2,128)(2,1)S(1)}, bf16[2,3,256]{2,0,1:T(2,128)(2,1)S(1)}, u32[]{:S(2)}, u32[]{:S(2)}) collective-permute-start(bf16[2,3,256]{2,0,1:T(2,128)(2,1)S(1)} %slice.84), channel_id=1, source_target_pairs={{0,16},{16,32},{32,48},{48,64},{64,80},{80,96},{96,112},{112,128},... | collective-permute-start | bytes 9224 | tf_op jit(solution)/shard_map/ppermute | solution.py:12
  54.3 8.8 %copy-start.5 = (f32[16,256]{1,0:T(8,128)S(1)}, f32[16,256]{1,0:T(8,128)}, u32[]{:S(2)}) copy-start(f32[16,256]{1,0:T(8,128)} %param.15) | copy-start | bytes 49156
  56.5 11.9 %all-to-all-start = ((f32[16,16,256]{2,1,0:T(8,128)}), f32[16,16,256]{2,1,0:T(8,128)S(1)}, u32[]{:S(2)}, u32[]{:S(2)}) async-start(f32[16,16,256]{2,1,0:T(8,128)} %tile.2), calls=%async_computation | async-start | bytes 524288 | tf_op jit(solution)/shard_map/all_to_all | solution.py:143
  62.4 3.9 %copy-start.1 = (bf16[256,4096]{1,0:T(8,128)(2,1)S(1)}, bf16[256,4096]{1,0:T(8,128)(2,1)}, u32[]{:S(2)}) copy-start(bf16[256,4096]{1,0:T(8,128)(2,1)} %param.17) | copy-start | bytes 6291460
  67.0 2.5 %copy-start.4 = (f32[256]{0:T(256)S(1)}, f32[256]{0:T(256)}, u32[]{:S(2)}) copy-start(f32[256]{0:T(256)} %param.16) | copy-start | bytes 3076
  70.9 9.7 %collective-permute-start.9 = (bf16[256,2,256]{0,2,1:T(8,128)(2,1)S(1)}, bf16[256,2,256]{0,2,1:T(8,128)(2,1)S(1)}, u32[]{:S(2)}, u32[]{:S(2)}) collective-permute-start(bf16[256,2,256]{0,2,1:T(8,128)(2,1)S(1)} %get-tuple-element.11), channel_id=1, source_target_pairs={{0,1},{1,2},{2,3},{3,4},{4,5},{5,6},{6,7},{7,0},{8,9},{9,10},{10,1... | collective-permute-start | bytes 786440 | tf_op jit(solution)/shard_map/ppermute | solution.py:62
  80.7 8.9 %collective-permute-start.10 = (bf16[256,2,256]{0,2,1:T(8,128)(2,1)S(1)}, bf16[256,2,256]{0,2,1:T(8,128)(2,1)S(1)}, u32[]{:S(2)}, u32[]{:S(2)}) collective-permute-start(bf16[256,2,256]{0,2,1:T(8,128)(2,1)S(1)} %fusion.24), channel_id=1, source_target_pairs={{0,1},{1,2},{2,3},{3,4},{4,5},{5,6},{6,7},{7,0},{8,9},{9,10},{10,1... | collective-permute-start | bytes 786440 | tf_op jit(solution)/shard_map/ppermute | solution.py:62
  80.8 8.9 %collective-permute-start.13 = (bf16[256,2,256]{0,2,1:T(8,128)(2,1)S(1)}, bf16[256,2,256]{0,2,1:T(8,128)(2,1)S(1)}, u32[]{:S(2)}, u32[]{:S(2)}) collective-permute-start(bf16[256,2,256]{0,2,1:T(8,128)(2,1)S(1)} %get-tuple-element.12), channel_id=1, source_target_pairs={{0,7},{1,0},{2,1},{3,2},{4,3},{5,4},{6,5},{7,6},{8,15},{9,8},{10,9... | collective-permute-start | bytes 786440 | tf_op jit(solution)/shard_map/ppermute | solution.py:62
  89.6 8.0 %collective-permute-start.11 = (bf16[256,2,256]{0,2,1:T(8,128)(2,1)S(1)}, bf16[256,2,256]{0,2,1:T(8,128)(2,1)S(1)}, u32[]{:S(2)}, u32[]{:S(2)}) collective-permute-start(bf16[256,2,256]{0,2,1:T(8,128)(2,1)S(1)} %fusion.22), channel_id=1, source_target_pairs={{0,1},{1,2},{2,3},{3,4},{4,5},{5,6},{6,7},{7,0},{8,9},{9,10},{10,1... | collective-permute-start | bytes 786440 | tf_op jit(solution)/shard_map/ppermute | solution.py:62
  97.8 7.2 %collective-permute-start.14 = (bf16[256,2,256]{0,2,1:T(8,128)(2,1)S(1)}, bf16[256,2,256]{0,2,1:T(8,128)(2,1)S(1)}, u32[]{:S(2)}, u32[]{:S(2)}) collective-permute-start(bf16[256,2,256]{0,2,1:T(8,128)(2,1)S(1)} %get-tuple-element.10), channel_id=1, source_target_pairs={{0,7},{1,0},{2,1},{3,2},{4,3},{5,4},{6,5},{7,6},{8,15},{9,8},{10,9... | collective-permute-start | bytes 786440 | tf_op jit(solution)/shard_map/ppermute | solution.py:62
  97.9 7.7 %collective-permute-start.12 = (bf16[256,2,256]{0,2,1:T(8,128)(2,1)S(1)}, bf16[256,2,256]{0,2,1:T(8,128)(2,1)S(1)}, u32[]{:S(2)}, u32[]{:S(2)}) collective-permute-start(bf16[256,2,256]{0,2,1:T(8,128)(2,1)S(1)} %get-tuple-element.9), channel_id=1, source_target_pairs={{0,1},{1,2},{2,3},{3,4},{4,5},{5,6},{6,7},{7,0},{8,9},{9,10},{10,1... | collective-permute-start | bytes 786440 | tf_op jit(solution)/shard_map/ppermute | solution.py:62
  105.1 6.5 %collective-permute-start.15 = (bf16[256,2,256]{0,2,1:T(8,128)(2,1)S(1)}, bf16[256,2,256]{0,2,1:T(8,128)(2,1)S(1)}, u32[]{:S(2)}, u32[]{:S(2)}) collective-permute-start(bf16[256,2,256]{0,2,1:T(8,128)(2,1)S(1)} %fusion.16), channel_id=1, source_target_pairs={{0,7},{1,0},{2,1},{3,2},{4,3},{5,4},{6,5},{7,6},{8,15},{9,8},{10,9... | collective-permute-start | bytes 786440 | tf_op jit(solution)/shard_map/ppermute | solution.py:62
  111.7 8.0 %collective-permute-start.16 = (f32[256,256]{0,1:T(8,128)S(1)}, f32[256,256]{0,1:T(8,128)S(1)}, u32[]{:S(2)}, u32[]{:S(2)}) collective-permute-start(f32[256,256]{0,1:T(8,128)S(1)} %select_bitcast_fusion), channel_id=1, source_target_pairs={{0,8},{1,9},{2,10},{3,11},{4,12},{5,13},{6,14},{7,15},{8,0},{9,1},... | collective-permute-start | bytes 786440 | tf_op jit(solution)/shard_map/ppermute | solution.py:85

commit v8 on v7

--- a/solution.py
+++ b/solution.py
@@ -25,20 +25,26 @@
         ]
         return lax.ppermute(value, "chan", pairs)
 
+    def around(value):
+        ahead, behind = [], []
+        fwd, bwd = value, value
+        for step in range(1, ring // 2 + 1):
+            fwd = along_ring(fwd, 1)
+            behind.append(fwd)
+            if step < ring - ring // 2:
+                bwd = along_ring(bwd, -1)
+                ahead.append(bwd)
+        by_offset = jnp.stack([value] + ahead + behind[::-1])
+        return jnp.roll(by_offset, where_in_ring, axis=0)
+
     other = lax.ppermute(block, "chan", [(i, (i + ring) % chan_devices) for i in range(chan_devices)])
-    pair = jnp.where(upper, jnp.stack([other, block]), jnp.stack([block, other]))
-    ahead, behind = [], []
-    fwd, bwd = pair, pair
-    for step in range(1, ring // 2 + 1):
-        fwd = along_ring(fwd, 1)
-        behind.append(fwd)
-        if step < ring - ring // 2:
-            bwd = along_ring(bwd, -1)
-            ahead.append(bwd)
-    by_offset = jnp.stack([pair] + ahead + behind[::-1])
-    by_place = jnp.roll(by_offset, where_in_ring, axis=0)
+    own_side = around(block)
+    other_side = around(other)
+    by_place = jnp.where(
+        upper, jnp.stack([other_side, own_side]), jnp.stack([own_side, other_side])
+    )
     rows = block.shape[0]
-    return by_place.transpose(2, 1, 0, 3).reshape(rows, chan_devices * block.shape[1])
+    return by_place.transpose(2, 0, 1, 3).reshape(rows, chan_devices * block.shape[1])
 
 
 def reduce_chan(hidden, out_weight, chan_devices, width):
@@ -61,8 +67,10 @@
         ]
         return lax.ppermute(value, "chan", pairs)
 
+    pieces = lax.optimization_barrier(tuple(slabs[:, :, o] for o in range(ring)))
+
     def slab(offset):
-        return slabs[:, :, offset % ring]
+        return pieces[offset % ring]
 
     forward_steps = ring // 2
     backward_steps = ring - 1 - forward_steps

time: 121 us -> 125 us (1.033)
  waiting for transfers between devices: 66.8 us -> 44.7 us
  starting transfers between devices: 32.3 us -> 46.4 us
  local copies, waits for them, and re-layouts: 5.75 us -> 10.9 us
  other arithmetic: 7.48 us -> 11.7 us
  matrix products: 7.57 us -> 10.3 us
    ppermute x14 -> x21, waiting for transfers between devices: 55 us -> 36.6 us  [along_ring(): return lax.ppermute(value, 'chan', pairs)]
    ppermute x14 -> x21, starting transfers between devices: 18.7 us -> 33.1 us  [along_ring(): return lax.ppermute(value, 'chan', pairs)]
    convert_element_type x1, local copies, waits for them, and re-layouts: 0.39 us -> 5.42 us  [on_device(): gathered_f = gathered.astype(jnp.float32)]
    ppermute x1, waiting for transfers between devices: 3.72 us -> 0.01 us  [gather_chan(): lax.ppermute(block, 'chan', [(i, (i + ring) % chan_devices) for i in rang...]
    dot_general x1, matrix products: 1.84 us -> 4.63 us  [on_device(): jnp.einsum('td,djc->tjc', normed, in_weight, preferred_element_type=jnp.f...]
    convert_element_type x1, other arithmetic: 0.45 us -> 2.31 us  [on_device(): gathered_f = gathered.astype(jnp.float32)]
    convert_element_type x1, other arithmetic: 1 us -> 2.58 us  [on_device(): normed = (gathered_f * scale * norm_gain[None, :]).astype(jnp.bfloat16)]
    unnamed x31 -> x27, local copies, waits for them, and re-layouts: 2.97 us -> 1.76 us
  transfers between devices with their start and end apart: 18 -> 25, of which waited for: 12 -> 12; matrix products, arithmetic and copies ran while one was open for 6% -> 6% of each run, Pallas kernels for 0% -> 0%
where the time goes in v8:
time: 125 us
  starting transfers between devices  46.4 us (37%)
  waiting for transfers between devices  44.7 us (36%)
  other arithmetic  11.7 us (9%)
  local copies, waits for them, and re-layouts  10.9 us (9%)
  matrix products  10.3 us (8%)
    ppermute x21, waiting for transfers between devices, along_ring(): return lax.ppermute(value, 'chan', pairs)  36.6 us
    ppermute x21, starting transfers between devices, along_ring(): return lax.ppermute(value, 'chan', pairs)  33.1 us
    all_to_all x1, starting transfers between devices, on_device(): lax.all_to_all(jnp.tile(device_end, (seq_devices, 1)), 'seq', 0, 0, tiled...  5.51 us
    convert_element_type x1, local copies, waits for them, and re-layouts, on_device(): gathered_f = gathered.astype(jnp.float32)  5.42 us
    ppermute x1, waiting for transfers between devices, reduce_chan(): return mine + lax.ppermute(theirs, 'chan', partners)  5.14 us
    dot_general x1, matrix products, on_device(): jnp.einsum('td,djc->tjc', normed, in_weight, preferred_element_type=jnp.f...  4.63 us
    dot_general x1, matrix products, on_device(): jnp.dot(lower, lifted.reshape(token_rows, modes * channels), precision=la...  3.26 us
    ppermute x1, starting transfers between devices, gather_chan(): lax.ppermute(block, 'chan', [(i, (i + ring) % chan_devices) for i in rang...  3.1 us
  transfers between devices with their start and end apart: 25, of which 12 were waited for; matrix products, arithmetic and copies ran while one was open for 6% of the time, Pallas kernels for 0%

profile of v8, /device:TPU:8, one launch (start us, length us, event | category | flops | bytes accessed | tf_op | source)
XLA Modules:
  0.0 124.6 jit_solution(6672759311125981808)
XLA Ops:
  0.0 0.9 copy-done
  1.0 1.0 bitcast_dynamic-update-slice_fusion.7
  2.0 3.1 %collective-permute-start = (bf16[256,256]{0,1:T(8,128)(2,1)S(1)}, bf16[256,256]{0,1:T(8,128)(2,1)S(1)}, u32[]{:S(2)}, u32[]{:S(2)}) collective-permute-start(bf16[256,256]{0,1:T(8,128)(2,1)S(1)} %get-tuple-element.40), channel_id=1, source_target_pairs={{0,8},{1,9},{2,10},{3,11},{4,12},{5,13},{6,14},{7,15},{8,0},{9,1},... | collective-permute-start | bytes 393224 | tf_op jit(solution)/shard_map/ppermute | solution.py:40
  5.1 5.9 %collective-permute-start.8 = (bf16[256,256]{0,1:T(8,128)(2,1)S(1)}, bf16[256,256]{0,1:T(8,128)(2,1)S(1)}, u32[]{:S(2)}, u32[]{:S(2)}) collective-permute-start(bf16[256,256]{0,1:T(8,128)(2,1)S(1)} %get-tuple-element.40), channel_id=1, source_target_pairs={{0,7},{1,0},{2,1},{3,2},{4,3},{5,4},{6,5},{7,6},{8,15},{9,8},{10,9... | collective-permute-start | bytes 393224 | tf_op jit(solution)/shard_map/ppermute | solution.py:26
  11.0 0.7 slice_bitcast_fusion.10
  11.7 3.3 %collective-permute-start.1 = (bf16[256,256]{0,1:T(8,128)(2,1)S(1)}, bf16[256,256]{0,1:T(8,128)(2,1)S(1)}, u32[]{:S(2)}, u32[]{:S(2)}) collective-permute-start(bf16[256,256]{0,1:T(8,128)(2,1)S(1)} %collective-permute-done), channel_id=1, source_target_pairs={{0,7},{1,0},{2,1},{3,2},{4,3},{5,4},{6,5},{7,6},{8,15},{9,8},{10,9... | collective-permute-start | bytes 393224 | tf_op jit(solution)/shard_map/ppermute | solution.py:26
  15.0 3.2 %collective-permute-start.9 = (bf16[256,256]{0,1:T(8,128)(2,1)S(1)}, bf16[256,256]{0,1:T(8,128)(2,1)S(1)}, u32[]{:S(2)}, u32[]{:S(2)}) collective-permute-start(bf16[256,256]{0,1:T(8,128)(2,1)S(1)} %collective-permute-done.8), channel_id=1, source_target_pairs={{0,7},{1,0},{2,1},{3,2},{4,3},{5,4},{6,5},{7,6},{8,15},{9,8},{10,9... | collective-permute-start | bytes 393224 | tf_op jit(solution)/shard_map/ppermute | solution.py:26
  18.3 0.1 collective-permute-start.12
  18.4 3.5 %collective-permute-start.2 = (bf16[256,256]{0,1:T(8,128)(2,1)S(1)}, bf16[256,256]{0,1:T(8,128)(2,1)S(1)}, u32[]{:S(2)}, u32[]{:S(2)}) collective-permute-start(bf16[256,256]{0,1:T(8,128)(2,1)S(1)} %collective-permute-done.1), channel_id=1, source_target_pairs={{0,7},{1,0},{2,1},{3,2},{4,3},{5,4},{6,5},{7,6},{8,15},{9,8},{10,9... | collective-permute-start | bytes 393224 | tf_op jit(solution)/shard_map/ppermute | solution.py:26
  21.9 0.2 collective-permute-done.4
  22.1 3.4 %collective-permute-start.10 = (bf16[256,256]{0,1:T(8,128)(2,1)S(1)}, bf16[256,256]{0,1:T(8,128)(2,1)S(1)}, u32[]{:S(2)}, u32[]{:S(2)}) collective-permute-start(bf16[256,256]{0,1:T(8,128)(2,1)S(1)} %collective-permute-done.9), channel_id=1, source_target_pairs={{0,7},{1,0},{2,1},{3,2},{4,3},{5,4},{6,5},{7,6},{8,15},{9,8},{10,9... | collective-permute-start | bytes 393224 | tf_op jit(solution)/shard_map/ppermute | solution.py:26
  25.5 0.4 collective-permute-done.12
  25.9 3.3 %collective-permute-start.3 = (bf16[256,256]{0,1:T(8,128)(2,1)S(1)}, bf16[256,256]{0,1:T(8,128)(2,1)S(1)}, u32[]{:S(2)}, u32[]{:S(2)}) collective-permute-start(bf16[256,256]{0,1:T(8,128)(2,1)S(1)} %collective-permute-done.2), channel_id=1, source_target_pairs={{0,7},{1,0},{2,1},{3,2},{4,3},{5,4},{6,5},{7,6},{8,15},{9,8},{10,9... | collective-permute-start | bytes 393224 | tf_op jit(solution)/shard_map/ppermute | solution.py:26
  29.2 3.6 %collective-permute-done.13 = bf16[256,256]{0,1:T(8,128)(2,1)S(1)} collective-permute-done((bf16[256,256]{0,1:T(8,128)(2,1)S(1)}, bf16[256,256]{0,1:T(8,128)(2,1)S(1)}, u32[]{:S(2)}, u32[]{:S(2)}) %collective-permute-start.13) | collective-permute-done | bytes 131104 | tf_op jit(solution)/shard_map/ppermute | solution.py:26
  32.9 2.5 %collective-permute-done.6 = bf16[256,256]{0,1:T(8,128)(2,1)S(1)} collective-permute-done((bf16[256,256]{0,1:T(8,128)(2,1)S(1)}, bf16[256,256]{0,1:T(8,128)(2,1)S(1)}, u32[]{:S(2)}, u32[]{:S(2)}) %collective-permute-start.6) | collective-permute-done | bytes 131104 | tf_op jit(solution)/shard_map/ppermute | solution.py:26
  35.4 3.6 %collective-permute-done.14 = bf16[256,256]{0,1:T(8,128)(2,1)S(1)} collective-permute-done((bf16[256,256]{0,1:T(8,128)(2,1)S(1)}, bf16[256,256]{0,1:T(8,128)(2,1)S(1)}, u32[]{:S(2)}, u32[]{:S(2)}) %collective-permute-start.14) | collective-permute-done | bytes 131104 | tf_op jit(solution)/shard_map/ppermute | solution.py:26
  39.1 2.5 %collective-permute-done.7 = bf16[256,256]{0,1:T(8,128)(2,1)S(1)} collective-permute-done((bf16[256,256]{0,1:T(8,128)(2,1)S(1)}, bf16[256,256]{0,1:T(8,128)(2,1)S(1)}, u32[]{:S(2)}, u32[]{:S(2)}) %collective-permute-start.7) | collective-permute-done | bytes 131104 | tf_op jit(solution)/shard_map/ppermute | solution.py:26
  41.7 0.9 fusion.12
  42.5 0.5 copy.54
  43.1 0.5 copy.53
  43.6 0.6 fusion
  44.2 2.3 %convert_bitcast_fusion = f32[256,2,8,256]{3,0,2,1:T(8,128)} fusion(bf16[1,8,256,256]{3,2,1,0:T(8,128)(2,1)S(1)} %bitcast.117, bf16[1,8,256,256]{3,2,1,0:T(8,128)(2,1)S(1)} %bitcast.115, pred[]{:T(512)S(6)} %ge.24), kind=kLoop, calls=%fused_computation.1 | loop fusion | flops 4194304 | bytes 6291457 | tf_op jit(solution)/shard_map/convert_element_type | solution.py:119
  46.6 5.4 %copy.55 = f32[256,2,8,256]{0,3,2,1:T(8,128)} copy(f32[256,2,8,256]{3,0,2,1:T(8,128)} %convert_bitcast_fusion) | data formatting | bytes 8388608 | tf_op jit(solution)/shard_map/convert_element_type | solution.py:119
  52.0 2.6 %fusion.2 = bf16[256,4096]{0,1:T(8,128)(2,1)S(1)} fusion(f32[256,2,8,256]{0,3,2,1:T(8,128)} %copy.55, f32[4096]{0:T(1024)S(1)} %copy-done.3, f32[256]{0:T(256)S(1)} %add_rsqrt_fusion), kind=kLoop, calls=%fused_computation.8 | loop fusion | flops 3145728 | bytes 6308864 | tf_op jit(solution)/shard_map/convert_element_type | solution.py:121
  54.6 0.0 copy-start.2
  54.6 4.6 %fusion.9 = bf16[256,3,256]{2,0,1:T(8,128)(2,1)S(1)} fusion(bf16[4096,3,256]{2,0,1:T(8,128)(2,1)} %param.14, bf16[256,4096]{0,1:T(8,128)(2,1)S(1)} %fusion.2), kind=kOutput, calls=%fused_computation.24 | convolution fusion | flops 1610809344 | bytes 8781824 | tf_op jit(solution)/shard_map/td,djc->tjc/dot_general | solution.py:122
  59.2 1.9 %collective-permute-start.15 = (bf16[2,3,256]{2,0,1:T(2,128)(2,1)S(1)}, bf16[2,3,256]{2,0,1:T(2,128)(2,1)S(1)}, u32[]{:S(2)}, u32[]{:S(2)}) collective-permute-start(bf16[2,3,256]{2,0,1:T(2,128)(2,1)S(1)} %slice.82), channel_id=1, source_target_pairs={{0,16},{16,32},{32,48},{48,64},{64,80},{80,96},{96,112},{112,128},... | collective-permute-start | bytes 9224 | tf_op jit(solution)/shard_map/ppermute | solution.py:12
  61.2 2.9 %collective-permute-done.15 = bf16[2,3,256]{2,0,1:T(2,128)(2,1)S(1)} collective-permute-done((bf16[2,3,256]{2,0,1:T(2,128)(2,1)S(1)}, bf16[2,3,256]{2,0,1:T(2,128)(2,1)S(1)}, u32[]{:S(2)}, u32[]{:S(2)}) %collective-permute-start.15) | collective-permute-done | bytes 3104 | tf_op jit(solution)/shard_map/ppermute | solution.py:12
  64.1 0.1 maximum_convert_fusion
  64.2 0.3 fusion.15
  64.5 0.1 copy.57
  64.7 1.3 %multiply_reduce_fusion.1 = f32[16,256]{1,0:T(8,128)S(1)} fusion(f32[16,256]{1,0:T(8,128)S(1)} %copy-done.2, f32[256,256]{0,1:T(8,128)S(1)} %copy.57), kind=kLoop, calls=%fused_computation.10 | loop fusion | flops 3141632 | bytes 294912 | tf_op jit(solution)/shard_map/reduce_sum | solution.py:149
  66.0 0.7 tile.2
  66.7 5.5 %all-to-all-start = ((f32[16,16,256]{2,1,0:T(8,128)}), f32[16,16,256]{2,1,0:T(8,128)S(1)}, u32[]{:S(2)}, u32[]{:S(2)}) async-start(f32[16,16,256]{2,1,0:T(8,128)} %tile.2), calls=%async_computation | async-start | bytes 524288 | tf_op jit(solution)/shard_map/all_to_all | solution.py:151
  72.3 0.6 bitcast_multiply_fusion
  72.9 3.3 %multiply_reduce_fusion.2 = f32[256,256]{1,0:T(8,128)S(1)} fusion(f32[16,256,256]{2,1,0:T(8,128)S(1)} %bitcast.119, f32[16,256]{1,0:T(8,128)S(1)} %get-tuple-element.34, f32[16,256]{1,0:T(8,128)S(1)} %copy-done.5), kind=kOutput, calls=%fused_computation.11 | convolution fusion | flops 3225419776 | bytes 4489216 | tf_op jit(solution)/shard_map/dot_general | solution.py:145
  76.2 0.6 copy.74
  76.8 1.4 %fusion.4 = bf16[2,8,256,256]{2,1,0,3:T(8,128)(2,1)S(1)} fusion(s32[]{:T(128)S(6)} %select_n.64, bf16[256,2,8,256]{3,2,1,0:T(8,128)(2,1)S(1)} %bitcast.118), kind=kLoop, calls=%fused_computation.14 | loop fusion | flops 4194304 | bytes 4194308 | tf_op jit(solution)/shard_map/dot_general | solution.py:58
  78.3 0.1 multiply_reduce_fusion.3
  78.4 0.9 multiply_reduce_fusion
  79.3 1.4 %fusion.5 = f32[256,2,8,256]{0,3,1,2:T(8,128)S(1)} fusion(bf16[2,8,256,256]{2,1,0,3:T(8,128)(2,1)S(1)} %fusion.4, f32[256,256]{1,0:T(8,128)S(1)} %multiply_reduce_fusion.2, f32[256,256]{1,0:T(8,128)S(1)} %multiply_reduce_fusion, bf16[256,3,256]{2,0,1:T(8,128)(2,1)S(1)} %fusion.15, f32[256]{0:T(256)S(1)} %copy-done.4), kind=kOutput, calls=%fused_computation.20 | convolution fusion | flops 537460736 | bytes 7209984 | tf_op jit(solution)/shard_map/dot_general | solution.py:58
  80.7 0.2 slice_bitcast_fusion
  81.0 0.1 slice_bitcast_fusion.2
  81.0 0.1 collective-permute-start.16
  81.1 3.2 %collective-permute-start.20 = (bf16[256,2,256]{0,2,1:T(8,128)(2,1)S(1)}, bf16[256,2,256]{0,2,1:T(8,128)(2,1)S(1)}, u32[]{:S(2)}, u32[]{:S(2)}) collective-permute-start(bf16[256,2,256]{0,2,1:T(8,128)(2,1)S(1)} %get-tuple-element.23), channel_id=1, source_target_pairs={{0,7},{1,0},{2,1},{3,2},{4,3},{5,4},{6,5},{7,6},{8,15},{9,8},{10,9... | collective-permute-start | bytes 786440 | tf_op jit(solution)/shard_map/ppermute | solution.py:68
  84.3 6.4 %collective-permute-done.16 = bf16[256,2,256]{0,2,1:T(8,128)(2,1)S(1)} collective-permute-done((bf16[256,2,256]{0,2,1:T(8,128)(2,1)S(1)}, bf16[256,2,256]{0,2,1:T(8,128)(2,1)S(1)}, u32[]{:S(2)}, u32[]{:S(2)}) %collective-permute-start.16) | collective-permute-done | bytes 262176 | tf_op jit(solution)/shard_map/ppermute | solution.py:68
  90.7 0.1 add_convert_fusion.4
  90.8 0.1 collective-permute-start.17
  90.9 0.1 add_convert_fusion.1
  91.0 3.3 %collective-permute-start.21 = (bf16[256,2,256]{0,2,1:T(8,128)(2,1)S(1)}, bf16[256,2,256]{0,2,1:T(8,128)(2,1)S(1)}, u32[]{:S(2)}, u32[]{:S(2)}) collective-permute-start(bf16[256,2,256]{0,2,1:T(8,128)(2,1)S(1)} %add_convert_fusion.1), channel_id=1, source_target_pairs={{0,7},{1,0},{2,1},{3,2},{4,3},{5,4},{6,5},{7,6},{8,15},{9,8},{10,9... | collective-permute-start | bytes 786440 | tf_op jit(solution)/shard_map/ppermute | solution.py:68
  94.3 5.4 %collective-permute-done.17 = bf16[256,2,256]{0,2,1:T(8,128)(2,1)S(1)} collective-permute-done((bf16[256,2,256]{0,2,1:T(8,128)(2,1)S(1)}, bf16[256,2,256]{0,2,1:T(8,128)(2,1)S(1)}, u32[]{:S(2)}, u32[]{:S(2)}) %collective-permute-start.17) | collective-permute-done | bytes 262176 | tf_op jit(solution)/shard_map/ppermute | solution.py:68
  99.6 0.1 add_convert_fusion.3
  99.7 0.3 collective-permute-start.18
  100.0 0.1 add_convert_fusion
  100.1 3.3 %collective-permute-start.22 = (bf16[256,2,256]{0,2,1:T(8,128)(2,1)S(1)}, bf16[256,2,256]{0,2,1:T(8,128)(2,1)S(1)}, u32[]{:S(2)}, u32[]{:S(2)}) collective-permute-start(bf16[256,2,256]{0,2,1:T(8,128)(2,1)S(1)} %add_convert_fusion), channel_id=1, source_target_pairs={{0,7},{1,0},{2,1},{3,2},{4,3},{5,4},{6,5},{7,6},{8,15},{9,8},{10,9... | collective-permute-start | bytes 786440 | tf_op jit(solution)/shard_map/ppermute | solution.py:68
  103.4 4.5 %collective-permute-done.18 = bf16[256,2,256]{0,2,1:T(8,128)(2,1)S(1)} collective-permute-done((bf16[256,2,256]{0,2,1:T(8,128)(2,1)S(1)}, bf16[256,2,256]{0,2,1:T(8,128)(2,1)S(1)}, u32[]{:S(2)}, u32[]{:S(2)}) %collective-permute-start.18) | collective-permute-done | bytes 262176 | tf_op jit(solution)/shard_map/ppermute | solution.py:68
  107.9 0.1 add_convert_fusion.2
  108.0 0.1 collective-permute-start.19
  108.1 7.6 %collective-permute-done.19 = bf16[256,2,256]{0,2,1:T(8,128)(2,1)S(1)} collective-permute-done((bf16[256,2,256]{0,2,1:T(8,128)(2,1)S(1)}, bf16[256,2,256]{0,2,1:T(8,128)(2,1)S(1)}, u32[]{:S(2)}, u32[]{:S(2)}) %collective-permute-start.19) | collective-permute-done | bytes 262176 | tf_op jit(solution)/shard_map/ppermute | solution.py:68
  115.6 0.1 convert_add_fusion
  115.8 2.8 %collective-permute-start.23 = (f32[256,256]{0,1:T(8,128)S(1)}, f32[256,256]{0,1:T(8,128)S(1)}, u32[]{:S(2)}, u32[]{:S(2)}) collective-permute-start(f32[256,256]{0,1:T(8,128)S(1)} %select_bitcast_fusion), channel_id=1, source_target_pairs={{0,8},{1,9},{2,10},{3,11},{4,12},{5,13},{6,14},{7,15},{8,0},{9,1},... | collective-permute-start | bytes 786440 | tf_op jit(solution)/shard_map/ppermute | solution.py:93
  118.6 5.1 %collective-permute-done.23 = f32[256,256]{0,1:T(8,128)S(1)} collective-permute-done((f32[256,256]{0,1:T(8,128)S(1)}, f32[256,256]{0,1:T(8,128)S(1)}, u32[]{:S(2)}, u32[]{:S(2)}) %collective-permute-start.23) | collective-permute-done | bytes 262176 | tf_op jit(solution)/shard_map/ppermute | solution.py:93
  123.7 0.1 fusion.18
  123.8 0.8 copy.67
  (54 shorter events, 0.4 us)
Async XLA Ops:
  0.0 1.0 copy-start
  2.0 9.7 %collective-permute-start = (bf16[256,256]{0,1:T(8,128)(2,1)S(1)}, bf16[256,256]{0,1:T(8,128)(2,1)S(1)}, u32[]{:S(2)}, u32[]{:S(2)}) collective-permute-start(bf16[256,256]{0,1:T(8,128)(2,1)S(1)} %get-tuple-element.40), channel_id=1, source_target_pairs={{0,8},{1,9},{2,10},{3,11},{4,12},{5,13},{6,14},{7,15},{8,0},{9,1},... | collective-permute-start | bytes 393224 | tf_op jit(solution)/shard_map/ppermute | solution.py:40
  5.1 9.9 %collective-permute-start.8 = (bf16[256,256]{0,1:T(8,128)(2,1)S(1)}, bf16[256,256]{0,1:T(8,128)(2,1)S(1)}, u32[]{:S(2)}, u32[]{:S(2)}) collective-permute-start(bf16[256,256]{0,1:T(8,128)(2,1)S(1)} %get-tuple-element.40), channel_id=1, source_target_pairs={{0,7},{1,0},{2,1},{3,2},{4,3},{5,4},{6,5},{7,6},{8,15},{9,8},{10,9... | collective-permute-start | bytes 393224 | tf_op jit(solution)/shard_map/ppermute | solution.py:26
  11.0 7.3 %collective-permute-start.11 = (bf16[256,256]{0,1:T(8,128)(2,1)S(1)}, bf16[256,256]{0,1:T(8,128)(2,1)S(1)}, u32[]{:S(2)}, u32[]{:S(2)}) collective-permute-start(bf16[256,256]{0,1:T(8,128)(2,1)S(1)} %get-tuple-element.40), channel_id=1, source_target_pairs={{0,1},{1,2},{2,3},{3,4},{4,5},{5,6},{6,7},{7,0},{8,9},{9,10},{10,1... | collective-permute-start | bytes 393224 | tf_op jit(solution)/shard_map/ppermute | solution.py:26
  11.7 6.7 %collective-permute-start.1 = (bf16[256,256]{0,1:T(8,128)(2,1)S(1)}, bf16[256,256]{0,1:T(8,128)(2,1)S(1)}, u32[]{:S(2)}, u32[]{:S(2)}) collective-permute-start(bf16[256,256]{0,1:T(8,128)(2,1)S(1)} %collective-permute-done), channel_id=1, source_target_pairs={{0,7},{1,0},{2,1},{3,2},{4,3},{5,4},{6,5},{7,6},{8,15},{9,8},{10,9... | collective-permute-start | bytes 393224 | tf_op jit(solution)/shard_map/ppermute | solution.py:26
  15.0 7.1 %collective-permute-start.4 = (bf16[256,256]{0,1:T(8,128)(2,1)S(1)}, bf16[256,256]{0,1:T(8,128)(2,1)S(1)}, u32[]{:S(2)}, u32[]{:S(2)}) collective-permute-start(bf16[256,256]{0,1:T(8,128)(2,1)S(1)} %collective-permute-done), channel_id=1, source_target_pairs={{0,1},{1,2},{2,3},{3,4},{4,5},{5,6},{6,7},{7,0},{8,9},{9,10},{10,1... | collective-permute-start | bytes 393224 | tf_op jit(solution)/shard_map/ppermute | solution.py:26
  15.0 7.1 %collective-permute-start.9 = (bf16[256,256]{0,1:T(8,128)(2,1)S(1)}, bf16[256,256]{0,1:T(8,128)(2,1)S(1)}, u32[]{:S(2)}, u32[]{:S(2)}) collective-permute-start(bf16[256,256]{0,1:T(8,128)(2,1)S(1)} %collective-permute-done.8), channel_id=1, source_target_pairs={{0,7},{1,0},{2,1},{3,2},{4,3},{5,4},{6,5},{7,6},{8,15},{9,8},{10,9... | collective-permute-start | bytes 393224 | tf_op jit(solution)/shard_map/ppermute | solution.py:26
  18.3 7.6 %collective-permute-start.12 = (bf16[256,256]{0,1:T(8,128)(2,1)S(1)}, bf16[256,256]{0,1:T(8,128)(2,1)S(1)}, u32[]{:S(2)}, u32[]{:S(2)}) collective-permute-start(bf16[256,256]{0,1:T(8,128)(2,1)S(1)} %collective-permute-done.11), channel_id=1, source_target_pairs={{0,1},{1,2},{2,3},{3,4},{4,5},{5,6},{6,7},{7,0},{8,9},{9,10},{10,1... | collective-permute-start | bytes 393224 | tf_op jit(solution)/shard_map/ppermute | solution.py:26
  18.4 7.5 %collective-permute-start.2 = (bf16[256,256]{0,1:T(8,128)(2,1)S(1)}, bf16[256,256]{0,1:T(8,128)(2,1)S(1)}, u32[]{:S(2)}, u32[]{:S(2)}) collective-permute-start(bf16[256,256]{0,1:T(8,128)(2,1)S(1)} %collective-permute-done.1), channel_id=1, source_target_pairs={{0,7},{1,0},{2,1},{3,2},{4,3},{5,4},{6,5},{7,6},{8,15},{9,8},{10,9... | collective-permute-start | bytes 393224 | tf_op jit(solution)/shard_map/ppermute | solution.py:26
  22.1 7.2 %collective-permute-start.5 = (bf16[256,256]{0,1:T(8,128)(2,1)S(1)}, bf16[256,256]{0,1:T(8,128)(2,1)S(1)}, u32[]{:S(2)}, u32[]{:S(2)}) collective-permute-start(bf16[256,256]{0,1:T(8,128)(2,1)S(1)} %collective-permute-done.4), channel_id=1, source_target_pairs={{0,1},{1,2},{2,3},{3,4},{4,5},{5,6},{6,7},{7,0},{8,9},{9,10},{10,1... | collective-permute-start | bytes 393224 | tf_op jit(solution)/shard_map/ppermute | solution.py:26
  22.1 10.8 %collective-permute-start.10 = (bf16[256,256]{0,1:T(8,128)(2,1)S(1)}, bf16[256,256]{0,1:T(8,128)(2,1)S(1)}, u32[]{:S(2)}, u32[]{:S(2)}) collective-permute-start(bf16[256,256]{0,1:T(8,128)(2,1)S(1)} %collective-permute-done.9), channel_id=1, source_target_pairs={{0,7},{1,0},{2,1},{3,2},{4,3},{5,4},{6,5},{7,6},{8,15},{9,8},{10,9... | collective-permute-start | bytes 393224 | tf_op jit(solution)/shard_map/ppermute | solution.py:26
  25.9 7.0 %collective-permute-start.13 = (bf16[256,256]{0,1:T(8,128)(2,1)S(1)}, bf16[256,256]{0,1:T(8,128)(2,1)S(1)}, u32[]{:S(2)}, u32[]{:S(2)}) collective-permute-start(bf16[256,256]{0,1:T(8,128)(2,1)S(1)} %collective-permute-done.12), channel_id=1, source_target_pairs={{0,1},{1,2},{2,3},{3,4},{4,5},{5,6},{6,7},{7,0},{8,9},{9,10},{10,1... | collective-permute-start | bytes 393224 | tf_op jit(solution)/shard_map/ppermute | solution.py:26
  25.9 13.2 %collective-permute-start.3 = (bf16[256,256]{0,1:T(8,128)(2,1)S(1)}, bf16[256,256]{0,1:T(8,128)(2,1)S(1)}, u32[]{:S(2)}, u32[]{:S(2)}) collective-permute-start(bf16[256,256]{0,1:T(8,128)(2,1)S(1)} %collective-permute-done.2), channel_id=1, source_target_pairs={{0,7},{1,0},{2,1},{3,2},{4,3},{5,4},{6,5},{7,6},{8,15},{9,8},{10,9... | collective-permute-start | bytes 393224 | tf_op jit(solution)/shard_map/ppermute | solution.py:26
  29.2 6.2 %collective-permute-start.6 = (bf16[256,256]{0,1:T(8,128)(2,1)S(1)}, bf16[256,256]{0,1:T(8,128)(2,1)S(1)}, u32[]{:S(2)}, u32[]{:S(2)}) collective-permute-start(bf16[256,256]{0,1:T(8,128)(2,1)S(1)} %collective-permute-done.5), channel_id=1, source_target_pairs={{0,1},{1,2},{2,3},{3,4},{4,5},{5,6},{6,7},{7,0},{8,9},{9,10},{10,1... | collective-permute-start | bytes 393224 | tf_op jit(solution)/shard_map/ppermute | solution.py:26
  32.9 6.2 %collective-permute-start.14 = (bf16[256,256]{0,1:T(8,128)(2,1)S(1)}, bf16[256,256]{0,1:T(8,128)(2,1)S(1)}, u32[]{:S(2)}, u32[]{:S(2)}) collective-permute-start(bf16[256,256]{0,1:T(8,128)(2,1)S(1)} %collective-permute-done.13), channel_id=1, source_target_pairs={{0,1},{1,2},{2,3},{3,4},{4,5},{5,6},{6,7},{7,0},{8,9},{9,10},{10,1... | collective-permute-start | bytes 393224 | tf_op jit(solution)/shard_map/ppermute | solution.py:26
  35.4 6.2 %collective-permute-start.7 = (bf16[256,256]{0,1:T(8,128)(2,1)S(1)}, bf16[256,256]{0,1:T(8,128)(2,1)S(1)}, u32[]{:S(2)}, u32[]{:S(2)}) collective-permute-start(bf16[256,256]{0,1:T(8,128)(2,1)S(1)} %collective-permute-done.6), channel_id=1, source_target_pairs={{0,1},{1,2},{2,3},{3,4},{4,5},{5,6},{6,7},{7,0},{8,9},{9,10},{10,1... | collective-permute-start | bytes 393224 | tf_op jit(solution)/shard_map/ppermute | solution.py:26
  46.6 5.4 %copy-start.3 = (f32[4096]{0:T(1024)S(1)}, f32[4096]{0:T(1024)}, u32[]{:S(2)}) copy-start(f32[4096]{0:T(1024)} %param.13) | copy-start | bytes 49156
  54.6 6.6 %copy-start.2 = (f32[16,256]{1,0:T(8,128)S(1)}, f32[16,256]{1,0:T(8,128)}, u32[]{:S(2)}) copy-start(f32[16,256]{1,0:T(8,128)} %param.16) | copy-start | bytes 49156
  59.2 4.9 %collective-permute-start.15 = (bf16[2,3,256]{2,0,1:T(2,128)(2,1)S(1)}, bf16[2,3,256]{2,0,1:T(2,128)(2,1)S(1)}, u32[]{:S(2)}, u32[]{:S(2)}) collective-permute-start(bf16[2,3,256]{2,0,1:T(2,128)(2,1)S(1)} %slice.82), channel_id=1, source_target_pairs={{0,16},{16,32},{32,48},{48,64},{64,80},{80,96},{96,112},{112,128},... | collective-permute-start | bytes 9224 | tf_op jit(solution)/shard_map/ppermute | solution.py:12
  64.5 8.4 %copy-start.5 = (f32[16,256]{1,0:T(8,128)S(1)}, f32[16,256]{1,0:T(8,128)}, u32[]{:S(2)}) copy-start(f32[16,256]{1,0:T(8,128)} %param.17) | copy-start | bytes 49156
  66.7 11.5 %all-to-all-start = ((f32[16,16,256]{2,1,0:T(8,128)}), f32[16,16,256]{2,1,0:T(8,128)S(1)}, u32[]{:S(2)}, u32[]{:S(2)}) async-start(f32[16,16,256]{2,1,0:T(8,128)} %tile.2), calls=%async_computation | async-start | bytes 524288 | tf_op jit(solution)/shard_map/all_to_all | solution.py:151
  72.3 3.9 %copy-start.1 = (bf16[256,4096]{1,0:T(8,128)(2,1)S(1)}, bf16[256,4096]{1,0:T(8,128)(2,1)}, u32[]{:S(2)}) copy-start(bf16[256,4096]{1,0:T(8,128)(2,1)} %param.19) | copy-start | bytes 6291460
  76.8 2.5 %copy-start.4 = (f32[256]{0:T(256)S(1)}, f32[256]{0:T(256)}, u32[]{:S(2)}) copy-start(f32[256]{0:T(256)} %param.18) | copy-start | bytes 3076
  81.0 9.7 %collective-permute-start.16 = (bf16[256,2,256]{0,2,1:T(8,128)(2,1)S(1)}, bf16[256,2,256]{0,2,1:T(8,128)(2,1)S(1)}, u32[]{:S(2)}, u32[]{:S(2)}) collective-permute-start(bf16[256,2,256]{0,2,1:T(8,128)(2,1)S(1)} %get-tuple-element.19), channel_id=1, source_target_pairs={{0,1},{1,2},{2,3},{3,4},{4,5},{5,6},{6,7},{7,0},{8,9},{9,10},{10,1... | collective-permute-start | bytes 786440 | tf_op jit(solution)/shard_map/ppermute | solution.py:68
  81.1 9.8 %collective-permute-start.20 = (bf16[256,2,256]{0,2,1:T(8,128)(2,1)S(1)}, bf16[256,2,256]{0,2,1:T(8,128)(2,1)S(1)}, u32[]{:S(2)}, u32[]{:S(2)}) collective-permute-start(bf16[256,2,256]{0,2,1:T(8,128)(2,1)S(1)} %get-tuple-element.23), channel_id=1, source_target_pairs={{0,7},{1,0},{2,1},{3,2},{4,3},{5,4},{6,5},{7,6},{8,15},{9,8},{10,9... | collective-permute-start | bytes 786440 | tf_op jit(solution)/shard_map/ppermute | solution.py:68
  90.8 8.8 %collective-permute-start.17 = (bf16[256,2,256]{0,2,1:T(8,128)(2,1)S(1)}, bf16[256,2,256]{0,2,1:T(8,128)(2,1)S(1)}, u32[]{:S(2)}, u32[]{:S(2)}) collective-permute-start(bf16[256,2,256]{0,2,1:T(8,128)(2,1)S(1)} %add_convert_fusion.4), channel_id=1, source_target_pairs={{0,1},{1,2},{2,3},{3,4},{4,5},{5,6},{6,7},{7,0},{8,9},{9,10},{10,1... | collective-permute-start | bytes 786440 | tf_op jit(solution)/shard_map/ppermute | solution.py:68
  91.0 9.1 %collective-permute-start.21 = (bf16[256,2,256]{0,2,1:T(8,128)(2,1)S(1)}, bf16[256,2,256]{0,2,1:T(8,128)(2,1)S(1)}, u32[]{:S(2)}, u32[]{:S(2)}) collective-permute-start(bf16[256,2,256]{0,2,1:T(8,128)(2,1)S(1)} %add_convert_fusion.1), channel_id=1, source_target_pairs={{0,7},{1,0},{2,1},{3,2},{4,3},{5,4},{6,5},{7,6},{8,15},{9,8},{10,9... | collective-permute-start | bytes 786440 | tf_op jit(solution)/shard_map/ppermute | solution.py:68
  99.7 8.2 %collective-permute-start.18 = (bf16[256,2,256]{0,2,1:T(8,128)(2,1)S(1)}, bf16[256,2,256]{0,2,1:T(8,128)(2,1)S(1)}, u32[]{:S(2)}, u32[]{:S(2)}) collective-permute-start(bf16[256,2,256]{0,2,1:T(8,128)(2,1)S(1)} %add_convert_fusion.3), channel_id=1, source_target_pairs={{0,1},{1,2},{2,3},{3,4},{4,5},{5,6},{6,7},{7,0},{8,9},{9,10},{10,1... | collective-permute-start | bytes 786440 | tf_op jit(solution)/shard_map/ppermute | solution.py:68
  100.1 8.0 %collective-permute-start.22 = (bf16[256,2,256]{0,2,1:T(8,128)(2,1)S(1)}, bf16[256,2,256]{0,2,1:T(8,128)(2,1)S(1)}, u32[]{:S(2)}, u32[]{:S(2)}) collective-permute-start(bf16[256,2,256]{0,2,1:T(8,128)(2,1)S(1)} %add_convert_fusion), channel_id=1, source_target_pairs={{0,7},{1,0},{2,1},{3,2},{4,3},{5,4},{6,5},{7,6},{8,15},{9,8},{10,9... | collective-permute-start | bytes 786440 | tf_op jit(solution)/shard_map/ppermute | solution.py:68
  108.0 7.7 %collective-permute-start.19 = (bf16[256,2,256]{0,2,1:T(8,128)(2,1)S(1)}, bf16[256,2,256]{0,2,1:T(8,128)(2,1)S(1)}, u32[]{:S(2)}, u32[]{:S(2)}) collective-permute-start(bf16[256,2,256]{0,2,1:T(8,128)(2,1)S(1)} %add_convert_fusion.2), channel_id=1, source_target_pairs={{0,1},{1,2},{2,3},{3,4},{4,5},{5,6},{6,7},{7,0},{8,9},{9,10},{10,1... | collective-permute-start | bytes 786440 | tf_op jit(solution)/shard_map/ppermute | solution.py:68
  115.8 8.0 %collective-permute-start.23 = (f32[256,256]{0,1:T(8,128)S(1)}, f32[256,256]{0,1:T(8,128)S(1)}, u32[]{:S(2)}, u32[]{:S(2)}) collective-permute-start(f32[256,256]{0,1:T(8,128)S(1)} %select_bitcast_fusion), channel_id=1, source_target_pairs={{0,8},{1,9},{2,10},{3,11},{4,12},{5,13},{6,14},{7,15},{8,0},{9,1},... | collective-permute-start | bytes 786440 | tf_op jit(solution)/shard_map/ppermute | solution.py:93

commit v9 on v7

--- a/solution.py
+++ b/solution.py
@@ -61,8 +61,10 @@
         ]
         return lax.ppermute(value, "chan", pairs)
 
+    pieces = lax.optimization_barrier(tuple(slabs[:, :, o] for o in range(ring)))
+
     def slab(offset):
-        return slabs[:, :, offset % ring]
+        return pieces[offset % ring]
 
     forward_steps = ring // 2
     backward_steps = ring - 1 - forward_steps
@@ -82,7 +84,7 @@
     mine = jnp.where(upper, total[:, 1], total[:, 0])
     theirs = jnp.where(upper, total[:, 0], total[:, 1])
     partners = [(i, (i + ring) % chan_devices) for i in range(chan_devices)]
-    return mine + lax.ppermute(theirs, "chan", partners)
+    return mine + lax.ppermute(theirs.astype(jnp.bfloat16), "chan", partners).astype(jnp.float32)
 
 
 def on_device(

time: 121 us -> 114 us (0.942)
  waiting for transfers between devices: 66.8 us -> 55.2 us
  starting transfers between devices: 32.3 us -> 36.6 us
    ppermute x14, waiting for transfers between devices: 55 us -> 44.8 us  [along_ring(): return lax.ppermute(value, 'chan', pairs)]
    ppermute x14, starting transfers between devices: 18.7 us -> 22.9 us  [along_ring(): return lax.ppermute(value, 'chan', pairs)]
    ppermute x1, waiting for transfers between devices: 5.18 us -> 3.76 us  [reduce_chan(): lax.ppermute(theirs.astype(jnp.bfloat16), 'chan', partners)]
  transfers between devices with their start and end apart: 18 -> 18, of which waited for: 12 -> 11; matrix products, arithmetic and copies ran while one was open for 6% -> 6% of each run, Pallas kernels for 0% -> 0%
where the time goes in v9:
time: 114 us; the launch traced here: 113 us
  waiting for transfers between devices  55.2 us (48%)
  starting transfers between devices  36.6 us (32%)
  matrix products  7.56 us (7%)
  other arithmetic  7.47 us (7%)
  local copies, waits for them, and re-layouts  6.09 us (5%)
    ppermute x14, waiting for transfers between devices, along_ring(): return lax.ppermute(value, 'chan', pairs)  44.8 us
    ppermute x14, starting transfers between devices, along_ring(): return lax.ppermute(value, 'chan', pairs)  22.9 us
    all_to_all x1, starting transfers between devices, on_device(): lax.all_to_all(jnp.tile(device_end, (seq_devices, 1)), 'seq', 0, 0, tiled...  5.86 us
    ppermute x1, waiting for transfers between devices, reduce_chan(): lax.ppermute(theirs.astype(jnp.bfloat16), 'chan', partners)  3.76 us
    ppermute x1, waiting for transfers between devices, gather_chan(): lax.ppermute(block, 'chan', [(i, (i + ring) % chan_devices) for i in rang...  3.72 us
    dot_general x1, matrix products, on_device(): jnp.dot(lower, lifted.reshape(token_rows, modes * channels), precision=la...  3.25 us
    ppermute x1, starting transfers between devices, gather_chan(): lax.ppermute(block, 'chan', [(i, (i + ring) % chan_devices) for i in rang...  3.1 us
    unnamed x31, local copies, waits for them, and re-layouts  2.97 us
  transfers between devices with their start and end apart: 18, of which 11 were waited for; matrix products, arithmetic and copies ran while one was open for 6% of the time, Pallas kernels for 0%

profile of v9, /device:TPU:8, one launch (start us, length us, event | category | flops | bytes accessed | tf_op | source)
XLA Modules:
  0.0 113.4 jit_solution(10609377201732525776)
XLA Ops:
  0.0 0.9 copy-done
  1.0 1.0 convolution_convert_fusion
  2.0 3.1 %collective-permute-start = (bf16[256,256]{0,1:T(8,128)(2,1)S(1)}, bf16[256,256]{0,1:T(8,128)(2,1)S(1)}, u32[]{:S(2)}, u32[]{:S(2)}) collective-permute-start(bf16[256,256]{0,1:T(8,128)(2,1)S(1)} %convolution_convert_fusion), channel_id=1, source_target_pairs={{0,8},{1,9},{2,10},{3,11},{4,12},{5,13},{6,14},{7,15},{8,0},{9,1},... | collective-permute-start | bytes 393224 | tf_op jit(solution)/shard_map/ppermute | solution.py:28
  5.1 3.7 %collective-permute-done = bf16[256,256]{0,1:T(8,128)(2,1)S(1)} collective-permute-done((bf16[256,256]{0,1:T(8,128)(2,1)S(1)}, bf16[256,256]{0,1:T(8,128)(2,1)S(1)}, u32[]{:S(2)}, u32[]{:S(2)}) %collective-permute-start) | collective-permute-done | bytes 131104 | tf_op jit(solution)/shard_map/ppermute | solution.py:28
  8.9 2.0 %collective-permute-start.4 = (bf16[2,256,256]{1,2,0:T(8,128)(2,1)S(1)}, bf16[2,256,256]{1,2,0:T(8,128)(2,1)S(1)}, u32[]{:S(2)}, u32[]{:S(2)}) collective-permute-start(bf16[2,256,256]{1,2,0:T(8,128)(2,1)S(1)} %maximum_select_fusion.1), channel_id=1, source_target_pairs={{0,1},{1,2},{2,3},{3,4},{4,5},{5,6},{6,7},{7,0},{8,9},{9,10},{10,1... | collective-permute-start | bytes 786440 | tf_op jit(solution)/shard_map/ppermute | solution.py:26
  10.8 4.0 %collective-permute-start.1 = (bf16[2,256,256]{1,2,0:T(8,128)(2,1)S(1)}, bf16[2,256,256]{1,2,0:T(8,128)(2,1)S(1)}, u32[]{:S(2)}, u32[]{:S(2)}) collective-permute-start(bf16[2,256,256]{1,2,0:T(8,128)(2,1)S(1)} %maximum_select_fusion.1), channel_id=1, source_target_pairs={{0,7},{1,0},{2,1},{3,2},{4,3},{5,4},{6,5},{7,6},{8,15},{9,8},{10,9... | collective-permute-start | bytes 786440 | tf_op jit(solution)/shard_map/ppermute | solution.py:26
  14.9 5.4 %collective-permute-done.4 = bf16[2,256,256]{1,2,0:T(8,128)(2,1)S(1)} collective-permute-done((bf16[2,256,256]{1,2,0:T(8,128)(2,1)S(1)}, bf16[2,256,256]{1,2,0:T(8,128)(2,1)S(1)}, u32[]{:S(2)}, u32[]{:S(2)}) %collective-permute-start.4) | collective-permute-done | bytes 262176 | tf_op jit(solution)/shard_map/ppermute | solution.py:26
  20.2 3.2 %collective-permute-start.2 = (bf16[2,256,256]{1,2,0:T(8,128)(2,1)S(1)}, bf16[2,256,256]{1,2,0:T(8,128)(2,1)S(1)}, u32[]{:S(2)}, u32[]{:S(2)}) collective-permute-start(bf16[2,256,256]{1,2,0:T(8,128)(2,1)S(1)} %collective-permute-done.1), channel_id=1, source_target_pairs={{0,7},{1,0},{2,1},{3,2},{4,3},{5,4},{6,5},{7,6},{8,15},{9,8},{10,9... | collective-permute-start | bytes 786440 | tf_op jit(solution)/shard_map/ppermute | solution.py:26
  23.5 0.7 slice_bitcast_fusion.10
  24.2 3.9 %collective-permute-done.5 = bf16[2,256,256]{1,2,0:T(8,128)(2,1)S(1)} collective-permute-done((bf16[2,256,256]{1,2,0:T(8,128)(2,1)S(1)}, bf16[2,256,256]{1,2,0:T(8,128)(2,1)S(1)}, u32[]{:S(2)}, u32[]{:S(2)}) %collective-permute-start.5) | collective-permute-done | bytes 262176 | tf_op jit(solution)/shard_map/ppermute | solution.py:26
  28.1 0.0 collective-permute-start.6
  28.1 3.3 %collective-permute-start.3 = (bf16[2,256,256]{1,2,0:T(8,128)(2,1)S(1)}, bf16[2,256,256]{1,2,0:T(8,128)(2,1)S(1)}, u32[]{:S(2)}, u32[]{:S(2)}) collective-permute-start(bf16[2,256,256]{1,2,0:T(8,128)(2,1)S(1)} %collective-permute-done.2), channel_id=1, source_target_pairs={{0,7},{1,0},{2,1},{3,2},{4,3},{5,4},{6,5},{7,6},{8,15},{9,8},{10,9... | collective-permute-start | bytes 786440 | tf_op jit(solution)/shard_map/ppermute | solution.py:26
  31.5 4.2 %collective-permute-done.6 = bf16[2,256,256]{1,2,0:T(8,128)(2,1)S(1)} collective-permute-done((bf16[2,256,256]{1,2,0:T(8,128)(2,1)S(1)}, bf16[2,256,256]{1,2,0:T(8,128)(2,1)S(1)}, u32[]{:S(2)}, u32[]{:S(2)}) %collective-permute-start.6) | collective-permute-done | bytes 262176 | tf_op jit(solution)/shard_map/ppermute | solution.py:26
  35.7 7.5 %collective-permute-done.7 = bf16[2,256,256]{1,2,0:T(8,128)(2,1)S(1)} collective-permute-done((bf16[2,256,256]{1,2,0:T(8,128)(2,1)S(1)}, bf16[2,256,256]{1,2,0:T(8,128)(2,1)S(1)}, u32[]{:S(2)}, u32[]{:S(2)}) %collective-permute-start.7) | collective-permute-done | bytes 262176 | tf_op jit(solution)/shard_map/ppermute | solution.py:26
  43.3 0.1 fusion.31
  43.6 0.6 fusion
  44.2 0.5 convert_bitcast_fusion
  44.6 0.0 copy-start.3
  44.6 0.0 slice-start.1
  44.7 0.4 copy.34
  45.1 0.5 copy-done.3
  45.6 1.0 fusion.2
  46.6 0.6 slice-done.1
  47.2 1.8 %fusion.9 = bf16[256,3,256]{2,0,1:T(8,128)(2,1)S(1)} fusion(bf16[4096,3,256]{2,0,1:T(8,128)(2,1)S(1)} %bitcast.106, bf16[256,4096]{0,1:T(8,128)(2,1)S(1)} %fusion.2), kind=kOutput, calls=%fused_computation.19 | convolution fusion | flops 1610809344 | bytes 8781824 | tf_op jit(solution)/shard_map/td,djc->tjc/dot_general | solution.py:116
  49.0 1.9 %collective-permute-start.8 = (bf16[2,3,256]{2,0,1:T(2,128)(2,1)S(1)}, bf16[2,3,256]{2,0,1:T(2,128)(2,1)S(1)}, u32[]{:S(2)}, u32[]{:S(2)}) collective-permute-start(bf16[2,3,256]{2,0,1:T(2,128)(2,1)S(1)} %slice.82), channel_id=1, source_target_pairs={{0,16},{16,32},{32,48},{48,64},{64,80},{80,96},{96,112},{112,128},... | collective-permute-start | bytes 9224 | tf_op jit(solution)/shard_map/ppermute | solution.py:12
  51.0 2.9 %collective-permute-done.8 = bf16[2,3,256]{2,0,1:T(2,128)(2,1)S(1)} collective-permute-done((bf16[2,3,256]{2,0,1:T(2,128)(2,1)S(1)}, bf16[2,3,256]{2,0,1:T(2,128)(2,1)S(1)}, u32[]{:S(2)}, u32[]{:S(2)}) %collective-permute-start.8) | collective-permute-done | bytes 3104 | tf_op jit(solution)/shard_map/ppermute | solution.py:12
  53.9 0.1 maximum_convert_fusion
  54.0 0.3 fusion.13
  54.3 0.0 copy-start.5
  54.3 0.1 copy.36
  54.5 1.3 %multiply_reduce_fusion.1 = f32[16,256]{1,0:T(8,128)S(1)} fusion(f32[16,256]{1,0:T(8,128)S(1)} %copy-done.2, f32[256,256]{0,1:T(8,128)S(1)} %copy.36), kind=kLoop, calls=%fused_computation.10 | loop fusion | flops 3141632 | bytes 294912 | tf_op jit(solution)/shard_map/reduce_sum | solution.py:143
  55.8 0.7 tile.2
  56.6 5.9 %all-to-all-start = ((f32[16,16,256]{2,1,0:T(8,128)}), f32[16,16,256]{2,1,0:T(8,128)S(1)}, u32[]{:S(2)}, u32[]{:S(2)}) async-start(f32[16,16,256]{2,1,0:T(8,128)} %tile.2), calls=%async_computation | async-start | bytes 524288 | tf_op jit(solution)/shard_map/all_to_all | solution.py:145
  62.4 0.6 bitcast_multiply_fusion
  63.1 3.2 %multiply_reduce_fusion.2 = f32[256,256]{1,0:T(8,128)S(1)} fusion(f32[16,256,256]{2,1,0:T(8,128)S(1)} %bitcast.108, f32[16,256]{1,0:T(8,128)S(1)} %get-tuple-element.33, f32[16,256]{1,0:T(8,128)S(1)} %copy-done.5), kind=kOutput, calls=%fused_computation.11 | convolution fusion | flops 3225419776 | bytes 4489216 | tf_op jit(solution)/shard_map/dot_general | solution.py:139
  66.3 0.6 copy.53
  67.0 0.0 copy-start.4
  67.0 1.4 %fusion.4 = bf16[2,8,256,256]{2,1,0,3:T(8,128)(2,1)S(1)} fusion(s32[]{:T(128)S(6)} %select_n.80, bf16[256,2,8,256]{3,2,1,0:T(8,128)(2,1)S(1)} %bitcast.107), kind=kLoop, calls=%fused_computation.14 | loop fusion | flops 4194304 | bytes 4194308 | tf_op jit(solution)/shard_map/dot_general | solution.py:52
  68.5 0.1 multiply_reduce_fusion.3
  68.6 0.9 multiply_reduce_fusion
  69.5 1.4 %fusion.5 = f32[256,2,8,256]{0,3,1,2:T(8,128)S(1)} fusion(bf16[2,8,256,256]{2,1,0,3:T(8,128)(2,1)S(1)} %fusion.4, f32[256,256]{1,0:T(8,128)S(1)} %multiply_reduce_fusion.2, f32[256,256]{1,0:T(8,128)S(1)} %multiply_reduce_fusion, bf16[256,3,256]{2,0,1:T(8,128)(2,1)S(1)} %fusion.13, f32[256]{0:T(256)S(1)} %copy-done.4), kind=kOutput, calls=%fused_computation.15 | convolution fusion | flops 537460736 | bytes 7209984 | tf_op jit(solution)/shard_map/dot_general | solution.py:52
  70.9 0.1 slice_bitcast_fusion.2
  71.0 0.3 slice_bitcast_fusion
  71.3 0.1 collective-permute-start.9
  71.4 3.2 %collective-permute-start.13 = (bf16[256,2,256]{0,2,1:T(8,128)(2,1)S(1)}, bf16[256,2,256]{0,2,1:T(8,128)(2,1)S(1)}, u32[]{:S(2)}, u32[]{:S(2)}) collective-permute-start(bf16[256,2,256]{0,2,1:T(8,128)(2,1)S(1)} %get-tuple-element.22), channel_id=1, source_target_pairs={{0,7},{1,0},{2,1},{3,2},{4,3},{5,4},{6,5},{7,6},{8,15},{9,8},{10,9... | collective-permute-start | bytes 786440 | tf_op jit(solution)/shard_map/ppermute | solution.py:62
  74.6 6.4 %collective-permute-done.9 = bf16[256,2,256]{0,2,1:T(8,128)(2,1)S(1)} collective-permute-done((bf16[256,2,256]{0,2,1:T(8,128)(2,1)S(1)}, bf16[256,2,256]{0,2,1:T(8,128)(2,1)S(1)}, u32[]{:S(2)}, u32[]{:S(2)}) %collective-permute-start.9) | collective-permute-done | bytes 262176 | tf_op jit(solution)/shard_map/ppermute | solution.py:62
  81.0 0.1 add_convert_fusion.4
  81.1 0.1 collective-permute-start.10
  81.2 0.1 add_convert_fusion.1
  81.2 3.3 %collective-permute-start.14 = (bf16[256,2,256]{0,2,1:T(8,128)(2,1)S(1)}, bf16[256,2,256]{0,2,1:T(8,128)(2,1)S(1)}, u32[]{:S(2)}, u32[]{:S(2)}) collective-permute-start(bf16[256,2,256]{0,2,1:T(8,128)(2,1)S(1)} %add_convert_fusion.1), channel_id=1, source_target_pairs={{0,7},{1,0},{2,1},{3,2},{4,3},{5,4},{6,5},{7,6},{8,15},{9,8},{10,9... | collective-permute-start | bytes 786440 | tf_op jit(solution)/shard_map/ppermute | solution.py:62
  84.5 5.4 %collective-permute-done.10 = bf16[256,2,256]{0,2,1:T(8,128)(2,1)S(1)} collective-permute-done((bf16[256,2,256]{0,2,1:T(8,128)(2,1)S(1)}, bf16[256,2,256]{0,2,1:T(8,128)(2,1)S(1)}, u32[]{:S(2)}, u32[]{:S(2)}) %collective-permute-start.10) | collective-permute-done | bytes 262176 | tf_op jit(solution)/shard_map/ppermute | solution.py:62
  89.9 0.1 add_convert_fusion.3
  90.0 0.3 collective-permute-start.11
  90.3 0.1 add_convert_fusion
  90.4 3.3 %collective-permute-start.15 = (bf16[256,2,256]{0,2,1:T(8,128)(2,1)S(1)}, bf16[256,2,256]{0,2,1:T(8,128)(2,1)S(1)}, u32[]{:S(2)}, u32[]{:S(2)}) collective-permute-start(bf16[256,2,256]{0,2,1:T(8,128)(2,1)S(1)} %add_convert_fusion), channel_id=1, source_target_pairs={{0,7},{1,0},{2,1},{3,2},{4,3},{5,4},{6,5},{7,6},{8,15},{9,8},{10,9... | collective-permute-start | bytes 786440 | tf_op jit(solution)/shard_map/ppermute | solution.py:62
  93.7 4.5 %collective-permute-done.11 = bf16[256,2,256]{0,2,1:T(8,128)(2,1)S(1)} collective-permute-done((bf16[256,2,256]{0,2,1:T(8,128)(2,1)S(1)}, bf16[256,2,256]{0,2,1:T(8,128)(2,1)S(1)}, u32[]{:S(2)}, u32[]{:S(2)}) %collective-permute-start.11) | collective-permute-done | bytes 262176 | tf_op jit(solution)/shard_map/ppermute | solution.py:62
  98.2 0.1 add_convert_fusion.2
  98.2 0.1 collective-permute-start.12
  98.3 7.6 %collective-permute-done.12 = bf16[256,2,256]{0,2,1:T(8,128)(2,1)S(1)} collective-permute-done((bf16[256,2,256]{0,2,1:T(8,128)(2,1)S(1)}, bf16[256,2,256]{0,2,1:T(8,128)(2,1)S(1)}, u32[]{:S(2)}, u32[]{:S(2)}) %collective-permute-start.12) | collective-permute-done | bytes 262176 | tf_op jit(solution)/shard_map/ppermute | solution.py:62
  105.9 0.1 convert_add_fusion
  106.1 2.8 %collective-permute-start.16 = (bf16[256,256]{0,1:T(8,128)(2,1)S(1)}, bf16[256,256]{0,1:T(8,128)(2,1)S(1)}, u32[]{:S(2)}, u32[]{:S(2)}) collective-permute-start(bf16[256,256]{0,1:T(8,128)(2,1)S(1)} %fusion.23), channel_id=1, source_target_pairs={{0,8},{1,9},{2,10},{3,11},{4,12},{5,13},{6,14},{7,15},{8,0},{9,1},... | collective-permute-start | bytes 393224 | tf_op jit(solution)/shard_map/ppermute | solution.py:87
  108.8 3.8 %collective-permute-done.16 = bf16[256,256]{0,1:T(8,128)(2,1)S(1)} collective-permute-done((bf16[256,256]{0,1:T(8,128)(2,1)S(1)}, bf16[256,256]{0,1:T(8,128)(2,1)S(1)}, u32[]{:S(2)}, u32[]{:S(2)}) %collective-permute-start.16) | collective-permute-done | bytes 131104 | tf_op jit(solution)/shard_map/ppermute | solution.py:87
  112.6 0.1 fusion.16
  112.7 0.8 copy.46
  (44 shorter events, 0.5 us)
Async XLA Ops:
  0.0 1.0 copy-start
  2.0 6.8 %collective-permute-start = (bf16[256,256]{0,1:T(8,128)(2,1)S(1)}, bf16[256,256]{0,1:T(8,128)(2,1)S(1)}, u32[]{:S(2)}, u32[]{:S(2)}) collective-permute-start(bf16[256,256]{0,1:T(8,128)(2,1)S(1)} %convolution_convert_fusion), channel_id=1, source_target_pairs={{0,8},{1,9},{2,10},{3,11},{4,12},{5,13},{6,14},{7,15},{8,0},{9,1},... | collective-permute-start | bytes 393224 | tf_op jit(solution)/shard_map/ppermute | solution.py:28
  8.9 11.4 %collective-permute-start.4 = (bf16[2,256,256]{1,2,0:T(8,128)(2,1)S(1)}, bf16[2,256,256]{1,2,0:T(8,128)(2,1)S(1)}, u32[]{:S(2)}, u32[]{:S(2)}) collective-permute-start(bf16[2,256,256]{1,2,0:T(8,128)(2,1)S(1)} %maximum_select_fusion.1), channel_id=1, source_target_pairs={{0,1},{1,2},{2,3},{3,4},{4,5},{5,6},{6,7},{7,0},{8,9},{9,10},{10,1... | collective-permute-start | bytes 786440 | tf_op jit(solution)/shard_map/ppermute | solution.py:26
  10.8 9.4 %collective-permute-start.1 = (bf16[2,256,256]{1,2,0:T(8,128)(2,1)S(1)}, bf16[2,256,256]{1,2,0:T(8,128)(2,1)S(1)}, u32[]{:S(2)}, u32[]{:S(2)}) collective-permute-start(bf16[2,256,256]{1,2,0:T(8,128)(2,1)S(1)} %maximum_select_fusion.1), channel_id=1, source_target_pairs={{0,7},{1,0},{2,1},{3,2},{4,3},{5,4},{6,5},{7,6},{8,15},{9,8},{10,9... | collective-permute-start | bytes 786440 | tf_op jit(solution)/shard_map/ppermute | solution.py:26
  20.2 7.8 %collective-permute-start.5 = (bf16[2,256,256]{1,2,0:T(8,128)(2,1)S(1)}, bf16[2,256,256]{1,2,0:T(8,128)(2,1)S(1)}, u32[]{:S(2)}, u32[]{:S(2)}) collective-permute-start(bf16[2,256,256]{1,2,0:T(8,128)(2,1)S(1)} %collective-permute-done.4), channel_id=1, source_target_pairs={{0,1},{1,2},{2,3},{3,4},{4,5},{5,6},{6,7},{7,0},{8,9},{9,10},{10,1... | collective-permute-start | bytes 786440 | tf_op jit(solution)/shard_map/ppermute | solution.py:26
  20.2 7.9 %collective-permute-start.2 = (bf16[2,256,256]{1,2,0:T(8,128)(2,1)S(1)}, bf16[2,256,256]{1,2,0:T(8,128)(2,1)S(1)}, u32[]{:S(2)}, u32[]{:S(2)}) collective-permute-start(bf16[2,256,256]{1,2,0:T(8,128)(2,1)S(1)} %collective-permute-done.1), channel_id=1, source_target_pairs={{0,7},{1,0},{2,1},{3,2},{4,3},{5,4},{6,5},{7,6},{8,15},{9,8},{10,9... | collective-permute-start | bytes 786440 | tf_op jit(solution)/shard_map/ppermute | solution.py:26
  28.1 7.6 %collective-permute-start.6 = (bf16[2,256,256]{1,2,0:T(8,128)(2,1)S(1)}, bf16[2,256,256]{1,2,0:T(8,128)(2,1)S(1)}, u32[]{:S(2)}, u32[]{:S(2)}) collective-permute-start(bf16[2,256,256]{1,2,0:T(8,128)(2,1)S(1)} %collective-permute-done.5), channel_id=1, source_target_pairs={{0,1},{1,2},{2,3},{3,4},{4,5},{5,6},{6,7},{7,0},{8,9},{9,10},{10,1... | collective-permute-start | bytes 786440 | tf_op jit(solution)/shard_map/ppermute | solution.py:26
  28.1 7.5 %collective-permute-start.3 = (bf16[2,256,256]{1,2,0:T(8,128)(2,1)S(1)}, bf16[2,256,256]{1,2,0:T(8,128)(2,1)S(1)}, u32[]{:S(2)}, u32[]{:S(2)}) collective-permute-start(bf16[2,256,256]{1,2,0:T(8,128)(2,1)S(1)} %collective-permute-done.2), channel_id=1, source_target_pairs={{0,7},{1,0},{2,1},{3,2},{4,3},{5,4},{6,5},{7,6},{8,15},{9,8},{10,9... | collective-permute-start | bytes 786440 | tf_op jit(solution)/shard_map/ppermute | solution.py:26
  35.6 7.6 %collective-permute-start.7 = (bf16[2,256,256]{1,2,0:T(8,128)(2,1)S(1)}, bf16[2,256,256]{1,2,0:T(8,128)(2,1)S(1)}, u32[]{:S(2)}, u32[]{:S(2)}) collective-permute-start(bf16[2,256,256]{1,2,0:T(8,128)(2,1)S(1)} %collective-permute-done.6), channel_id=1, source_target_pairs={{0,1},{1,2},{2,3},{3,4},{4,5},{5,6},{6,7},{7,0},{8,9},{9,10},{10,1... | collective-permute-start | bytes 786440 | tf_op jit(solution)/shard_map/ppermute | solution.py:26
  44.2 2.4 %slice-start = ((s8[6291456]{0:T(1024)(128)(4,1)}), s8[4194304]{0:T(1024)(128)(4,1)S(1)}, s32[]{:S(2)}) async-start(s8[6291456]{0:T(1024)(128)(4,1)} %bitcast.105), calls=%async_computation.1 | async-start | bytes 8388608
  44.6 1.0 copy-start.3
  44.6 2.5 %slice-start.1 = ((s8[6291456]{0:T(1024)(128)(4,1)}), s8[2097152]{0:T(1024)(128)(4,1)S(1)}, s32[]{:S(2)}) async-start(s8[6291456]{0:T(1024)(128)(4,1)} %bitcast.105), calls=%async_computation.2 | async-start | bytes 4194304
  47.2 3.8 %copy-start.2 = (f32[16,256]{1,0:T(8,128)S(1)}, f32[16,256]{1,0:T(8,128)}, u32[]{:S(2)}) copy-start(f32[16,256]{1,0:T(8,128)} %param.14) | copy-start | bytes 49156
  49.0 4.9 %collective-permute-start.8 = (bf16[2,3,256]{2,0,1:T(2,128)(2,1)S(1)}, bf16[2,3,256]{2,0,1:T(2,128)(2,1)S(1)}, u32[]{:S(2)}, u32[]{:S(2)}) collective-permute-start(bf16[2,3,256]{2,0,1:T(2,128)(2,1)S(1)} %slice.82), channel_id=1, source_target_pairs={{0,16},{16,32},{32,48},{48,64},{64,80},{80,96},{96,112},{112,128},... | collective-permute-start | bytes 9224 | tf_op jit(solution)/shard_map/ppermute | solution.py:12
  54.3 8.8 %copy-start.5 = (f32[16,256]{1,0:T(8,128)S(1)}, f32[16,256]{1,0:T(8,128)}, u32[]{:S(2)}) copy-start(f32[16,256]{1,0:T(8,128)} %param.15) | copy-start | bytes 49156
  56.6 11.9 %all-to-all-start = ((f32[16,16,256]{2,1,0:T(8,128)}), f32[16,16,256]{2,1,0:T(8,128)S(1)}, u32[]{:S(2)}, u32[]{:S(2)}) async-start(f32[16,16,256]{2,1,0:T(8,128)} %tile.2), calls=%async_computation | async-start | bytes 524288 | tf_op jit(solution)/shard_map/all_to_all | solution.py:145
  62.4 3.9 %copy-start.1 = (bf16[256,4096]{1,0:T(8,128)(2,1)S(1)}, bf16[256,4096]{1,0:T(8,128)(2,1)}, u32[]{:S(2)}) copy-start(bf16[256,4096]{1,0:T(8,128)(2,1)} %param.17) | copy-start | bytes 6291460
  67.0 2.5 %copy-start.4 = (f32[256]{0:T(256)S(1)}, f32[256]{0:T(256)}, u32[]{:S(2)}) copy-start(f32[256]{0:T(256)} %param.16) | copy-start | bytes 3076
  71.3 9.7 %collective-permute-start.9 = (bf16[256,2,256]{0,2,1:T(8,128)(2,1)S(1)}, bf16[256,2,256]{0,2,1:T(8,128)(2,1)S(1)}, u32[]{:S(2)}, u32[]{:S(2)}) collective-permute-start(bf16[256,2,256]{0,2,1:T(8,128)(2,1)S(1)} %get-tuple-element.18), channel_id=1, source_target_pairs={{0,1},{1,2},{2,3},{3,4},{4,5},{5,6},{6,7},{7,0},{8,9},{9,10},{10,1... | collective-permute-start | bytes 786440 | tf_op jit(solution)/shard_map/ppermute | solution.py:62
  71.4 9.8 %collective-permute-start.13 = (bf16[256,2,256]{0,2,1:T(8,128)(2,1)S(1)}, bf16[256,2,256]{0,2,1:T(8,128)(2,1)S(1)}, u32[]{:S(2)}, u32[]{:S(2)}) collective-permute-start(bf16[256,2,256]{0,2,1:T(8,128)(2,1)S(1)} %get-tuple-element.22), channel_id=1, source_target_pairs={{0,7},{1,0},{2,1},{3,2},{4,3},{5,4},{6,5},{7,6},{8,15},{9,8},{10,9... | collective-permute-start | bytes 786440 | tf_op jit(solution)/shard_map/ppermute | solution.py:62
  81.1 8.8 %collective-permute-start.10 = (bf16[256,2,256]{0,2,1:T(8,128)(2,1)S(1)}, bf16[256,2,256]{0,2,1:T(8,128)(2,1)S(1)}, u32[]{:S(2)}, u32[]{:S(2)}) collective-permute-start(bf16[256,2,256]{0,2,1:T(8,128)(2,1)S(1)} %add_convert_fusion.4), channel_id=1, source_target_pairs={{0,1},{1,2},{2,3},{3,4},{4,5},{5,6},{6,7},{7,0},{8,9},{9,10},{10,1... | collective-permute-start | bytes 786440 | tf_op jit(solution)/shard_map/ppermute | solution.py:62
  81.2 9.1 %collective-permute-start.14 = (bf16[256,2,256]{0,2,1:T(8,128)(2,1)S(1)}, bf16[256,2,256]{0,2,1:T(8,128)(2,1)S(1)}, u32[]{:S(2)}, u32[]{:S(2)}) collective-permute-start(bf16[256,2,256]{0,2,1:T(8,128)(2,1)S(1)} %add_convert_fusion.1), channel_id=1, source_target_pairs={{0,7},{1,0},{2,1},{3,2},{4,3},{5,4},{6,5},{7,6},{8,15},{9,8},{10,9... | collective-permute-start | bytes 786440 | tf_op jit(solution)/shard_map/ppermute | solution.py:62
  90.0 8.2 %collective-permute-start.11 = (bf16[256,2,256]{0,2,1:T(8,128)(2,1)S(1)}, bf16[256,2,256]{0,2,1:T(8,128)(2,1)S(1)}, u32[]{:S(2)}, u32[]{:S(2)}) collective-permute-start(bf16[256,2,256]{0,2,1:T(8,128)(2,1)S(1)} %add_convert_fusion.3), channel_id=1, source_target_pairs={{0,1},{1,2},{2,3},{3,4},{4,5},{5,6},{6,7},{7,0},{8,9},{9,10},{10,1... | collective-permute-start | bytes 786440 | tf_op jit(solution)/shard_map/ppermute | solution.py:62
  90.4 8.0 %collective-permute-start.15 = (bf16[256,2,256]{0,2,1:T(8,128)(2,1)S(1)}, bf16[256,2,256]{0,2,1:T(8,128)(2,1)S(1)}, u32[]{:S(2)}, u32[]{:S(2)}) collective-permute-start(bf16[256,2,256]{0,2,1:T(8,128)(2,1)S(1)} %add_convert_fusion), channel_id=1, source_target_pairs={{0,7},{1,0},{2,1},{3,2},{4,3},{5,4},{6,5},{7,6},{8,15},{9,8},{10,9... | collective-permute-start | bytes 786440 | tf_op jit(solution)/shard_map/ppermute | solution.py:62
  98.2 7.7 %collective-permute-start.12 = (bf16[256,2,256]{0,2,1:T(8,128)(2,1)S(1)}, bf16[256,2,256]{0,2,1:T(8,128)(2,1)S(1)}, u32[]{:S(2)}, u32[]{:S(2)}) collective-permute-start(bf16[256,2,256]{0,2,1:T(8,128)(2,1)S(1)} %add_convert_fusion.2), channel_id=1, source_target_pairs={{0,1},{1,2},{2,3},{3,4},{4,5},{5,6},{6,7},{7,0},{8,9},{9,10},{10,1... | collective-permute-start | bytes 786440 | tf_op jit(solution)/shard_map/ppermute | solution.py:62
  106.1 6.6 %collective-permute-start.16 = (bf16[256,256]{0,1:T(8,128)(2,1)S(1)}, bf16[256,256]{0,1:T(8,128)(2,1)S(1)}, u32[]{:S(2)}, u32[]{:S(2)}) collective-permute-start(bf16[256,256]{0,1:T(8,128)(2,1)S(1)} %fusion.23), channel_id=1, source_target_pairs={{0,8},{1,9},{2,10},{3,11},{4,12},{5,13},{6,14},{7,15},{8,0},{9,1},... | collective-permute-start | bytes 393224 | tf_op jit(solution)/shard_map/ppermute | solution.py:87

commit v10 on v9

--- a/solution.py
+++ b/solution.py
@@ -99,15 +99,11 @@
     out_weight,
 ):
     token_rows = tokens.shape[0]
-    vocab_size = embedding.shape[0]
     channels = embedding.shape[1]
     modes = decay_rate.shape[0]
     seq_devices = lax.axis_size("seq")
 
-    one_hot = (tokens[:, None] == jnp.arange(vocab_size, dtype=jnp.int32)[None, :]).astype(
-        jnp.bfloat16
-    )
-    stream = jnp.dot(one_hot, embedding, preferred_element_type=jnp.float32).astype(jnp.bfloat16)
+    stream = jnp.take(embedding, tokens, axis=0, mode="clip")
     chan_devices = lax.axis_size("chan")
     gathered = gather_chan(stream, chan_devices)
     gathered_f = gathered.astype(jnp.float32)

time: 114 us -> 129 us (1.13)
  local copies, waits for them, and re-layouts: 6.09 us -> 14.2 us
  other arithmetic: 7.47 us -> 13.6 us
    convert_element_type x1, local copies, waits for them, and re-layouts: 0.39 us -> 5.4 us  [on_device(): gathered_f = gathered.astype(jnp.float32)]
    dynamic_slice x0 -> x1, local copies, waits for them, and re-layouts: none -> 3.01 us  [reduce_chan(): jnp.roll(out_weight.reshape(out_weight.shape[0], 2, ring, width), -where_...]
    dot_general x1, matrix products: 1.84 us -> 4.63 us  [on_device(): jnp.einsum('td,djc->tjc', normed, in_weight, preferred_element_type=jnp.f...]
    concatenate x0 -> x1, other arithmetic: none -> 2.76 us  [reduce_chan(): jnp.roll(out_weight.reshape(out_weight.shape[0], 2, ring, width), -where_...]
    convert_element_type x1, other arithmetic: 0.45 us -> 2.4 us  [on_device(): gathered_f = gathered.astype(jnp.float32)]
    convert_element_type x1, other arithmetic: 1 us -> 2.6 us  [on_device(): normed = (gathered_f * scale * norm_gain[None, :]).astype(jnp.bfloat16)]
    dot_general x1 -> x0, other arithmetic: 1.43 us -> none  [reduce_chan(): jnp.dot(hidden, rolled, preferred_element_type=jnp.float32)]
    unnamed x31 -> x25, local copies, waits for them, and re-layouts: 2.97 us -> 2.74 us
  transfers between devices with their start and end apart: 18 -> 18, of which waited for: 11 -> 11; matrix products, arithmetic and copies ran while one was open for 6% -> 10% of each run, Pallas kernels for 0% -> 0%
where the time goes in v10:
time: 129 us; the launch traced here: 128 us
  waiting for transfers between devices  54.9 us (43%)
  starting transfers between devices  36.4 us (28%)
  local copies, waits for them, and re-layouts  14.2 us (11%)
  other arithmetic  13.6 us (11%)
  matrix products  8.64 us (7%)
    ppermute x14, waiting for transfers between devices, along_ring(): return lax.ppermute(value, 'chan', pairs)  44.5 us
    ppermute x14, starting transfers between devices, along_ring(): return lax.ppermute(value, 'chan', pairs)  22.7 us
    all_to_all x1, starting transfers between devices, on_device(): lax.all_to_all(jnp.tile(device_end, (seq_devices, 1)), 'seq', 0, 0, tiled...  5.86 us
    convert_element_type x1, local copies, waits for them, and re-layouts, on_device(): gathered_f = gathered.astype(jnp.float32)  5.4 us
    dot_general x1, matrix products, on_device(): jnp.einsum('td,djc->tjc', normed, in_weight, preferred_element_type=jnp.f...  4.63 us
    ppermute x1, waiting for transfers between devices, reduce_chan(): lax.ppermute(theirs.astype(jnp.bfloat16), 'chan', partners)  3.74 us
    ppermute x1, waiting for transfers between devices, gather_chan(): lax.ppermute(block, 'chan', [(i, (i + ring) % chan_devices) for i in rang...  3.72 us
    dot_general x1, matrix products, on_device(): jnp.dot(lower, lifted.reshape(token_rows, modes * channels), precision=la...  3.25 us
  transfers between devices with their start and end apart: 18, of which 11 were waited for; matrix products, arithmetic and copies ran while one was open for 10% of the time, Pallas kernels for 0%

profile of v10, /device:TPU:8, one launch (start us, length us, event | category | flops | bytes accessed | tf_op | source)
XLA Modules:
  0.0 128.2 jit_solution(10881530123287266106)
XLA Ops:
  0.0 0.7 pad_clamp_fusion
  0.7 0.2 copy-done
  1.0 1.1 gather_fusion
  2.1 3.1 %collective-permute-start = (bf16[256,256]{1,0:T(8,128)(2,1)S(1)}, bf16[256,256]{1,0:T(8,128)(2,1)S(1)}, u32[]{:S(2)}, u32[]{:S(2)}) collective-permute-start(bf16[256,256]{1,0:T(8,128)(2,1)S(1)} %gather_fusion), channel_id=1, source_target_pairs={{0,8},{1,9},{2,10},{3,11},{4,12},{5,13},{6,14},{7,15},{8,0},{9,1},... | collective-permute-start | bytes 393224 | tf_op jit(solution)/shard_map/ppermute | solution.py:28
  5.2 3.7 %collective-permute-done = bf16[256,256]{1,0:T(8,128)(2,1)S(1)} collective-permute-done((bf16[256,256]{1,0:T(8,128)(2,1)S(1)}, bf16[256,256]{1,0:T(8,128)(2,1)S(1)}, u32[]{:S(2)}, u32[]{:S(2)}) %collective-permute-start) | collective-permute-done | bytes 131104 | tf_op jit(solution)/shard_map/ppermute | solution.py:28
  9.0 2.0 %collective-permute-start.4 = (bf16[2,256,256]{2,1,0:T(8,128)(2,1)S(1)}, bf16[2,256,256]{2,1,0:T(8,128)(2,1)S(1)}, u32[]{:S(2)}, u32[]{:S(2)}) collective-permute-start(bf16[2,256,256]{2,1,0:T(8,128)(2,1)S(1)} %maximum_select_fusion.1), channel_id=1, source_target_pairs={{0,1},{1,2},{2,3},{3,4},{4,5},{5,6},{6,7},{7,0},{8,9},{9,10},{10,1... | collective-permute-start | bytes 786440 | tf_op jit(solution)/shard_map/ppermute | solution.py:26
  11.0 4.0 %collective-permute-start.1 = (bf16[2,256,256]{2,1,0:T(8,128)(2,1)S(1)}, bf16[2,256,256]{2,1,0:T(8,128)(2,1)S(1)}, u32[]{:S(2)}, u32[]{:S(2)}) collective-permute-start(bf16[2,256,256]{2,1,0:T(8,128)(2,1)S(1)} %maximum_select_fusion.1), channel_id=1, source_target_pairs={{0,7},{1,0},{2,1},{3,2},{4,3},{5,4},{6,5},{7,6},{8,15},{9,8},{10,9... | collective-permute-start | bytes 786440 | tf_op jit(solution)/shard_map/ppermute | solution.py:26
  15.0 5.4 %collective-permute-done.4 = bf16[2,256,256]{2,1,0:T(8,128)(2,1)S(1)} collective-permute-done((bf16[2,256,256]{2,1,0:T(8,128)(2,1)S(1)}, bf16[2,256,256]{2,1,0:T(8,128)(2,1)S(1)}, u32[]{:S(2)}, u32[]{:S(2)}) %collective-permute-start.4) | collective-permute-done | bytes 262176 | tf_op jit(solution)/shard_map/ppermute | solution.py:26
  20.4 0.0 collective-permute-start.5
  20.4 3.2 %collective-permute-start.2 = (bf16[2,256,256]{2,1,0:T(8,128)(2,1)S(1)}, bf16[2,256,256]{2,1,0:T(8,128)(2,1)S(1)}, u32[]{:S(2)}, u32[]{:S(2)}) collective-permute-start(bf16[2,256,256]{2,1,0:T(8,128)(2,1)S(1)} %collective-permute-done.1), channel_id=1, source_target_pairs={{0,7},{1,0},{2,1},{3,2},{4,3},{5,4},{6,5},{7,6},{8,15},{9,8},{10,9... | collective-permute-start | bytes 786440 | tf_op jit(solution)/shard_map/ppermute | solution.py:26
  23.6 0.7 slice_bitcast_fusion.10
  24.3 3.9 %collective-permute-done.5 = bf16[2,256,256]{2,1,0:T(8,128)(2,1)S(1)} collective-permute-done((bf16[2,256,256]{2,1,0:T(8,128)(2,1)S(1)}, bf16[2,256,256]{2,1,0:T(8,128)(2,1)S(1)}, u32[]{:S(2)}, u32[]{:S(2)}) %collective-permute-start.5) | collective-permute-done | bytes 262176 | tf_op jit(solution)/shard_map/ppermute | solution.py:26
  28.2 0.0 collective-permute-start.6
  28.2 0.0 collective-permute-done.2
  28.2 3.3 %collective-permute-start.3 = (bf16[2,256,256]{2,1,0:T(8,128)(2,1)S(1)}, bf16[2,256,256]{2,1,0:T(8,128)(2,1)S(1)}, u32[]{:S(2)}, u32[]{:S(2)}) collective-permute-start(bf16[2,256,256]{2,1,0:T(8,128)(2,1)S(1)} %collective-permute-done.2), channel_id=1, source_target_pairs={{0,7},{1,0},{2,1},{3,2},{4,3},{5,4},{6,5},{7,6},{8,15},{9,8},{10,9... | collective-permute-start | bytes 786440 | tf_op jit(solution)/shard_map/ppermute | solution.py:26
  31.6 4.2 %collective-permute-done.6 = bf16[2,256,256]{2,1,0:T(8,128)(2,1)S(1)} collective-permute-done((bf16[2,256,256]{2,1,0:T(8,128)(2,1)S(1)}, bf16[2,256,256]{2,1,0:T(8,128)(2,1)S(1)}, u32[]{:S(2)}, u32[]{:S(2)}) %collective-permute-start.6) | collective-permute-done | bytes 262176 | tf_op jit(solution)/shard_map/ppermute | solution.py:26
  35.8 0.0 collective-permute-start.7
  35.8 7.5 %collective-permute-done.7 = bf16[2,256,256]{2,1,0:T(8,128)(2,1)S(1)} collective-permute-done((bf16[2,256,256]{2,1,0:T(8,128)(2,1)S(1)}, bf16[2,256,256]{2,1,0:T(8,128)(2,1)S(1)}, u32[]{:S(2)}, u32[]{:S(2)}) %collective-permute-start.7) | collective-permute-done | bytes 262176 | tf_op jit(solution)/shard_map/ppermute | solution.py:26
  43.5 0.1 fusion.29
  43.7 0.5 fusion
  44.2 2.4 %convert_bitcast_fusion = f32[256,2,8,256]{3,0,1,2:T(8,128)} fusion(bf16[16,2,256,256]{3,2,1,0:T(8,128)(2,1)S(1)} %bitcast_dynamic-update-slice_fusion.1, s32[]{:T(128)S(6)} %select_n.77), kind=kLoop, calls=%fused_computation.2 | loop fusion | flops 1048576 | bytes 6291460 | tf_op jit(solution)/shard_map/convert_element_type | solution.py:109
  46.6 5.4 %copy.30 = f32[256,2,8,256]{0,3,2,1:T(8,128)} copy(f32[256,2,8,256]{3,0,1,2:T(8,128)} %convert_bitcast_fusion) | data formatting | bytes 8388608 | tf_op jit(solution)/shard_map/convert_element_type | solution.py:109
  52.0 2.6 %fusion.2 = bf16[256,4096]{0,1:T(8,128)(2,1)S(1)} fusion(f32[256,2,8,256]{0,3,2,1:T(8,128)} %copy.30, f32[4096]{0:T(1024)S(1)} %copy-done.2, f32[256]{0:T(256)S(1)} %add_rsqrt_fusion), kind=kLoop, calls=%fused_computation.9 | loop fusion | flops 3145728 | bytes 6308864 | tf_op jit(solution)/shard_map/convert_element_type | solution.py:111
  54.6 0.0 copy-start.1
  54.6 4.6 %fusion.8 = bf16[256,3,256]{2,0,1:T(8,128)(2,1)S(1)} fusion(bf16[4096,3,256]{2,0,1:T(8,128)(2,1)} %param.12, bf16[256,4096]{0,1:T(8,128)(2,1)S(1)} %fusion.2), kind=kOutput, calls=%fused_computation.19 | convolution fusion | flops 1610809344 | bytes 8781824 | tf_op jit(solution)/shard_map/td,djc->tjc/dot_general | solution.py:112
  59.3 1.9 %collective-permute-start.8 = (bf16[2,3,256]{2,0,1:T(2,128)(2,1)S(1)}, bf16[2,3,256]{2,0,1:T(2,128)(2,1)S(1)}, u32[]{:S(2)}, u32[]{:S(2)}) collective-permute-start(bf16[2,3,256]{2,0,1:T(2,128)(2,1)S(1)} %slice.84), channel_id=1, source_target_pairs={{0,16},{16,32},{32,48},{48,64},{64,80},{80,96},{96,112},{112,128},... | collective-permute-start | bytes 9224 | tf_op jit(solution)/shard_map/ppermute | solution.py:12
  61.3 2.9 %collective-permute-done.8 = bf16[2,3,256]{2,0,1:T(2,128)(2,1)S(1)} collective-permute-done((bf16[2,3,256]{2,0,1:T(2,128)(2,1)S(1)}, bf16[2,3,256]{2,0,1:T(2,128)(2,1)S(1)}, u32[]{:S(2)}, u32[]{:S(2)}) %collective-permute-start.8) | collective-permute-done | bytes 3104 | tf_op jit(solution)/shard_map/ppermute | solution.py:12
  64.2 0.1 maximum_convert_fusion
  64.3 0.3 fusion.12
  64.6 0.1 copy.32
  64.7 1.3 %multiply_reduce_fusion.1 = f32[16,256]{1,0:T(8,128)S(1)} fusion(f32[16,256]{1,0:T(8,128)S(1)} %copy-done.1, f32[256,256]{0,1:T(8,128)S(1)} %copy.32), kind=kLoop, calls=%fused_computation.11 | loop fusion | flops 3141632 | bytes 294912 | tf_op jit(solution)/shard_map/reduce_sum | solution.py:139
  66.1 0.7 tile.2
  66.8 5.9 %all-to-all-start = ((f32[16,16,256]{2,1,0:T(8,128)}), f32[16,16,256]{2,1,0:T(8,128)S(1)}, u32[]{:S(2)}, u32[]{:S(2)}) async-start(f32[16,16,256]{2,1,0:T(8,128)} %tile.2), calls=%async_computation | async-start | bytes 524288 | tf_op jit(solution)/shard_map/all_to_all | solution.py:141
  72.6 2.2 %copy.52 = bf16[32,8,16,256]{3,2,1,0:T(8,128)(2,1)S(1)} copy(bf16[32,8,16,256]{3,1,2,0:T(8,128)(2,1)} %bitcast.127) | data formatting | bytes 4194304
  74.9 2.8 %fusion.3 = bf16[256,2,8,256]{3,2,1,0:T(8,128)(2,1)} fusion(s32[]{:T(128)S(6)} %select_n.80, bf16[256,2,8,256]{3,2,1,0:T(8,128)(2,1)S(1)} %bitcast.122), kind=kLoop, calls=%fused_computation.14 | loop fusion | flops 4194304 | bytes 4194308 | tf_op jit(solution)/shard_map/jit(_roll_dynamic)/concatenate | solution.py:49
  77.6 3.0 %copy.33 = bf16[256,2,8,256]{0,3,2,1:T(8,128)(2,1)S(1)} copy(bf16[256,2,8,256]{3,2,1,0:T(8,128)(2,1)} %fusion.3) | data formatting | bytes 4194304 | tf_op jit(solution)/shard_map/jit(_roll_dynamic)/dynamic_slice | solution.py:49
  80.7 0.6 bitcast_multiply_fusion
  81.3 0.0 copy-start.3
  81.3 3.2 %multiply_reduce_fusion.2 = f32[256,256]{1,0:T(8,128)S(1)} fusion(f32[16,256,256]{2,1,0:T(8,128)S(1)} %bitcast.123, f32[16,256]{1,0:T(8,128)S(1)} %get-tuple-element.33, f32[16,256]{1,0:T(8,128)S(1)} %copy-done.4), kind=kOutput, calls=%fused_computation.12 | convolution fusion | flops 3225419776 | bytes 4489216 | tf_op jit(solution)/shard_map/dot_general | solution.py:135
  84.6 0.1 multiply_reduce_fusion.3
  84.7 0.9 multiply_reduce_fusion
  85.6 0.8 fusion.4
  86.4 0.1 slice_bitcast_fusion.2
  86.4 0.2 slice_bitcast_fusion
  86.7 0.1 collective-permute-start.9
  86.7 3.2 %collective-permute-start.13 = (bf16[256,2,256]{2,0,1:T(8,128)(2,1)S(1)}, bf16[256,2,256]{2,0,1:T(8,128)(2,1)S(1)}, u32[]{:S(2)}, u32[]{:S(2)}) collective-permute-start(bf16[256,2,256]{2,0,1:T(8,128)(2,1)S(1)} %get-tuple-element.22), channel_id=1, source_target_pairs={{0,7},{1,0},{2,1},{3,2},{4,3},{5,4},{6,5},{7,6},{8,15},{9,8},{10,9... | collective-permute-start | bytes 786440 | tf_op jit(solution)/shard_map/ppermute | solution.py:62
  90.0 6.3 %collective-permute-done.9 = bf16[256,2,256]{2,0,1:T(8,128)(2,1)S(1)} collective-permute-done((bf16[256,2,256]{2,0,1:T(8,128)(2,1)S(1)}, bf16[256,2,256]{2,0,1:T(8,128)(2,1)S(1)}, u32[]{:S(2)}, u32[]{:S(2)}) %collective-permute-start.9) | collective-permute-done | bytes 262176 | tf_op jit(solution)/shard_map/ppermute | solution.py:62
  96.3 0.1 add_convert_fusion.4
  96.3 0.1 collective-permute-start.10
  96.4 0.1 add_convert_fusion.1
  96.5 3.3 %collective-permute-start.14 = (bf16[256,2,256]{2,0,1:T(8,128)(2,1)S(1)}, bf16[256,2,256]{2,0,1:T(8,128)(2,1)S(1)}, u32[]{:S(2)}, u32[]{:S(2)}) collective-permute-start(bf16[256,2,256]{2,0,1:T(8,128)(2,1)S(1)} %add_convert_fusion.1), channel_id=1, source_target_pairs={{0,7},{1,0},{2,1},{3,2},{4,3},{5,4},{6,5},{7,6},{8,15},{9,8},{10,9... | collective-permute-start | bytes 786440 | tf_op jit(solution)/shard_map/ppermute | solution.py:62
  99.8 5.3 %collective-permute-done.10 = bf16[256,2,256]{2,0,1:T(8,128)(2,1)S(1)} collective-permute-done((bf16[256,2,256]{2,0,1:T(8,128)(2,1)S(1)}, bf16[256,2,256]{2,0,1:T(8,128)(2,1)S(1)}, u32[]{:S(2)}, u32[]{:S(2)}) %collective-permute-start.10) | collective-permute-done | bytes 262176 | tf_op jit(solution)/shard_map/ppermute | solution.py:62
  105.1 0.1 add_convert_fusion.3
  105.2 0.1 collective-permute-start.11
  105.3 0.1 add_convert_fusion
  105.3 3.3 %collective-permute-start.15 = (bf16[256,2,256]{2,0,1:T(8,128)(2,1)S(1)}, bf16[256,2,256]{2,0,1:T(8,128)(2,1)S(1)}, u32[]{:S(2)}, u32[]{:S(2)}) collective-permute-start(bf16[256,2,256]{2,0,1:T(8,128)(2,1)S(1)} %add_convert_fusion), channel_id=1, source_target_pairs={{0,7},{1,0},{2,1},{3,2},{4,3},{5,4},{6,5},{7,6},{8,15},{9,8},{10,9... | collective-permute-start | bytes 786440 | tf_op jit(solution)/shard_map/ppermute | solution.py:62
  108.6 4.4 %collective-permute-done.11 = bf16[256,2,256]{2,0,1:T(8,128)(2,1)S(1)} collective-permute-done((bf16[256,2,256]{2,0,1:T(8,128)(2,1)S(1)}, bf16[256,2,256]{2,0,1:T(8,128)(2,1)S(1)}, u32[]{:S(2)}, u32[]{:S(2)}) %collective-permute-start.11) | collective-permute-done | bytes 262176 | tf_op jit(solution)/shard_map/ppermute | solution.py:62
  113.1 0.1 add_convert_fusion.2
  113.1 0.1 collective-permute-start.12
  113.2 7.6 %collective-permute-done.12 = bf16[256,2,256]{2,0,1:T(8,128)(2,1)S(1)} collective-permute-done((bf16[256,2,256]{2,0,1:T(8,128)(2,1)S(1)}, bf16[256,2,256]{2,0,1:T(8,128)(2,1)S(1)}, u32[]{:S(2)}, u32[]{:S(2)}) %collective-permute-start.12) | collective-permute-done | bytes 262176 | tf_op jit(solution)/shard_map/ppermute | solution.py:62
  120.8 0.1 convert_add_fusion
  120.9 2.8 %collective-permute-start.16 = (bf16[256,256]{1,0:T(8,128)(2,1)S(1)}, bf16[256,256]{1,0:T(8,128)(2,1)S(1)}, u32[]{:S(2)}, u32[]{:S(2)}) collective-permute-start(bf16[256,256]{1,0:T(8,128)(2,1)S(1)} %fusion.21), channel_id=1, source_target_pairs={{0,8},{1,9},{2,10},{3,11},{4,12},{5,13},{6,14},{7,15},{8,0},{9,1},... | collective-permute-start | bytes 393224 | tf_op jit(solution)/shard_map/ppermute | solution.py:87
  123.7 3.7 %collective-permute-done.16 = bf16[256,256]{1,0:T(8,128)(2,1)S(1)} collective-permute-done((bf16[256,256]{1,0:T(8,128)(2,1)S(1)}, bf16[256,256]{1,0:T(8,128)(2,1)S(1)}, u32[]{:S(2)}, u32[]{:S(2)}) %collective-permute-start.16) | collective-permute-done | bytes 131104 | tf_op jit(solution)/shard_map/ppermute | solution.py:87
  127.5 0.7 fusion.15
  (38 shorter events, 0.5 us)
Async XLA Ops:
  0.0 1.0 copy-start
  2.1 6.8 %collective-permute-start = (bf16[256,256]{1,0:T(8,128)(2,1)S(1)}, bf16[256,256]{1,0:T(8,128)(2,1)S(1)}, u32[]{:S(2)}, u32[]{:S(2)}) collective-permute-start(bf16[256,256]{1,0:T(8,128)(2,1)S(1)} %gather_fusion), channel_id=1, source_target_pairs={{0,8},{1,9},{2,10},{3,11},{4,12},{5,13},{6,14},{7,15},{8,0},{9,1},... | collective-permute-start | bytes 393224 | tf_op jit(solution)/shard_map/ppermute | solution.py:28
  9.0 11.4 %collective-permute-start.4 = (bf16[2,256,256]{2,1,0:T(8,128)(2,1)S(1)}, bf16[2,256,256]{2,1,0:T(8,128)(2,1)S(1)}, u32[]{:S(2)}, u32[]{:S(2)}) collective-permute-start(bf16[2,256,256]{2,1,0:T(8,128)(2,1)S(1)} %maximum_select_fusion.1), channel_id=1, source_target_pairs={{0,1},{1,2},{2,3},{3,4},{4,5},{5,6},{6,7},{7,0},{8,9},{9,10},{10,1... | collective-permute-start | bytes 786440 | tf_op jit(solution)/shard_map/ppermute | solution.py:26
  11.0 9.4 %collective-permute-start.1 = (bf16[2,256,256]{2,1,0:T(8,128)(2,1)S(1)}, bf16[2,256,256]{2,1,0:T(8,128)(2,1)S(1)}, u32[]{:S(2)}, u32[]{:S(2)}) collective-permute-start(bf16[2,256,256]{2,1,0:T(8,128)(2,1)S(1)} %maximum_select_fusion.1), channel_id=1, source_target_pairs={{0,7},{1,0},{2,1},{3,2},{4,3},{5,4},{6,5},{7,6},{8,15},{9,8},{10,9... | collective-permute-start | bytes 786440 | tf_op jit(solution)/shard_map/ppermute | solution.py:26
  20.4 7.8 %collective-permute-start.5 = (bf16[2,256,256]{2,1,0:T(8,128)(2,1)S(1)}, bf16[2,256,256]{2,1,0:T(8,128)(2,1)S(1)}, u32[]{:S(2)}, u32[]{:S(2)}) collective-permute-start(bf16[2,256,256]{2,1,0:T(8,128)(2,1)S(1)} %collective-permute-done.4), channel_id=1, source_target_pairs={{0,1},{1,2},{2,3},{3,4},{4,5},{5,6},{6,7},{7,0},{8,9},{9,10},{10,1... | collective-permute-start | bytes 786440 | tf_op jit(solution)/shard_map/ppermute | solution.py:26
  20.4 7.9 %collective-permute-start.2 = (bf16[2,256,256]{2,1,0:T(8,128)(2,1)S(1)}, bf16[2,256,256]{2,1,0:T(8,128)(2,1)S(1)}, u32[]{:S(2)}, u32[]{:S(2)}) collective-permute-start(bf16[2,256,256]{2,1,0:T(8,128)(2,1)S(1)} %collective-permute-done.1), channel_id=1, source_target_pairs={{0,7},{1,0},{2,1},{3,2},{4,3},{5,4},{6,5},{7,6},{8,15},{9,8},{10,9... | collective-permute-start | bytes 786440 | tf_op jit(solution)/shard_map/ppermute | solution.py:26
  28.2 7.6 %collective-permute-start.6 = (bf16[2,256,256]{2,1,0:T(8,128)(2,1)S(1)}, bf16[2,256,256]{2,1,0:T(8,128)(2,1)S(1)}, u32[]{:S(2)}, u32[]{:S(2)}) collective-permute-start(bf16[2,256,256]{2,1,0:T(8,128)(2,1)S(1)} %collective-permute-done.5), channel_id=1, source_target_pairs={{0,1},{1,2},{2,3},{3,4},{4,5},{5,6},{6,7},{7,0},{8,9},{9,10},{10,1... | collective-permute-start | bytes 786440 | tf_op jit(solution)/shard_map/ppermute | solution.py:26
  28.2 7.5 %collective-permute-start.3 = (bf16[2,256,256]{2,1,0:T(8,128)(2,1)S(1)}, bf16[2,256,256]{2,1,0:T(8,128)(2,1)S(1)}, u32[]{:S(2)}, u32[]{:S(2)}) collective-permute-start(bf16[2,256,256]{2,1,0:T(8,128)(2,1)S(1)} %collective-permute-done.2), channel_id=1, source_target_pairs={{0,7},{1,0},{2,1},{3,2},{4,3},{5,4},{6,5},{7,6},{8,15},{9,8},{10,9... | collective-permute-start | bytes 786440 | tf_op jit(solution)/shard_map/ppermute | solution.py:26
  35.8 7.6 %collective-permute-start.7 = (bf16[2,256,256]{2,1,0:T(8,128)(2,1)S(1)}, bf16[2,256,256]{2,1,0:T(8,128)(2,1)S(1)}, u32[]{:S(2)}, u32[]{:S(2)}) collective-permute-start(bf16[2,256,256]{2,1,0:T(8,128)(2,1)S(1)} %collective-permute-done.6), channel_id=1, source_target_pairs={{0,1},{1,2},{2,3},{3,4},{4,5},{5,6},{6,7},{7,0},{8,9},{9,10},{10,1... | collective-permute-start | bytes 786440 | tf_op jit(solution)/shard_map/ppermute | solution.py:26
  46.6 5.4 %copy-start.2 = (f32[4096]{0:T(1024)S(1)}, f32[4096]{0:T(1024)}, u32[]{:S(2)}) copy-start(f32[4096]{0:T(1024)} %param.11) | copy-start | bytes 49156
  54.6 6.6 %copy-start.1 = (f32[16,256]{1,0:T(8,128)S(1)}, f32[16,256]{1,0:T(8,128)}, u32[]{:S(2)}) copy-start(f32[16,256]{1,0:T(8,128)} %param.14) | copy-start | bytes 49156
  59.3 4.9 %collective-permute-start.8 = (bf16[2,3,256]{2,0,1:T(2,128)(2,1)S(1)}, bf16[2,3,256]{2,0,1:T(2,128)(2,1)S(1)}, u32[]{:S(2)}, u32[]{:S(2)}) collective-permute-start(bf16[2,3,256]{2,0,1:T(2,128)(2,1)S(1)} %slice.84), channel_id=1, source_target_pairs={{0,16},{16,32},{32,48},{48,64},{64,80},{80,96},{96,112},{112,128},... | collective-permute-start | bytes 9224 | tf_op jit(solution)/shard_map/ppermute | solution.py:12
  66.8 17.8 %all-to-all-start = ((f32[16,16,256]{2,1,0:T(8,128)}), f32[16,16,256]{2,1,0:T(8,128)S(1)}, u32[]{:S(2)}, u32[]{:S(2)}) async-start(f32[16,16,256]{2,1,0:T(8,128)} %tile.2), calls=%async_computation | async-start | bytes 524288 | tf_op jit(solution)/shard_map/all_to_all | solution.py:141
  77.6 3.7 %copy-start.4 = (f32[16,256]{1,0:T(8,128)S(1)}, f32[16,256]{1,0:T(8,128)}, u32[]{:S(2)}) copy-start(f32[16,256]{1,0:T(8,128)} %param.15) | copy-start | bytes 49156
  81.3 4.3 %copy-start.3 = (f32[256]{0:T(256)S(1)}, f32[256]{0:T(256)}, u32[]{:S(2)}) copy-start(f32[256]{0:T(256)} %param.16) | copy-start | bytes 3076
  86.7 9.6 %collective-permute-start.9 = (bf16[256,2,256]{2,0,1:T(8,128)(2,1)S(1)}, bf16[256,2,256]{2,0,1:T(8,128)(2,1)S(1)}, u32[]{:S(2)}, u32[]{:S(2)}) collective-permute-start(bf16[256,2,256]{2,0,1:T(8,128)(2,1)S(1)} %get-tuple-element.18), channel_id=1, source_target_pairs={{0,1},{1,2},{2,3},{3,4},{4,5},{5,6},{6,7},{7,0},{8,9},{9,10},{10,1... | collective-permute-start | bytes 786440 | tf_op jit(solution)/shard_map/ppermute | solution.py:62
  86.7 9.7 %collective-permute-start.13 = (bf16[256,2,256]{2,0,1:T(8,128)(2,1)S(1)}, bf16[256,2,256]{2,0,1:T(8,128)(2,1)S(1)}, u32[]{:S(2)}, u32[]{:S(2)}) collective-permute-start(bf16[256,2,256]{2,0,1:T(8,128)(2,1)S(1)} %get-tuple-element.22), channel_id=1, source_target_pairs={{0,7},{1,0},{2,1},{3,2},{4,3},{5,4},{6,5},{7,6},{8,15},{9,8},{10,9... | collective-permute-start | bytes 786440 | tf_op jit(solution)/shard_map/ppermute | solution.py:62
  96.3 8.8 %collective-permute-start.10 = (bf16[256,2,256]{2,0,1:T(8,128)(2,1)S(1)}, bf16[256,2,256]{2,0,1:T(8,128)(2,1)S(1)}, u32[]{:S(2)}, u32[]{:S(2)}) collective-permute-start(bf16[256,2,256]{2,0,1:T(8,128)(2,1)S(1)} %add_convert_fusion.4), channel_id=1, source_target_pairs={{0,1},{1,2},{2,3},{3,4},{4,5},{5,6},{6,7},{7,0},{8,9},{9,10},{10,1... | collective-permute-start | bytes 786440 | tf_op jit(solution)/shard_map/ppermute | solution.py:62
  96.5 8.7 %collective-permute-start.14 = (bf16[256,2,256]{2,0,1:T(8,128)(2,1)S(1)}, bf16[256,2,256]{2,0,1:T(8,128)(2,1)S(1)}, u32[]{:S(2)}, u32[]{:S(2)}) collective-permute-start(bf16[256,2,256]{2,0,1:T(8,128)(2,1)S(1)} %add_convert_fusion.1), channel_id=1, source_target_pairs={{0,7},{1,0},{2,1},{3,2},{4,3},{5,4},{6,5},{7,6},{8,15},{9,8},{10,9... | collective-permute-start | bytes 786440 | tf_op jit(solution)/shard_map/ppermute | solution.py:62
  105.2 7.9 %collective-permute-start.11 = (bf16[256,2,256]{2,0,1:T(8,128)(2,1)S(1)}, bf16[256,2,256]{2,0,1:T(8,128)(2,1)S(1)}, u32[]{:S(2)}, u32[]{:S(2)}) collective-permute-start(bf16[256,2,256]{2,0,1:T(8,128)(2,1)S(1)} %add_convert_fusion.3), channel_id=1, source_target_pairs={{0,1},{1,2},{2,3},{3,4},{4,5},{5,6},{6,7},{7,0},{8,9},{9,10},{10,1... | collective-permute-start | bytes 786440 | tf_op jit(solution)/shard_map/ppermute | solution.py:62
  105.3 7.9 %collective-permute-start.15 = (bf16[256,2,256]{2,0,1:T(8,128)(2,1)S(1)}, bf16[256,2,256]{2,0,1:T(8,128)(2,1)S(1)}, u32[]{:S(2)}, u32[]{:S(2)}) collective-permute-start(bf16[256,2,256]{2,0,1:T(8,128)(2,1)S(1)} %add_convert_fusion), channel_id=1, source_target_pairs={{0,7},{1,0},{2,1},{3,2},{4,3},{5,4},{6,5},{7,6},{8,15},{9,8},{10,9... | collective-permute-start | bytes 786440 | tf_op jit(solution)/shard_map/ppermute | solution.py:62
  113.1 7.7 %collective-permute-start.12 = (bf16[256,2,256]{2,0,1:T(8,128)(2,1)S(1)}, bf16[256,2,256]{2,0,1:T(8,128)(2,1)S(1)}, u32[]{:S(2)}, u32[]{:S(2)}) collective-permute-start(bf16[256,2,256]{2,0,1:T(8,128)(2,1)S(1)} %add_convert_fusion.2), channel_id=1, source_target_pairs={{0,1},{1,2},{2,3},{3,4},{4,5},{5,6},{6,7},{7,0},{8,9},{9,10},{10,1... | collective-permute-start | bytes 786440 | tf_op jit(solution)/shard_map/ppermute | solution.py:62
  120.9 6.6 %collective-permute-start.16 = (bf16[256,256]{1,0:T(8,128)(2,1)S(1)}, bf16[256,256]{1,0:T(8,128)(2,1)S(1)}, u32[]{:S(2)}, u32[]{:S(2)}) collective-permute-start(bf16[256,256]{1,0:T(8,128)(2,1)S(1)} %fusion.21), channel_id=1, source_target_pairs={{0,8},{1,9},{2,10},{3,11},{4,12},{5,13},{6,14},{7,15},{8,0},{9,1},... | collective-permute-start | bytes 393224 | tf_op jit(solution)/shard_map/ppermute | solution.py:87
